TPU v7x, 512 devices: a whole 4x4x16 slice. The times are simulated.
512 devices in a mesh: dp: 16 (over z), expert: 32 (over y, x, core).
Axes of the slice: x: 4, y: 4, z: 16, core: 2. Of those that a mesh axis runs over, the one named last changes fastest.
Arguments:
- tokens: bfloat16 [65536, 1024], P(('dp', 'expert')), may hold values from -24 to 24
- expert_ids: int32 [65536, 2], P(('dp', 'expert')), may hold values from 0 to 31, all different within a row; in each aligned block of 128 rows (0 to 127, 128 to 255, ...) at most 32 rows name the same one
- route_probs: float32 [65536, 2], P(('dp', 'expert')), may hold values from 0.1 to 1
- w_gate: bfloat16 [32, 1024, 384], P('expert', 'dp'), may hold values from -0.1875 to 0.1875
- w_up: bfloat16 [32, 1024, 384], P('expert', 'dp'), may hold values from -0.1875 to 0.1875
- w_down: bfloat16 [32, 384, 1024], P('expert', None, 'dp'), may hold values from -0.3125 to 0.3125
- grad_out: bfloat16 [65536, 1024], P(('dp', 'expert')), may hold values from -2.5 to 2.5
Outputs:
- mixed_out: bfloat16 [65536, 1024], P(('dp', 'expert'))
- grad_tokens: bfloat16 [65536, 1024], P(('dp', 'expert'))
- grad_probs: float32 [65536, 2], P(('dp', 'expert'))
- grad_w_gate: bfloat16 [32, 1024, 384], P('expert', 'dp')
- grad_w_up: bfloat16 [32, 1024, 384], P('expert', 'dp')
- grad_w_down: bfloat16 [32, 384, 1024], P('expert', None, 'dp')
Inputs may be any that keep to these rules, and one draw needn't show every extreme that they name: `expert_ids`: each row names 2 different experts. Within the rows of one device no expert is named by more than 32 rows, and in every draw some expert is named by exactly 32 rows of some device.
All inputs are finite; a program needn't handle non-finite values.
Results may differ from a plain program's by a relative error of at most 0.017.
Values may be sent and summed in bfloat16 or wider, within the bound.
No kernel may reach another device: no remote copies, remote signals or barrier semaphores. Data moves between devices by JAX's collectives and lax.ppermute only.
A program may use at most 128 MiB of HBM per device.

v0:
```python
import jax
import jax.numpy as jnp
from jax import lax
from jax.sharding import PartitionSpec as P


def route_slots(expert_ids, experts):
    flat_ids = expert_ids.reshape(-1)
    onehot = (flat_ids[:, None] == jnp.arange(experts, dtype=jnp.int32)[None, :]).astype(jnp.int32)
    before = jnp.cumsum(onehot, axis=0) - onehot
    slot_of = jnp.sum(before * onehot, axis=1)
    return (flat_ids, slot_of, jnp.sum(onehot, axis=0))


def contract_rows(left_op, right_op):
    return lax.dot_general(
        left_op, right_op, (((0,), (0,)), ((), ())), preferred_element_type=jnp.float32
    )


def contract_cols(left_op, right_op):
    return lax.dot_general(
        left_op, right_op, (((1,), (1,)), ((), ())), preferred_element_type=jnp.float32
    )


def forward_whole(slot_rows, gate_full, up_full, down_full):
    gate_pre = jnp.dot(slot_rows, gate_full, preferred_element_type=jnp.float32)
    up_pre = jnp.dot(slot_rows, up_full, preferred_element_type=jnp.float32)
    hidden = (gate_pre * jax.nn.sigmoid(gate_pre) * up_pre).astype(jnp.bfloat16)
    expert_out = jnp.dot(hidden, down_full, preferred_element_type=jnp.float32).astype(jnp.bfloat16)
    return (gate_pre, up_pre, hidden, expert_out)


def backward_whole(slot_rows, stored, grad_in, gate_full, up_full, down_full):
    gate_pre, up_pre, hidden, expert_out = stored
    back_hidden = contract_cols(grad_in, down_full)
    sigmoid_g = jax.nn.sigmoid(gate_pre)
    activated = gate_pre * sigmoid_g
    back_gate = (back_hidden * up_pre * sigmoid_g * (1.0 + gate_pre * (1.0 - sigmoid_g))).astype(
        jnp.bfloat16
    )
    back_up = (back_hidden * activated).astype(jnp.bfloat16)
    back_rows = (contract_cols(back_gate, gate_full) + contract_cols(back_up, up_full)).astype(
        jnp.bfloat16
    )
    return (
        back_rows,
        contract_rows(slot_rows, back_gate),
        contract_rows(slot_rows, back_up),
        contract_rows(hidden, grad_in),
    )


def shards(tokens, expert_ids, route_probs, w_gate, w_up, w_down, grad_out):
    senders = lax.axis_size("expert")
    tok_rows, model_width = tokens.shape
    top_count = expert_ids.shape[1]
    capacity = min(tok_rows, 4 * tok_rows * top_count // senders)
    total_rows = senders * capacity
    flat_ids, slot_of, local_counts = route_slots(expert_ids, senders)
    slot_place = flat_ids * capacity + slot_of
    token_of = jnp.arange(tok_rows * top_count, dtype=jnp.int32) // top_count
    outgoing = (
        jnp.zeros((total_rows, model_width), jnp.bfloat16).at[slot_place].set(tokens[token_of])
    )
    gathered = (
        lax.all_gather(w_gate, "dp", axis=1, tiled=True),
        lax.all_gather(w_up, "dp", axis=1, tiled=True),
        lax.all_gather(w_down, "dp", axis=2, tiled=True),
    )
    gate_full, up_full, down_full = (gathered[0][0], gathered[1][0], gathered[2][0])
    arrived = lax.all_to_all(
        outgoing.reshape(senders, capacity, model_width),
        "expert",
        split_axis=0,
        concat_axis=0,
        tiled=True,
    )
    slot_rows = arrived.reshape(total_rows, model_width)
    stored = forward_whole(slot_rows, gate_full, up_full, down_full)
    returned = lax.all_to_all(
        stored[3].reshape(senders, capacity, model_width),
        "expert",
        split_axis=0,
        concat_axis=0,
        tiled=True,
    )
    picked = (
        returned.reshape(total_rows, model_width)[slot_place]
        .reshape(tok_rows, top_count, model_width)
        .astype(jnp.float32)
    )
    mixed_out = jnp.sum(route_probs[:, :, None] * picked, axis=1).astype(jnp.bfloat16)
    grad_wide = grad_out.astype(jnp.float32)
    grad_probs = jnp.sum(grad_wide[:, None, :] * picked, axis=2)
    scaled = (
        (route_probs[:, :, None] * grad_wide[:, None, :])
        .astype(jnp.bfloat16)
        .reshape(tok_rows * top_count, model_width)
    )
    grad_send = jnp.zeros((total_rows, model_width), jnp.bfloat16).at[slot_place].set(scaled)
    grad_in = lax.all_to_all(
        grad_send.reshape(senders, capacity, model_width),
        "expert",
        split_axis=0,
        concat_axis=0,
        tiled=True,
    ).reshape(total_rows, model_width)
    back_rows, grad_gate, grad_up, grad_down = backward_whole(
        slot_rows, stored, grad_in, gate_full, up_full, down_full
    )
    sent_back = lax.all_to_all(
        back_rows.reshape(senders, capacity, model_width),
        "expert",
        split_axis=0,
        concat_axis=0,
        tiled=True,
    )
    back_picked = sent_back.reshape(total_rows, model_width)[slot_place].reshape(
        tok_rows, top_count, model_width
    )
    grad_tokens = jnp.sum(back_picked.astype(jnp.float32), axis=1).astype(jnp.bfloat16)
    shares = (
        lax.psum_scatter(
            grad_gate[None].astype(jnp.bfloat16), "dp", scatter_dimension=1, tiled=True
        ).astype(jnp.float32),
        lax.psum_scatter(
            grad_up[None].astype(jnp.bfloat16), "dp", scatter_dimension=1, tiled=True
        ).astype(jnp.float32),
        lax.psum_scatter(
            grad_down[None].astype(jnp.bfloat16), "dp", scatter_dimension=2, tiled=True
        ).astype(jnp.float32),
    )
    return (
        mixed_out,
        grad_tokens,
        grad_probs,
        shares[0].astype(jnp.bfloat16),
        shares[1].astype(jnp.bfloat16),
        shares[2].astype(jnp.bfloat16),
    )


def solution(mesh):
    placed = (
        P(("dp", "expert"), None),
        P(("dp", "expert"), None),
        P(("dp", "expert"), None),
        P("expert", "dp", None),
        P("expert", "dp", None),
        P("expert", None, "dp"),
        P(("dp", "expert"), None),
    )
    return jax.shard_map(
        shards,
        mesh=mesh,
        in_specs=placed,
        out_specs=(
            P(("dp", "expert"), None),
            P(("dp", "expert"), None),
            P(("dp", "expert"), None),
            P("expert", "dp", None),
            P("expert", "dp", None),
            P("expert", None, "dp"),
        ),
        check_vma=False,
    )
```

profile of v0, /device:TPU:12, one launch (start us, length us, event | category | flops | bytes accessed | tf_op | source)
XLA Modules:
  0.0 398.8 jit_solution(18079659399550357771)
XLA Ops:
  7.2 0.0 copy-start
  7.2 0.7 broadcast_multiply_fusion
  7.9 0.8 copy.24
  8.7 0.1 eq.29
  8.8 0.1 eq.25
  9.0 0.1 copy.23
  9.1 0.1 mul.80
  9.3 0.6 reduce-window.6
  9.9 0.2 slice_reduce_fusion
  10.1 0.1 fusion.22
  10.2 0.0 copy-done
  10.2 5.0 %scatter_custom_fusion = bf16[1024,1024]{1,0:T(8,128)(2,1)} fusion(s32[256]{0:T(256)S(1)} %bitcast.81, bf16[]{:T(256)} %constant.26.clone.1, bf16[128,1024]{1,0:T(8,128)(2,1)S(1)} %copy-done, s32[1024]{0:T(1024)S(1)} %pad_clamp_fusion.1), kind=kCustom, calls=%fused_computation.23 | custom fusion | bytes 2097154 | tf_op jit(solution)/shard_map/scatter | solution.py:65
  15.2 10.3 %all-to-all-start = ((bf16[32,32,1024]{2,1,0:T(8,128)(2,1)}), bf16[32,32,1024]{2,1,0:T(8,128)(2,1)}, u32[]{:S(2)}, u32[]{:S(2)}) async-start(bf16[32,32,1024]{2,1,0:T(8,128)(2,1)} %bitcast.4), calls=%async_computation | async-start | bytes 4194304 | tf_op jit(solution)/shard_map/all_to_all | solution.py:73
  25.5 0.0 copy-done.8
  25.6 0.1 copy.22
  25.7 0.1 mul.85
  25.8 0.0 copy-done.3
  25.8 0.3 mul.87
  26.1 0.7 mul.88
  26.8 3.3 scatter_custom_fusion.1
  30.1 21.2 %all-to-all-done = bf16[32,32,1024]{2,1,0:T(8,128)(2,1)} async-done(((bf16[32,32,1024]{2,1,0:T(8,128)(2,1)}), bf16[32,32,1024]{2,1,0:T(8,128)(2,1)}, u32[]{:S(2)}, u32[]{:S(2)}) %all-to-all-start) | async-done | bytes 2097184 | tf_op jit(solution)/shard_map/all_to_all | solution.py:73
  51.3 8.4 %all-to-all-start.2 = ((bf16[32,32,1024]{2,1,0:T(8,128)(2,1)}), bf16[32,32,1024]{2,1,0:T(8,128)(2,1)S(1)}, u32[]{:S(2)}, u32[]{:S(2)}) async-start(bf16[32,32,1024]{2,1,0:T(8,128)(2,1)} %bitcast.76), calls=%async_computation.2 | async-start | bytes 4194304 | tf_op jit(solution)/shard_map/all_to_all | solution.py:103
  59.7 0.0 reduce-scatter.10.cloned.1.call-start
  59.8 0.0 copy-done.7
  59.8 37.6 %all_gather.9 = bf16[1,1024,384]{2,1,0:T(8,128)(2,1)S(1)} all-gather(bf16[1,64,384]{2,1,0:T(8,128)(2,1)S(1)} %copy-done.7), channel_id=1, replica_groups=mesh['dp'=16,'expert'=32] {'dp'}, dimensions={1}, use_global_device_ids=true | all-gather | bytes 835584 | tf_op jit(solution)/shard_map/all_gather | solution.py:68
  97.3 30.9 %all_gather.10 = bf16[1,1024,384]{2,1,0:T(8,128)(2,1)S(1)} all-gather(bf16[1,64,384]{2,1,0:T(8,128)(2,1)} %param.11), channel_id=1, replica_groups=mesh['dp'=16,'expert'=32] {'dp'}, dimensions={1}, use_global_device_ids=true | all-gather | bytes 835584 | tf_op jit(solution)/shard_map/all_gather | solution.py:69
  128.3 35.1 %all_gather.11 = bf16[1,384,1024]{1,2,0:T(8,128)(2,1)} all-gather(bf16[1,384,64]{1,2,0:T(8,128)(2,1)} %param.12), channel_id=1, replica_groups=mesh['dp'=16,'expert'=32] {'dp'}, dimensions={2}, use_global_device_ids=true | all-gather | bytes 835584 | tf_op jit(solution)/shard_map/all_gather | solution.py:70
  163.4 4.1 %fusion.12 = f32[1024,384]{1,0:T(8,128)} fusion(bf16[1024,1024]{1,0:T(8,128)(2,1)} %bitcast.5, bf16[1,1024,384]{2,1,0:T(8,128)(2,1)S(1)} %all_gather.10), kind=kOutput, calls=%fused_computation.30 | convolution fusion | flops 805306368 | bytes 4456448 | tf_op jit(solution)/shard_map/dot_general | solution.py:29
  167.5 0.0 copy-done.1
  167.5 4.0 fusion.16
  171.4 0.0 all-to-all-done.2
  171.4 5.1 %multiply_convert_fusion = (bf16[1024,384]{1,0:T(8,128)(2,1)}, bf16[1024,384]{1,0:T(8,128)(2,1)}, bf16[1024,384]{1,0:T(8,128)(2,1)S(1)}) fusion(f32[1024,384]{1,0:T(8,128)} %fusion.16, f32[1024,384]{1,0:T(8,128)} %fusion.12, bf16[1024,1024]{1,0:T(8,128)(2,1)S(1)} %bitcast.74, bf16[1,384,1024]{1,2,0:T(8,128)(2,1)} %all_gather.11), kind=kOutput, calls=%fused_computation.7 | convolution fusion | flops 811204608 | bytes 8388608 | tf_op jit(solution)/shard_map/dot_general | solution.py:22
  176.5 0.9 copy-done.4
  177.4 1.9 fusion.3
  179.3 4.1 %copy.30 = bf16[1,384,1024]{1,0,2:T(2,128)(2,1)S(1)} copy(bf16[1,384,1024]{2,1,0:T(8,128)(2,1)} %fusion.3) | data formatting | bytes 1572864
  183.5 1.0 copy.37
  184.5 0.0 reduce-scatter.10.cloned.1.call-update
  184.5 4.0 %convolution_convert_fusion = bf16[1024,1024]{1,0:T(8,128)(2,1)} fusion(bf16[1024,384]{1,0:T(8,128)(2,1)} %copy-done.4, bf16[1,384,1024]{1,2,0:T(8,128)(2,1)} %all_gather.11), kind=kOutput, calls=%fused_computation.6 | convolution fusion | flops 806354944 | bytes 3670016 | tf_op jit(solution)/shard_map/dot_general | solution.py:31
  188.6 7.9 %all-to-all-start.1 = ((bf16[32,32,1024]{2,1,0:T(8,128)(2,1)}), bf16[32,32,1024]{2,1,0:T(8,128)(2,1)S(1)}, u32[]{:S(2)}, u32[]{:S(2)}) async-start(bf16[32,32,1024]{2,1,0:T(8,128)(2,1)} %bitcast.80), calls=%async_computation.1 | async-start | bytes 4194304 | tf_op jit(solution)/shard_map/all_to_all | solution.py:82
  196.5 0.0 reduce-scatter.6.cloned.1.call-start
  196.5 4.0 fusion.1
  200.5 0.0 reduce-scatter.6.cloned.1.call-update
  200.5 0.0 copy-start.2
  200.5 2.5 fusion.14
  203.1 2.6 add_convert_fusion
  205.7 16.5 %all-to-all-done.1 = bf16[32,32,1024]{2,1,0:T(8,128)(2,1)S(1)} async-done(((bf16[32,32,1024]{2,1,0:T(8,128)(2,1)}), bf16[32,32,1024]{2,1,0:T(8,128)(2,1)S(1)}, u32[]{:S(2)}, u32[]{:S(2)}) %all-to-all-start.1) | async-done | bytes 2097184 | tf_op jit(solution)/shard_map/all_to_all | solution.py:82
  222.2 9.1 %all-to-all-start.3 = ((bf16[32,32,1024]{2,1,0:T(8,128)(2,1)}), bf16[32,32,1024]{2,1,0:T(8,128)(2,1)}, u32[]{:S(2)}, u32[]{:S(2)}) async-start(bf16[32,32,1024]{2,1,0:T(8,128)(2,1)} %bitcast.77), calls=%async_computation.3 | async-start | bytes 4194304 | tf_op jit(solution)/shard_map/all_to_all | solution.py:113
  231.3 0.3 reduce-scatter.8.cloned.1.call-start
  231.6 3.8 fusion.2
  235.3 0.0 reduce-scatter.8.cloned.1.call-update
  235.4 0.9 convert_element_type.75
  236.2 14.0 %reduce-scatter.10.cloned.1.call-done = bf16[64,384]{1,0:T(8,128)(2,1)} async-done(((bf16[1024,384]{1,0:T(8,128)(2,1)}), bf16[64,384]{1,0:T(8,128)(2,1)}) %reduce-scatter.10.cloned.1.call-update) | async-done | bytes 49168
  250.2 0.9 reshape_bitcast_fusion
  251.1 0.6 copy.29
  251.7 2.0 gather_fusion
  253.7 1.7 reshape.159
  255.4 3.6 multiply_reduce_fusion
  259.0 0.6 copy.28
  259.6 0.0 all-to-all-done.3
  259.6 3.4 gather_fusion.1
  263.0 0.2 reshape.158
  263.2 2.1 reduce_sum.44
  265.3 56.0 %reduce-scatter.6.cloned.1.call-done = bf16[1,64,384]{2,1,0:T(8,128)(2,1)} async-done(((bf16[1,1024,384]{2,1,0:T(8,128)(2,1)}), bf16[1,64,384]{2,1,0:T(8,128)(2,1)}) %reduce-scatter.6.cloned.1.call-update) | async-done | bytes 49168 | tf_op jit(solution)/shard_map/reduce_scatter | solution.py:125
  321.3 70.9 %reduce-scatter.8.cloned.1.call-done = bf16[1,64,384]{2,1,0:T(8,128)(2,1)} async-done(((bf16[1,1024,384]{2,1,0:T(8,128)(2,1)}), bf16[1,64,384]{2,1,0:T(8,128)(2,1)}) %reduce-scatter.8.cloned.1.call-update) | async-done | bytes 49168 | tf_op jit(solution)/shard_map/reduce_scatter | solution.py:128
  (17 shorter events, 0.1 us)
Async XLA Ops:
  7.2 3.0 copy-start
  15.2 10.3 %copy-start.8 = (f32[128,2]{0,1:T(2,128)S(1)}, f32[128,2]{0,1:T(2,128)}, u32[]{:S(2)}) copy-start(f32[128,2]{0,1:T(2,128)} %param.9) | copy-start | bytes 3076
  15.2 10.6 %copy-start.3 = (bf16[128,1024]{1,0:T(8,128)(2,1)S(1)}, bf16[128,1024]{1,0:T(8,128)(2,1)}, u32[]{:S(2)}) copy-start(bf16[128,1024]{1,0:T(8,128)(2,1)} %param.13) | copy-start | bytes 786436
  15.2 36.1 %all-to-all-start = ((bf16[32,32,1024]{2,1,0:T(8,128)(2,1)}), bf16[32,32,1024]{2,1,0:T(8,128)(2,1)}, u32[]{:S(2)}, u32[]{:S(2)}) async-start(bf16[32,32,1024]{2,1,0:T(8,128)(2,1)} %bitcast.4), calls=%async_computation | async-start | bytes 4194304 | tf_op jit(solution)/shard_map/all_to_all | solution.py:73
  51.3 8.4 %copy-start.7 = (bf16[1,64,384]{2,1,0:T(8,128)(2,1)S(1)}, bf16[1,64,384]{2,1,0:T(8,128)(2,1)}, u32[]{:S(2)}) copy-start(bf16[1,64,384]{2,1,0:T(8,128)(2,1)} %param.10) | copy-start | bytes 147460
  51.3 120.1 %all-to-all-start.2 = ((bf16[32,32,1024]{2,1,0:T(8,128)(2,1)}), bf16[32,32,1024]{2,1,0:T(8,128)(2,1)S(1)}, u32[]{:S(2)}, u32[]{:S(2)}) async-start(bf16[32,32,1024]{2,1,0:T(8,128)(2,1)} %bitcast.76), calls=%async_computation.2 | async-start | bytes 4194304 | tf_op jit(solution)/shard_map/all_to_all | solution.py:103
  59.7 190.5 %reduce-scatter.10.cloned.1.call-start = ((), (), s32[]{:S(2)}) async-start(), calls=%async_computation.9 | async-start | bytes 835584
  128.3 39.2 %copy-start.1 = (bf16[1,1024,384]{2,1,0:T(8,128)(2,1)}, bf16[1,1024,384]{2,1,0:T(8,128)(2,1)S(1)}, u32[]{:S(2)}) copy-start(bf16[1,1024,384]{2,1,0:T(8,128)(2,1)S(1)} %all_gather.10) | copy-start | bytes 2359300
  176.5 0.9 copy-start.4
  188.6 33.6 %all-to-all-start.1 = ((bf16[32,32,1024]{2,1,0:T(8,128)(2,1)}), bf16[32,32,1024]{2,1,0:T(8,128)(2,1)S(1)}, u32[]{:S(2)}, u32[]{:S(2)}) async-start(bf16[32,32,1024]{2,1,0:T(8,128)(2,1)} %bitcast.80), calls=%async_computation.1 | async-start | bytes 4194304 | tf_op jit(solution)/shard_map/all_to_all | solution.py:82
  196.5 124.8 %reduce-scatter.6.cloned.1.call-start = ((), (), s32[]{:S(2)}) async-start(), calls=%async_computation.7 | async-start | bytes 835584 | tf_op jit(solution)/shard_map/reduce_scatter | solution.py:125
  200.5 2.6 copy-start.2
  200.5 2.6 copy-start.5
  222.2 9.3 %copy-start.6 = (bf16[1024,384]{1,0:T(8,128)(2,1)S(1)}, bf16[1024,384]{1,0:T(8,128)(2,1)}, u32[]{:S(2)}) copy-start(bf16[1024,384]{1,0:T(8,128)(2,1)} %get-tuple-element.26) | copy-start | bytes 2359300
  222.2 37.4 %all-to-all-start.3 = ((bf16[32,32,1024]{2,1,0:T(8,128)(2,1)}), bf16[32,32,1024]{2,1,0:T(8,128)(2,1)}, u32[]{:S(2)}, u32[]{:S(2)}) async-start(bf16[32,32,1024]{2,1,0:T(8,128)(2,1)} %bitcast.77), calls=%async_computation.3 | async-start | bytes 4194304 | tf_op jit(solution)/shard_map/all_to_all | solution.py:113
  231.3 160.9 %reduce-scatter.8.cloned.1.call-start = ((), (), s32[]{:S(2)}) async-start(), calls=%async_computation.8 | async-start | bytes 835584 | tf_op jit(solution)/shard_map/reduce_scatter | solution.py:128
Sparse Core Ops, SparseCore 0:
  184.6 65.5 reduce-scatter.9
  253.8 67.4 reduce-scatter.5
  324.7 67.4 reduce-scatter.7
where the time goes:
time: 400 us; the launch traced here: 399 us
  waiting for transfers between devices  179 us (45%)
  blocking collectives  104 us (26%)
  starting transfers between devices  36 us (9%)
  matrix products  32 us (8%)
  local copies, waits for them, and re-layouts  23.2 us (6%)
  between operations  14 us (4%)
  other arithmetic  11.4 us (3%)
    reduce_scatter x1, waiting for transfers between devices, shards(): lax.psum_scatter(grad_up[None].astype(jnp.bfloat16), 'dp', scatter_dimens...  70.9 us
    reduce_scatter x1, waiting for transfers between devices, shards(): lax.psum_scatter(grad_gate[None].astype(jnp.bfloat16), 'dp', scatter_dime...  56 us
    all_gather x1, blocking collectives, shards(): lax.all_gather(w_gate, 'dp', axis=1, tiled=True)  37.6 us
    all_gather x1, blocking collectives, shards(): lax.all_gather(w_down, 'dp', axis=2, tiled=True)  35.1 us
    all_gather x1, blocking collectives, shards(): lax.all_gather(w_up, 'dp', axis=1, tiled=True)  30.9 us
    all_to_all x1, waiting for transfers between devices, shards(): lax.all_to_all(outgoing.reshape(senders, capacity, model_width), 'expert'...  21.2 us
    all_to_all x1, waiting for transfers between devices, shards(): lax.all_to_all(stored[3].reshape(senders, capacity, model_width), 'expert...  16.5 us
    unnamed x4, waiting for transfers between devices  14 us
  transfers between devices with their start and end apart: 7, of which 5 were waited for; matrix products, arithmetic and copies ran while one was open for 11% of the time, Pallas kernels for 0%

commit v1 on v0

v1 whole, which is shorter than its diff:
```python
import jax
import jax.numpy as jnp
from jax import lax
from jax.sharding import PartitionSpec as P


def route_slots(expert_ids, experts):
    flat_ids = expert_ids.reshape(-1)
    onehot = (flat_ids[:, None] == jnp.arange(experts, dtype=jnp.int32)[None, :]).astype(jnp.int32)
    before = jnp.cumsum(onehot, axis=0) - onehot
    slot_of = jnp.sum(before * onehot, axis=1)
    return flat_ids, slot_of


def contract_rows(left_op, right_op):
    return lax.dot_general(
        left_op, right_op, (((0,), (0,)), ((), ())), preferred_element_type=jnp.float32
    )


def contract_cols(left_op, right_op):
    return lax.dot_general(
        left_op, right_op, (((1,), (1,)), ((), ())), preferred_element_type=jnp.float32
    )


def shards(tokens, expert_ids, route_probs, w_gate, w_up, w_down, grad_out):
    senders = lax.axis_size("expert")
    tok_rows, model_width = tokens.shape
    top_count = expert_ids.shape[1]
    hidden_width = w_gate.shape[2]
    capacity = min(tok_rows, 4 * tok_rows * top_count // senders)
    total_rows = senders * capacity
    flat_ids, slot_of = route_slots(expert_ids, senders)
    token_of = jnp.arange(tok_rows * top_count, dtype=jnp.int32) // top_count

    packed = jnp.concatenate([w_gate[0], w_up[0], w_down[0].T], axis=1)
    whole = lax.all_gather(packed, "dp", axis=0, tiled=True)
    gate_up = whole[:, : 2 * hidden_width]
    down_t = whole[:, 2 * hidden_width :]

    grad_wide = grad_out.astype(jnp.float32)
    scaled = (
        (route_probs[:, :, None] * grad_wide[:, None, :])
        .astype(jnp.bfloat16)
        .reshape(tok_rows * top_count, model_width)
    )
    base = flat_ids * (2 * capacity) + slot_of
    places = jnp.concatenate([base, base + capacity])
    values = jnp.concatenate([tokens[token_of], scaled], axis=0)
    outgoing = jnp.zeros((2 * total_rows, model_width), jnp.bfloat16).at[places].set(values)
    arrived = lax.all_to_all(
        outgoing.reshape(senders, 2 * capacity, model_width),
        "expert",
        split_axis=0,
        concat_axis=0,
        tiled=True,
    )
    slot_rows = arrived[:, :capacity].reshape(total_rows, model_width)
    grad_in = arrived[:, capacity:].reshape(total_rows, model_width)

    both_pre = jnp.dot(slot_rows, gate_up, preferred_element_type=jnp.float32)
    gate_pre = both_pre[:, :hidden_width]
    up_pre = both_pre[:, hidden_width:]
    sigmoid_g = jax.nn.sigmoid(gate_pre)
    activated = gate_pre * sigmoid_g
    hidden = (activated * up_pre).astype(jnp.bfloat16)
    back_hidden = jnp.dot(grad_in, down_t, preferred_element_type=jnp.float32)
    back_gate = (back_hidden * up_pre * sigmoid_g * (1.0 + gate_pre * (1.0 - sigmoid_g))).astype(
        jnp.bfloat16
    )
    back_up = (back_hidden * activated).astype(jnp.bfloat16)
    back_both = jnp.concatenate([back_gate, back_up], axis=1)

    grad_terms = jnp.concatenate(
        [
            contract_rows(slot_rows, back_both).astype(jnp.bfloat16),
            contract_rows(grad_in, hidden).astype(jnp.bfloat16),
        ],
        axis=1,
    )
    summed = lax.psum_scatter(grad_terms, "dp", scatter_dimension=0, tiled=True)

    expert_out = contract_cols(hidden, down_t).astype(jnp.bfloat16)
    returned = lax.all_to_all(
        expert_out.reshape(senders, capacity, model_width),
        "expert",
        split_axis=0,
        concat_axis=0,
        tiled=True,
    )
    back_rows = contract_cols(back_both, gate_up).astype(jnp.bfloat16)
    sent_back = lax.all_to_all(
        back_rows.reshape(senders, capacity, model_width),
        "expert",
        split_axis=0,
        concat_axis=0,
        tiled=True,
    )

    slot_place = flat_ids * capacity + slot_of
    picked = (
        returned.reshape(total_rows, model_width)[slot_place]
        .reshape(tok_rows, top_count, model_width)
        .astype(jnp.float32)
    )
    mixed_out = jnp.sum(route_probs[:, :, None] * picked, axis=1).astype(jnp.bfloat16)
    grad_probs = jnp.sum(grad_wide[:, None, :] * picked, axis=2)
    back_picked = sent_back.reshape(total_rows, model_width)[slot_place].reshape(
        tok_rows, top_count, model_width
    )
    grad_tokens = jnp.sum(back_picked.astype(jnp.float32), axis=1).astype(jnp.bfloat16)

    summed = summed.astype(jnp.float32).astype(jnp.bfloat16)
    grad_w_gate = summed[:, :hidden_width][None]
    grad_w_up = summed[:, hidden_width : 2 * hidden_width][None]
    grad_w_down = summed[:, 2 * hidden_width :].T[None]
    return (mixed_out, grad_tokens, grad_probs, grad_w_gate, grad_w_up, grad_w_down)


def solution(mesh):
    placed = (
        P(("dp", "expert"), None),
        P(("dp", "expert"), None),
        P(("dp", "expert"), None),
        P("expert", "dp", None),
        P("expert", "dp", None),
        P("expert", None, "dp"),
        P(("dp", "expert"), None),
    )
    return jax.shard_map(
        shards,
        mesh=mesh,
        in_specs=placed,
        out_specs=(
            P(("dp", "expert"), None),
            P(("dp", "expert"), None),
            P(("dp", "expert"), None),
            P("expert", "dp", None),
            P("expert", "dp", None),
            P("expert", None, "dp"),
        ),
        check_vma=False,
    )
```

time: 400 us -> 217 us (0.54)
  the two profiles are of different devices: /device:TPU:12 before, /device:TPU:32 now
where the time goes in v1:
time: 217 us; the launch traced here: 216 us
  waiting for transfers between devices  128 us (59%)
  local copies, waits for them, and re-layouts  23.9 us (11%)
  starting transfers between devices  20.3 us (9%)
  matrix products  17.4 us (8%)
  between operations  14.4 us (7%)
  other arithmetic  11.7 us (5%)
    all_to_all x1, waiting for transfers between devices, shards(): lax.all_to_all(outgoing.reshape(senders, 2 * capacity, model_width), 'exp...  52.5 us
    all_to_all x1, waiting for transfers between devices, shards(): lax.all_to_all(back_rows.reshape(senders, capacity, model_width), 'expert...  26.2 us
    all_to_all x1, waiting for transfers between devices, shards(): lax.all_to_all(expert_out.reshape(senders, capacity, model_width), 'exper...  25.9 us
    all_gather x1, waiting for transfers between devices, shards(): whole = lax.all_gather(packed, 'dp', axis=0, tiled=True)  23.6 us
    unnamed x34, local copies, waits for them, and re-layouts  9.42 us
    dot_general x2, matrix products, contract_cols(): lax.dot_general(left_op, right_op, (((1,), (1,)), ((), ())), preferred_el...  8.33 us
    all_to_all x1, starting transfers between devices, shards(): lax.all_to_all(outgoing.reshape(senders, 2 * capacity, model_width), 'exp...  7.58 us
    all_to_all x1, starting transfers between devices, shards(): lax.all_to_all(back_rows.reshape(senders, capacity, model_width), 'expert...  7.32 us
  transfers between devices with their start and end apart: 5, of which 4 were waited for; matrix products, arithmetic and copies ran while one was open for 11% of the time, Pallas kernels for 0%

profile of v1, /device:TPU:32, one launch (start us, length us, event | category | flops | bytes accessed | tf_op | source)
XLA Modules:
  0.0 215.9 jit_solution(539977144438162739)
XLA Ops:
  7.2 0.0 copy-start
  7.2 0.8 copy.27
  8.0 0.1 eq.26
  8.1 0.1 reshape.222
  8.3 0.6 reduce-window.6
  8.9 0.2 slice_reduce_fusion
  9.1 0.1 fusion.14
  9.3 0.8 copy.26
  10.0 0.1 mul.107
  10.2 1.2 mul.109
  11.4 0.7 mul.110
  12.2 0.1 multiply_convert_fusion.3
  12.3 0.0 copy-done
  12.3 1.2 gather_fusion
  13.5 5.2 %scatter_custom_fusion = bf16[2048,1024]{1,0:T(8,128)(2,1)} fusion(s32[512]{0:T(512)S(1)} %bitcast.67, bf16[]{:T(256)} %constant.15.clone.1, bf16[256,1024]{1,0:T(8,128)(2,1)S(1)} %multiply_convert_fusion.3, bf16[]{:T(256)} %constant.48, bf16[256,1024]{1,0:T(8,128)(2,1)S(1)} %gather_fusion), kind=kCustom, calls=%fused_computation.5 | custom fusion | flops 2097152 | bytes 5242884 | tf_op jit(solution)/shard_map/scatter | solution.py:51
  18.7 7.6 %all-to-all-start = ((bf16[32,64,1024]{2,1,0:T(8,128)(2,1)}), bf16[32,64,1024]{2,1,0:T(8,128)(2,1)}, u32[]{:S(2)}, u32[]{:S(2)}) async-start(bf16[32,64,1024]{2,1,0:T(8,128)(2,1)} %bitcast.50), calls=%async_computation | async-start | bytes 8388608 | tf_op jit(solution)/shard_map/all_to_all | solution.py:52
  26.3 0.0 all-gather.2.cloned.1.call-start
  26.4 0.0 copy-done.3
  26.4 0.0 copy-done.4
  26.4 0.0 copy-done.5
  26.4 0.7 pad_maximum_fusion.4
  27.1 0.0 all-gather.2.cloned.1.call-update
  27.1 0.2 reduce-scatter.4.cloned.1.call-start
  27.3 52.5 %all-to-all-done = bf16[32,64,1024]{2,1,0:T(8,128)(2,1)} async-done(((bf16[32,64,1024]{2,1,0:T(8,128)(2,1)}), bf16[32,64,1024]{2,1,0:T(8,128)(2,1)}, u32[]{:S(2)}, u32[]{:S(2)}) %all-to-all-start) | async-done | bytes 4194336 | tf_op jit(solution)/shard_map/all_to_all | solution.py:52
  79.8 4.2 %fusion.18 = (bf16[32,32,1024]{2,1,0:T(8,128)(2,1)}, bf16[32,32,1024]{2,1,0:T(8,128)(2,1)S(1)}) fusion(bf16[32,64,1024]{2,1,0:T(8,128)(2,1)} %all-to-all-done), kind=kLoop, calls=%fused_computation.53 | loop fusion | bytes 8388608 | tf_op jit(solution)/shard_map/slice | solution.py:60
  84.0 23.6 %all-gather.2.cloned.1.call-done = bf16[1024,1152]{1,0:T(8,128)(2,1)} async-done(((bf16[64,1152]{1,0:T(8,128)(2,1)}), bf16[1024,1152]{1,0:T(8,128)(2,1)}) %all-gather.2.cloned.1.call-update) | async-done | bytes 2359312 | tf_op jit(solution)/shard_map/all_gather | solution.py:38
  107.7 3.4 %fusion.4 = f32[1024,768]{0,1:T(8,128)S(1)} fusion(bf16[1024,1024]{1,0:T(8,128)(2,1)S(1)} %bitcast.53, bf16[1024,1152]{1,0:T(8,128)(2,1)} %all-gather.2.cloned.1.call-done), kind=kOutput, calls=%fused_computation.18 | convolution fusion | flops 1610612736 | bytes 6815744 | tf_op jit(solution)/shard_map/dot_general | solution.py:62
  111.1 0.0 copy-done.1
  111.1 2.8 %multiply_convert_fusion.1 = (bf16[1024,384]{0,1:T(8,128)(2,1)S(1)}, bf16[1024,384]{0,1:T(8,128)(2,1)S(1)}, bf16[1024,384]{0,1:T(8,128)(2,1)S(1)}) fusion(f32[1024,768]{0,1:T(8,128)S(1)} %fusion.4, bf16[1024,1024]{1,0:T(8,128)(2,1)S(1)} %bitcast.55, bf16[1024,1152]{1,0:T(8,128)(2,1)} %all-gather.2.cloned.1.call-done), kind=kOutput, calls=%fused_computation.12 | convolution fusion | flops 811204608 | bytes 8388608 | tf_op jit(solution)/shard_map/dot_general | solution.py:68
  113.9 0.0 copy-start.8
  113.9 0.0 copy-start.10
  113.9 0.0 copy-start.11
  114.0 1.0 convolution_convert_fusion.3
  115.0 0.0 copy-done.8
  115.0 0.1 copy-done.10
  115.1 0.3 copy-done.11
  115.4 1.8 convolution_convert_fusion.2
  117.2 0.2 pad_maximum_fusion
  117.4 2.6 %copy.36 = bf16[1024,1152]{1,0:T(8,128)(2,1)} copy(bf16[1024,1152]{0,1:T(8,128)(2,1)S(1)} %pad_maximum_fusion) | data formatting | bytes 4718592
  120.0 0.0 reduce-scatter.4.cloned.1.call-update
  120.0 1.6 copy-done.7
  121.6 4.5 %convolution_convert_fusion.1 = bf16[1024,1024]{1,0:T(8,128)(2,1)} fusion(bf16[1024,1152]{1,0:T(8,128)(2,1)S(1)} %copy-done.7, bf16[1024,384]{0,1:T(8,128)(2,1)} %copy-done.11, bf16[1024,384]{0,1:T(8,128)(2,1)} %copy-done.10), kind=kOutput, calls=%fused_computation.8 | convolution fusion | flops 1614807040 | bytes 5242880 | tf_op jit(solution)/shard_map/dot_general | solution.py:22
  126.2 7.3 %all-to-all-start.2 = ((bf16[32,32,1024]{2,1,0:T(8,128)(2,1)}), bf16[32,32,1024]{2,1,0:T(8,128)(2,1)S(1)}, u32[]{:S(2)}, u32[]{:S(2)}) async-start(bf16[32,32,1024]{2,1,0:T(8,128)(2,1)} %bitcast.52), calls=%async_computation.2 | async-start | bytes 4194304 | tf_op jit(solution)/shard_map/all_to_all | solution.py:93
  133.5 3.8 %convolution_convert_fusion = bf16[1024,1024]{1,0:T(8,128)(2,1)} fusion(bf16[1024,384]{0,1:T(8,128)(2,1)S(1)} %copy-done.9, bf16[1024,1152]{1,0:T(8,128)(2,1)} %all-gather.2.cloned.1.call-done), kind=kOutput, calls=%fused_computation.7 | convolution fusion | flops 806354944 | bytes 3670016 | tf_op jit(solution)/shard_map/dot_general | solution.py:22
  137.3 26.2 %all-to-all-done.2 = bf16[32,32,1024]{2,1,0:T(8,128)(2,1)S(1)} async-done(((bf16[32,32,1024]{2,1,0:T(8,128)(2,1)}), bf16[32,32,1024]{2,1,0:T(8,128)(2,1)S(1)}, u32[]{:S(2)}, u32[]{:S(2)}) %all-to-all-start.2) | async-done | bytes 2097184 | tf_op jit(solution)/shard_map/all_to_all | solution.py:93
  163.5 5.1 %all-to-all-start.1 = ((bf16[32,32,1024]{2,1,0:T(8,128)(2,1)}), bf16[32,32,1024]{2,1,0:T(8,128)(2,1)}, u32[]{:S(2)}, u32[]{:S(2)}) async-start(bf16[32,32,1024]{2,1,0:T(8,128)(2,1)} %bitcast.51), calls=%async_computation.1 | async-start | bytes 4194304 | tf_op jit(solution)/shard_map/all_to_all | solution.py:85
  168.6 0.0 copy-done.2
  168.7 0.1 copy.31
  168.8 0.1 mul.115
  169.0 1.2 gather_fusion.2
  170.1 0.2 reshape.231
  170.4 2.1 reduce_sum.44
  172.4 25.9 %all-to-all-done.1 = bf16[32,32,1024]{2,1,0:T(8,128)(2,1)} async-done(((bf16[32,32,1024]{2,1,0:T(8,128)(2,1)}), bf16[32,32,1024]{2,1,0:T(8,128)(2,1)}, u32[]{:S(2)}, u32[]{:S(2)}) %all-to-all-start.1) | async-done | bytes 2097184 | tf_op jit(solution)/shard_map/all_to_all | solution.py:85
  198.4 3.4 %gather_fusion.1 = bf16[256,1024]{1,0:T(8,128)(2,1)S(1)} fusion(bf16[1024,1024]{1,0:T(8,128)(2,1)} %bitcast.12, s32[1024]{0:T(1024)S(1)} %pad_clamp_fusion), kind=kCustom, calls=%fused_computation.1 | custom fusion | bytes 1049600 | tf_op jit(solution)/shard_map/gather | solution.py:103
  201.8 0.7 reshape.232
  202.4 2.6 %multiply_reduce_fusion = (f32[128,2]{1,0:T(8,128)S(1)}, bf16[128,1024]{1,0:T(8,128)(2,1)}) fusion(f32[128,2,1024]{2,1,0:T(2,128)S(1)} %reshape.232, f32[128,1024]{1,0:T(8,128)S(1)} %convert_element_type.54, f32[128,2]{1,0:T(8,128)S(1)} %copy.26), kind=kLoop, calls=%fused_computation.23 | loop fusion | flops 917248 | bytes 1837056 | tf_op jit(solution)/shard_map/reduce_sum | solution.py:108
  205.0 0.6 copy.32
  205.6 0.9 fusion.19
  206.5 0.1 copy.38
  206.6 0.7 copy.33
  207.3 0.1 copy.39
  207.5 0.7 copy.34
  208.2 0.1 copy.40
  208.3 0.7 copy.35
  (22 shorter events, 0.2 us)
Async XLA Ops:
  7.2 5.1 %copy-start = (bf16[128,1024]{1,0:T(8,128)(2,1)S(1)}, bf16[128,1024]{1,0:T(8,128)(2,1)}, u32[]{:S(2)}) copy-start(bf16[128,1024]{1,0:T(8,128)(2,1)} %param.7) | copy-start | bytes 786436
  18.7 7.6 %copy-start.3 = (bf16[1,384,64]{1,2,0:T(8,128)(2,1)S(1)}, bf16[1,384,64]{1,2,0:T(8,128)(2,1)}, u32[]{:S(2)}) copy-start(bf16[1,384,64]{1,2,0:T(8,128)(2,1)} %param.12) | copy-start | bytes 147460
  18.7 7.7 %copy-start.4 = (bf16[1,64,384]{2,1,0:T(8,128)(2,1)S(1)}, bf16[1,64,384]{2,1,0:T(8,128)(2,1)}, u32[]{:S(2)}) copy-start(bf16[1,64,384]{2,1,0:T(8,128)(2,1)} %param.11) | copy-start | bytes 147460
  18.7 7.7 %copy-start.5 = (bf16[1,64,384]{2,1,0:T(8,128)(2,1)S(1)}, bf16[1,64,384]{2,1,0:T(8,128)(2,1)}, u32[]{:S(2)}) copy-start(bf16[1,64,384]{2,1,0:T(8,128)(2,1)} %param.10) | copy-start | bytes 147460
  18.7 61.1 %all-to-all-start = ((bf16[32,64,1024]{2,1,0:T(8,128)(2,1)}), bf16[32,64,1024]{2,1,0:T(8,128)(2,1)}, u32[]{:S(2)}, u32[]{:S(2)}) async-start(bf16[32,64,1024]{2,1,0:T(8,128)(2,1)} %bitcast.50), calls=%async_computation | async-start | bytes 8388608 | tf_op jit(solution)/shard_map/all_to_all | solution.py:52
  26.3 81.3 %all-gather.2.cloned.1.call-start = ((), (), s32[]{:S(2)}) async-start(), calls=%async_computation.4 | async-start | bytes 2506752 | tf_op jit(solution)/shard_map/all_gather | solution.py:38
  27.1 178.5 %reduce-scatter.4.cloned.1.call-start = ((), (), s32[]{:S(2)}) async-start(), calls=%async_computation.5 | async-start | bytes 2506752
  107.7 3.4 %copy-start.1 = (bf16[32,32,1024]{2,1,0:T(8,128)(2,1)S(1)}, bf16[32,32,1024]{2,1,0:T(8,128)(2,1)}, u32[]{:S(2)}) copy-start(bf16[32,32,1024]{2,1,0:T(8,128)(2,1)} %get-tuple-element.30) | copy-start | bytes 6291460
  113.9 1.0 copy-start.8
  113.9 1.1 copy-start.10
  113.9 1.4 copy-start.11
  120.0 1.7 copy-start.7
  126.2 7.3 %copy-start.9 = (bf16[1024,384]{0,1:T(8,128)(2,1)S(1)}, bf16[1024,384]{0,1:T(8,128)(2,1)}, u32[]{:S(2)}) copy-start(bf16[1024,384]{0,1:T(8,128)(2,1)} %copy-done.8) | copy-start | bytes 2359300
  126.2 37.3 %all-to-all-start.2 = ((bf16[32,32,1024]{2,1,0:T(8,128)(2,1)}), bf16[32,32,1024]{2,1,0:T(8,128)(2,1)S(1)}, u32[]{:S(2)}, u32[]{:S(2)}) async-start(bf16[32,32,1024]{2,1,0:T(8,128)(2,1)} %bitcast.52), calls=%async_computation.2 | async-start | bytes 4194304 | tf_op jit(solution)/shard_map/all_to_all | solution.py:93
  163.5 5.1 %copy-start.2 = (bf16[128,1024]{1,0:T(8,128)(2,1)S(1)}, bf16[128,1024]{1,0:T(8,128)(2,1)}, u32[]{:S(2)}) copy-start(bf16[128,1024]{1,0:T(8,128)(2,1)} %param.13) | copy-start | bytes 786436
  163.5 5.2 %copy-start.6 = (s32[128,2]{0,1:T(2,128)S(1)}, s32[128,2]{0,1:T(2,128)}, u32[]{:S(2)}) copy-start(s32[128,2]{0,1:T(2,128)} %param.8) | copy-start | bytes 3076
  163.5 34.9 %all-to-all-start.1 = ((bf16[32,32,1024]{2,1,0:T(8,128)(2,1)}), bf16[32,32,1024]{2,1,0:T(8,128)(2,1)}, u32[]{:S(2)}, u32[]{:S(2)}) async-start(bf16[32,32,1024]{2,1,0:T(8,128)(2,1)} %bitcast.51), calls=%async_computation.1 | async-start | bytes 4194304 | tf_op jit(solution)/shard_map/all_to_all | solution.py:85
Sparse Core Ops, SparseCore 0:
  29.8 77.7 all-gather.1
  120.1 70.5 reduce-scatter.3

commit v2 on v1

--- a/solution.py
+++ b/solution.py
@@ -35,7 +35,7 @@
     token_of = jnp.arange(tok_rows * top_count, dtype=jnp.int32) // top_count
 
     packed = jnp.concatenate([w_gate[0], w_up[0], w_down[0].T], axis=1)
-    whole = lax.all_gather(packed, "dp", axis=0, tiled=True)
+    whole = lax.all_gather(packed[None], "dp", axis=1, tiled=True)[0]
     gate_up = whole[:, : 2 * hidden_width]
     down_t = whole[:, 2 * hidden_width :]
 
@@ -82,21 +82,17 @@
     summed = lax.psum_scatter(grad_terms, "dp", scatter_dimension=0, tiled=True)
 
     expert_out = contract_cols(hidden, down_t).astype(jnp.bfloat16)
-    returned = lax.all_to_all(
-        expert_out.reshape(senders, capacity, model_width),
-        "expert",
-        split_axis=0,
-        concat_axis=0,
-        tiled=True,
+    back_rows = contract_cols(back_both, gate_up).astype(jnp.bfloat16)
+    leaving = jnp.concatenate(
+        [
+            expert_out.reshape(senders, capacity, model_width),
+            back_rows.reshape(senders, capacity, model_width),
+        ],
+        axis=1,
     )
-    back_rows = contract_cols(back_both, gate_up).astype(jnp.bfloat16)
-    sent_back = lax.all_to_all(
-        back_rows.reshape(senders, capacity, model_width),
-        "expert",
-        split_axis=0,
-        concat_axis=0,
-        tiled=True,
-    )
+    back_home = lax.all_to_all(leaving, "expert", split_axis=0, concat_axis=0, tiled=True)
+    returned = back_home[:, :capacity]
+    sent_back = back_home[:, capacity:]
 
     slot_place = flat_ids * capacity + slot_of
     picked = (

time: 217 us -> 218 us (level)
  local copies, waits for them, and re-layouts: 23.9 us -> 29.9 us
  starting transfers between devices: 20.3 us -> 15.5 us
  other arithmetic: 11.7 us -> 16.3 us
  matrix products: 17.4 us -> 13.6 us
    all_to_all x2 -> x1, starting transfers between devices: 12.4 us -> 7.66 us  [shards(): lax.all_to_all(leaving, 'expert', split_axis=0, concat_axis=0, tiled=True)]
    slice x2 -> x3, local copies, waits for them, and re-layouts: 4.39 us -> 8.58 us  [the longest x1 4.2 us: shards(): slot_rows = arrived[:, :capacity].reshape(total_rows, model_width)]
    dot_general x2, matrix products: 8.33 us -> 4.6 us  [contract_cols(): lax.dot_general(left_op, right_op, (((1,), (1,)), ((), ())), preferred_el...]
    concatenate x0 -> x1, other arithmetic: none -> 2.69 us  [shards(): jnp.concatenate([expert_out.reshape(senders, capacity, model_width), back...]
    all_to_all x2 -> x1, waiting for transfers between devices: 52.1 us -> 52.1 us  [shards(): lax.all_to_all(leaving, 'expert', split_axis=0, concat_axis=0, tiled=True)]
  transfers between devices with their start and end apart: 5 -> 4, of which waited for: 4 -> 3; matrix products, arithmetic and copies ran while one was open for 11% -> 14% of each run, Pallas kernels for 0% -> 0%
where the time goes in v2:
time: 218 us
  waiting for transfers between devices  128 us (59%)
  local copies, waits for them, and re-layouts  29.9 us (14%)
  other arithmetic  16.3 us (7%)
  starting transfers between devices  15.5 us (7%)
  between operations  14.3 us (7%)
  matrix products  13.6 us (6%)
    all_to_all x1, waiting for transfers between devices, shards(): lax.all_to_all(outgoing.reshape(senders, 2 * capacity, model_width), 'exp...  52.5 us
    all_to_all x1, waiting for transfers between devices, shards(): lax.all_to_all(leaving, 'expert', split_axis=0, concat_axis=0, tiled=True)  52.1 us
    all_gather x1, waiting for transfers between devices, shards(): whole = lax.all_gather(packed[None], 'dp', axis=1, tiled=True)[0]  23.6 us
    unnamed x34, local copies, waits for them, and re-layouts  9.36 us
    all_to_all x1, starting transfers between devices, shards(): lax.all_to_all(leaving, 'expert', split_axis=0, concat_axis=0, tiled=True)  7.66 us
    all_to_all x1, starting transfers between devices, shards(): lax.all_to_all(outgoing.reshape(senders, 2 * capacity, model_width), 'exp...  7.58 us
    scatter x1, other arithmetic, shards(): jnp.zeros((2 * total_rows, model_width), jnp.bfloat16).at[places]  5.25 us
    dot_general x2, matrix products, contract_cols(): lax.dot_general(left_op, right_op, (((1,), (1,)), ((), ())), preferred_el...  4.6 us
  transfers between devices with their start and end apart: 4, of which 3 were waited for; matrix products, arithmetic and copies ran while one was open for 14% of the time, Pallas kernels for 0%

profile of v2, /device:TPU:32, one launch (start us, length us, event | category | flops | bytes accessed | tf_op | source)
XLA Modules:
  0.0 217.9 jit_solution(8114677060737856817)
XLA Ops:
  7.2 0.0 copy-start
  7.2 0.8 copy.27
  8.0 0.1 eq.26
  8.1 0.1 reshape.222
  8.3 0.6 reduce-window.6
  8.9 0.2 slice_reduce_fusion
  9.1 0.1 fusion.14
  9.3 0.8 copy.26
  10.0 0.1 mul.107
  10.2 1.2 mul.109
  11.4 0.7 mul.110
  12.2 0.1 multiply_convert_fusion.3
  12.3 0.0 copy-done
  12.3 1.2 gather_fusion
  13.5 5.3 %scatter_custom_fusion = bf16[2048,1024]{1,0:T(8,128)(2,1)} fusion(s32[512]{0:T(512)S(1)} %bitcast.68, bf16[]{:T(256)} %constant.15.clone.1, bf16[256,1024]{1,0:T(8,128)(2,1)S(1)} %multiply_convert_fusion.3, bf16[]{:T(256)} %constant.48, bf16[256,1024]{1,0:T(8,128)(2,1)S(1)} %gather_fusion), kind=kCustom, calls=%fused_computation.6 | custom fusion | flops 2097152 | bytes 5242884 | tf_op jit(solution)/shard_map/scatter | solution.py:51
  18.7 7.6 %all-to-all-start = ((bf16[32,64,1024]{2,1,0:T(8,128)(2,1)}), bf16[32,64,1024]{2,1,0:T(8,128)(2,1)}, u32[]{:S(2)}, u32[]{:S(2)}) async-start(bf16[32,64,1024]{2,1,0:T(8,128)(2,1)} %bitcast.51), calls=%async_computation | async-start | bytes 8388608 | tf_op jit(solution)/shard_map/all_to_all | solution.py:52
  26.3 0.0 all-gather.3.cloned.1.call-start
  26.4 0.0 copy-done.3
  26.4 0.0 copy-done.4
  26.4 0.0 copy-done.5
  26.4 0.7 pad_maximum_fusion.5
  27.1 0.0 all-gather.3.cloned.1.call-update
  27.1 0.2 reduce-scatter.4.cloned.1.call-start
  27.3 52.5 %all-to-all-done = bf16[32,64,1024]{2,1,0:T(8,128)(2,1)} async-done(((bf16[32,64,1024]{2,1,0:T(8,128)(2,1)}), bf16[32,64,1024]{2,1,0:T(8,128)(2,1)}, u32[]{:S(2)}, u32[]{:S(2)}) %all-to-all-start) | async-done | bytes 4194336 | tf_op jit(solution)/shard_map/all_to_all | solution.py:52
  79.8 4.2 %fusion.19 = (bf16[32,32,1024]{2,1,0:T(8,128)(2,1)S(1)}, bf16[32,32,1024]{2,1,0:T(8,128)(2,1)}) fusion(bf16[32,64,1024]{2,1,0:T(8,128)(2,1)} %all-to-all-done), kind=kLoop, calls=%fused_computation.55 | loop fusion | bytes 8388608 | tf_op jit(solution)/shard_map/slice | solution.py:59
  84.0 23.6 %all-gather.3.cloned.1.call-done = bf16[1024,1152]{1,0:T(8,128)(2,1)} async-done(((bf16[64,1152]{1,0:T(8,128)(2,1)}), bf16[1024,1152]{1,0:T(8,128)(2,1)}) %all-gather.3.cloned.1.call-update) | async-done | bytes 2359312 | tf_op jit(solution)/shard_map/all_gather | solution.py:38
  107.7 3.4 %fusion.4 = f32[1024,768]{0,1:T(8,128)S(1)} fusion(bf16[1024,1024]{1,0:T(8,128)(2,1)S(1)} %bitcast.52, bf16[1024,1152]{1,0:T(8,128)(2,1)} %all-gather.3.cloned.1.call-done), kind=kOutput, calls=%fused_computation.19 | convolution fusion | flops 1610612736 | bytes 6815744 | tf_op jit(solution)/shard_map/dot_general | solution.py:62
  111.1 0.0 copy-done.1
  111.1 2.8 %multiply_convert_fusion.1 = (bf16[1024,384]{0,1:T(8,128)(2,1)S(1)}, bf16[1024,384]{0,1:T(8,128)(2,1)S(1)}, bf16[1024,384]{0,1:T(8,128)(2,1)S(1)}) fusion(f32[1024,768]{0,1:T(8,128)S(1)} %fusion.4, bf16[1024,1024]{1,0:T(8,128)(2,1)S(1)} %bitcast.54, bf16[1024,1152]{1,0:T(8,128)(2,1)} %all-gather.3.cloned.1.call-done), kind=kOutput, calls=%fused_computation.13 | convolution fusion | flops 811204608 | bytes 8388608 | tf_op jit(solution)/shard_map/dot_general | solution.py:68
  113.9 0.0 copy-start.8
  113.9 0.0 copy-start.10
  114.0 0.0 copy-start.11
  114.0 1.0 convolution_convert_fusion.3
  115.0 0.0 copy-done.8
  115.0 0.1 copy-done.10
  115.1 0.3 copy-done.11
  115.3 1.8 convolution_convert_fusion.2
  117.2 0.2 pad_maximum_fusion.1
  117.4 2.5 %copy.36 = bf16[1024,1152]{1,0:T(8,128)(2,1)} copy(bf16[1024,1152]{0,1:T(8,128)(2,1)S(1)} %pad_maximum_fusion.1) | data formatting | bytes 4718592
  119.9 0.0 reduce-scatter.4.cloned.1.call-update
  119.9 1.6 copy-done.7
  121.6 3.3 %convolution_convert_fusion.1 = bf16[1024,1024]{1,0:T(8,128)(2,1)S(1)} fusion(bf16[1024,1152]{1,0:T(8,128)(2,1)S(1)} %copy-done.7, bf16[1024,384]{0,1:T(8,128)(2,1)} %copy-done.11, bf16[1024,384]{0,1:T(8,128)(2,1)} %copy-done.10), kind=kOutput, calls=%fused_computation.9 | convolution fusion | flops 1614807040 | bytes 5242880 | tf_op jit(solution)/shard_map/dot_general | solution.py:22
  124.9 1.3 convolution_convert_fusion
  126.2 2.7 %pad_maximum_fusion = bf16[32,64,1024]{2,1,0:T(8,128)(2,1)} fusion(bf16[32,32,1024]{2,1,0:T(8,128)(2,1)S(1)} %bitcast.56, bf16[32,32,1024]{2,1,0:T(8,128)(2,1)S(1)} %bitcast.57), kind=kLoop, calls=%fused_computation.4 | loop fusion | flops 8388608 | bytes 8388608 | tf_op jit(solution)/shard_map/concatenate | solution.py:86
  128.9 7.7 %all-to-all-start.1 = ((bf16[32,64,1024]{2,1,0:T(8,128)(2,1)}), bf16[32,64,1024]{2,1,0:T(8,128)(2,1)}, u32[]{:S(2)}, u32[]{:S(2)}) async-start(bf16[32,64,1024]{2,1,0:T(8,128)(2,1)} %pad_maximum_fusion), calls=%async_computation.1 | async-start | bytes 8388608 | tf_op jit(solution)/shard_map/all_to_all | solution.py:93
  136.6 0.8 convert_element_type.54
  137.4 0.1 copy.31
  137.5 0.1 mul.120
  137.7 52.1 %all-to-all-done.1 = bf16[32,64,1024]{2,1,0:T(8,128)(2,1)} async-done(((bf16[32,64,1024]{2,1,0:T(8,128)(2,1)}), bf16[32,64,1024]{2,1,0:T(8,128)(2,1)}, u32[]{:S(2)}, u32[]{:S(2)}) %all-to-all-start.1) | async-done | bytes 4194336 | tf_op jit(solution)/shard_map/all_to_all | solution.py:93
  189.8 4.2 %fusion.18 = (bf16[32,32,1024]{2,1,0:T(8,128)(2,1)S(1)}, bf16[32,32,1024]{2,1,0:T(8,128)(2,1)}) fusion(bf16[32,64,1024]{2,1,0:T(8,128)(2,1)} %all-to-all-done.1), kind=kLoop, calls=%fused_computation.54 | loop fusion | bytes 8388608 | tf_op jit(solution)/shard_map/slice | solution.py:95
  194.0 4.2 %gather_fusion.1 = bf16[256,1024]{1,0:T(8,128)(2,1)} fusion(bf16[1024,1024]{1,0:T(8,128)(2,1)} %bitcast.50, s32[1024]{0:T(1024)S(1)} %pad_clamp_fusion), kind=kCustom, calls=%fused_computation.1 | custom fusion | bytes 1049600 | tf_op jit(solution)/shard_map/gather | solution.py:99
  198.2 1.7 reshape.232
  199.9 3.6 %multiply_reduce_fusion = (f32[128,2]{1,0:T(8,128)S(1)}, bf16[128,1024]{1,0:T(8,128)(2,1)}) fusion(f32[128,2,1024]{2,1,0:T(2,128)S(1)} %reshape.232, f32[128,1024]{1,0:T(8,128)} %convert_element_type.54, f32[128,2]{1,0:T(8,128)S(1)} %copy.26), kind=kLoop, calls=%fused_computation.24 | loop fusion | flops 917248 | bytes 1837056 | tf_op jit(solution)/shard_map/reduce_sum | solution.py:104
  203.5 0.6 copy.32
  204.2 1.2 gather_fusion.2
  205.4 0.2 reshape.231
  205.6 2.1 reduce_sum.44
  207.6 0.9 fusion.20
  208.5 0.1 copy.38
  208.6 0.7 copy.33
  209.4 0.1 copy.39
  209.5 0.7 copy.34
  210.2 0.1 copy.40
  210.3 0.7 copy.35
  (22 shorter events, 0.1 us)
Async XLA Ops:
  7.2 5.1 %copy-start = (bf16[128,1024]{1,0:T(8,128)(2,1)S(1)}, bf16[128,1024]{1,0:T(8,128)(2,1)}, u32[]{:S(2)}) copy-start(bf16[128,1024]{1,0:T(8,128)(2,1)} %param.7) | copy-start | bytes 786436
  18.7 7.6 %copy-start.3 = (bf16[1,384,64]{1,2,0:T(8,128)(2,1)S(1)}, bf16[1,384,64]{1,2,0:T(8,128)(2,1)}, u32[]{:S(2)}) copy-start(bf16[1,384,64]{1,2,0:T(8,128)(2,1)} %param.12) | copy-start | bytes 147460
  18.7 7.7 %copy-start.4 = (bf16[1,64,384]{2,1,0:T(8,128)(2,1)S(1)}, bf16[1,64,384]{2,1,0:T(8,128)(2,1)}, u32[]{:S(2)}) copy-start(bf16[1,64,384]{2,1,0:T(8,128)(2,1)} %param.11) | copy-start | bytes 147460
  18.7 7.7 %copy-start.5 = (bf16[1,64,384]{2,1,0:T(8,128)(2,1)S(1)}, bf16[1,64,384]{2,1,0:T(8,128)(2,1)}, u32[]{:S(2)}) copy-start(bf16[1,64,384]{2,1,0:T(8,128)(2,1)} %param.10) | copy-start | bytes 147460
  18.7 61.1 %all-to-all-start = ((bf16[32,64,1024]{2,1,0:T(8,128)(2,1)}), bf16[32,64,1024]{2,1,0:T(8,128)(2,1)}, u32[]{:S(2)}, u32[]{:S(2)}) async-start(bf16[32,64,1024]{2,1,0:T(8,128)(2,1)} %bitcast.51), calls=%async_computation | async-start | bytes 8388608 | tf_op jit(solution)/shard_map/all_to_all | solution.py:52
  26.3 81.3 %all-gather.3.cloned.1.call-start = ((), (), s32[]{:S(2)}) async-start(), calls=%async_computation.3 | async-start | bytes 2506752 | tf_op jit(solution)/shard_map/all_gather | solution.py:38
  27.1 180.5 %reduce-scatter.4.cloned.1.call-start = ((), (), s32[]{:S(2)}) async-start(), calls=%async_computation.4 | async-start | bytes 2506752
  107.7 3.4 %copy-start.1 = (bf16[32,32,1024]{2,1,0:T(8,128)(2,1)S(1)}, bf16[32,32,1024]{2,1,0:T(8,128)(2,1)}, u32[]{:S(2)}) copy-start(bf16[32,32,1024]{2,1,0:T(8,128)(2,1)} %get-tuple-element.33) | copy-start | bytes 6291460
  113.9 1.0 copy-start.8
  113.9 1.1 copy-start.10
  114.0 1.4 copy-start.11
  119.9 1.7 copy-start.7
  121.6 3.3 %copy-start.9 = (bf16[1024,384]{0,1:T(8,128)(2,1)S(1)}, bf16[1024,384]{0,1:T(8,128)(2,1)}, u32[]{:S(2)}) copy-start(bf16[1024,384]{0,1:T(8,128)(2,1)} %copy-done.8) | copy-start | bytes 2359300
  128.9 7.7 %copy-start.2 = (bf16[128,1024]{1,0:T(8,128)(2,1)S(1)}, bf16[128,1024]{1,0:T(8,128)(2,1)}, u32[]{:S(2)}) copy-start(bf16[128,1024]{1,0:T(8,128)(2,1)} %param.13) | copy-start | bytes 786436
  128.9 8.5 %copy-start.6 = (s32[128,2]{0,1:T(2,128)S(1)}, s32[128,2]{0,1:T(2,128)}, u32[]{:S(2)}) copy-start(s32[128,2]{0,1:T(2,128)} %param.8) | copy-start | bytes 3076
  128.9 60.9 %all-to-all-start.1 = ((bf16[32,64,1024]{2,1,0:T(8,128)(2,1)}), bf16[32,64,1024]{2,1,0:T(8,128)(2,1)}, u32[]{:S(2)}, u32[]{:S(2)}) async-start(bf16[32,64,1024]{2,1,0:T(8,128)(2,1)} %pad_maximum_fusion), calls=%async_computation.1 | async-start | bytes 8388608 | tf_op jit(solution)/shard_map/all_to_all | solution.py:93
Sparse Core Ops, SparseCore 0:
  29.8 77.7 all-gather.2
  120.1 69.9 reduce-scatter.3

commit v3 on v2

--- a/solution.py
+++ b/solution.py
@@ -32,7 +32,6 @@
     capacity = min(tok_rows, 4 * tok_rows * top_count // senders)
     total_rows = senders * capacity
     flat_ids, slot_of = route_slots(expert_ids, senders)
-    token_of = jnp.arange(tok_rows * top_count, dtype=jnp.int32) // top_count
 
     packed = jnp.concatenate([w_gate[0], w_up[0], w_down[0].T], axis=1)
     whole = lax.all_gather(packed[None], "dp", axis=1, tiled=True)[0]
@@ -46,9 +45,13 @@
         .reshape(tok_rows * top_count, model_width)
     )
     base = flat_ids * (2 * capacity) + slot_of
-    places = jnp.concatenate([base, base + capacity])
-    values = jnp.concatenate([tokens[token_of], scaled], axis=0)
-    outgoing = jnp.zeros((2 * total_rows, model_width), jnp.bfloat16).at[places].set(values)
+    slots = jnp.arange(2 * total_rows, dtype=jnp.int32)[:, None]
+    pairs = base.reshape(tok_rows, top_count)
+    pick_tok = (slots == pairs[None, :, 0]) | (slots == pairs[None, :, 1])
+    pick_grad = slots == (base + capacity)[None, :]
+    chooser = jnp.concatenate([pick_tok, pick_grad], axis=1).astype(jnp.bfloat16)
+    sources = jnp.concatenate([tokens, scaled], axis=0)
+    outgoing = jnp.dot(chooser, sources, preferred_element_type=jnp.float32).astype(jnp.bfloat16)
     arrived = lax.all_to_all(
         outgoing.reshape(senders, 2 * capacity, model_width),
         "expert",
@@ -91,21 +94,15 @@
         axis=1,
     )
     back_home = lax.all_to_all(leaving, "expert", split_axis=0, concat_axis=0, tiled=True)
-    returned = back_home[:, :capacity]
-    sent_back = back_home[:, capacity:]
 
-    slot_place = flat_ids * capacity + slot_of
-    picked = (
-        returned.reshape(total_rows, model_width)[slot_place]
-        .reshape(tok_rows, top_count, model_width)
-        .astype(jnp.float32)
-    )
-    mixed_out = jnp.sum(route_probs[:, :, None] * picked, axis=1).astype(jnp.bfloat16)
-    grad_probs = jnp.sum(grad_wide[:, None, :] * picked, axis=2)
-    back_picked = sent_back.reshape(total_rows, model_width)[slot_place].reshape(
-        tok_rows, top_count, model_width
-    )
-    grad_tokens = jnp.sum(back_picked.astype(jnp.float32), axis=1).astype(jnp.bfloat16)
+    home_flat = back_home.reshape(2 * total_rows, model_width)
+    own_place = base.reshape(tok_rows, top_count).T.reshape(-1)
+    picked = home_flat[own_place].reshape(top_count, tok_rows, model_width).astype(jnp.float32)
+    back_picked = home_flat[own_place + capacity].reshape(top_count, tok_rows, model_width)
+    probs_k = route_probs.T[:, :, None]
+    mixed_out = jnp.sum(probs_k * picked, axis=0).astype(jnp.bfloat16)
+    grad_probs = jnp.sum(grad_wide[None] * picked, axis=2).T
+    grad_tokens = jnp.sum(back_picked.astype(jnp.float32), axis=0).astype(jnp.bfloat16)
 
     summed = summed.astype(jnp.float32).astype(jnp.bfloat16)
     grad_w_gate = summed[:, :hidden_width][None]

time: 218 us -> 209 us (0.959)
  other arithmetic: 16.3 us -> 7.6 us
  local copies, waits for them, and re-layouts: 29.9 us -> 24.2 us
  matrix products: 13.6 us -> 18 us
    scatter x1 -> x0, other arithmetic: 5.25 us -> none  [shards(): jnp.zeros((2 * total_rows, model_width), jnp.bfloat16).at[places]]
    dot_general x0 -> x1, matrix products: none -> 4.33 us  [shards(): jnp.dot(chooser, sources, preferred_element_type=jnp.float32)]
    slice x2 -> x1, local copies, waits for them, and re-layouts: 4.38 us -> 0.18 us  [the longest x1 4.2 us: shards(): sent_back = back_home[:, capacity:]]
    reduce_sum x2, other arithmetic: 5.7 us -> 1.85 us  [the longest x1 1.01 us: shards(): grad_probs = jnp.sum(grad_wide[None] * picked, axis=2).T]
    gather x3 -> x2, local copies, waits for them, and re-layouts: 6.55 us -> 8.57 us  [the longest x1 4.29 us: shards(): home_flat[own_place].reshape(top_count, tok_rows, model_width)]
    unnamed x34 -> x29, local copies, waits for them, and re-layouts: 9.36 us -> 7.79 us
  transfers between devices with their start and end apart: 4 -> 4, of which waited for: 3 -> 3; matrix products, arithmetic and copies ran while one was open for 14% -> 11% of each run, Pallas kernels for 0% -> 0%
where the time goes in v3:
time: 209 us
  waiting for transfers between devices  129 us (62%)
  local copies, waits for them, and re-layouts  24.2 us (12%)
  matrix products  18 us (9%)
  starting transfers between devices  15.5 us (7%)
  between operations  14.3 us (7%)
  other arithmetic  7.6 us (4%)
    all_to_all x1, waiting for transfers between devices, shards(): lax.all_to_all(leaving, 'expert', split_axis=0, concat_axis=0, tiled=True)  53.2 us
    all_to_all x1, waiting for transfers between devices, shards(): lax.all_to_all(outgoing.reshape(senders, 2 * capacity, model_width), 'exp...  52.5 us
    all_gather x1, waiting for transfers between devices, shards(): whole = lax.all_gather(packed[None], 'dp', axis=1, tiled=True)[0]  23.6 us
    unnamed x29, local copies, waits for them, and re-layouts  7.79 us
    all_to_all x1, starting transfers between devices, shards(): lax.all_to_all(leaving, 'expert', split_axis=0, concat_axis=0, tiled=True)  7.66 us
    all_to_all x1, starting transfers between devices, shards(): lax.all_to_all(outgoing.reshape(senders, 2 * capacity, model_width), 'exp...  7.58 us
    dot_general x2, matrix products, contract_cols(): lax.dot_general(left_op, right_op, (((1,), (1,)), ((), ())), preferred_el...  4.53 us
    dot_general x1, matrix products, shards(): jnp.dot(chooser, sources, preferred_element_type=jnp.float32)  4.33 us
  transfers between devices with their start and end apart: 4, of which 3 were waited for; matrix products, arithmetic and copies ran while one was open for 11% of the time, Pallas kernels for 0%

profile of v3, /device:TPU:32, one launch (start us, length us, event | category | flops | bytes accessed | tf_op | source)
XLA Modules:
  0.0 208.9 jit_solution(11753814388352524966)
XLA Ops:
  7.2 0.8 copy.45
  8.0 0.1 eq.73
  8.1 0.1 eq.69
  8.2 0.0 copy-start.5
  8.3 0.6 reduce-window.6
  8.9 0.2 slice_reduce_fusion
  9.1 0.1 fusion.18
  9.2 0.1 reduce_sum.42
  9.3 0.1 copy.48
  9.4 0.7 multiply_add_fusion
  10.1 0.3 iota_compare_fusion
  10.5 1.2 mul.85
  11.7 0.0 copy-start.7
  11.7 0.7 mul.86
  12.4 0.0 copy-done.5
  12.4 0.1 copy.49
  12.6 0.1 mul.83
  12.7 0.2 fusion.9
  12.9 0.1 multiply_convert_fusion.3
  13.0 0.0 copy-done.7
  13.1 4.3 %convolution_convert_fusion = bf16[2048,1024]{1,0:T(8,128)(2,1)} fusion(pred[2048,256]{1,0:T(32,128)(4,1)S(1)} %iota_compare_fusion, pred[2048,128]{1,0:T(32,128)(4,1)S(1)} %fusion.9, bf16[256,1024]{1,0:T(8,128)(2,1)S(1)} %multiply_convert_fusion.3, bf16[128,1024]{1,0:T(8,128)(2,1)S(1)} %copy-done.7), kind=kOutput, calls=%fused_computation.3 | convolution fusion | flops 1615069184 | bytes 5767168 | tf_op jit(solution)/shard_map/dot_general | solution.py:54
  17.4 0.0 copy-start.2
  17.4 0.0 copy-start.3
  17.4 7.6 %all-to-all-start = ((bf16[32,64,1024]{2,1,0:T(8,128)(2,1)}), bf16[32,64,1024]{2,1,0:T(8,128)(2,1)}, u32[]{:S(2)}, u32[]{:S(2)}) async-start(bf16[32,64,1024]{2,1,0:T(8,128)(2,1)} %bitcast.56), calls=%async_computation | async-start | bytes 8388608 | tf_op jit(solution)/shard_map/all_to_all | solution.py:55
  25.0 0.0 all-gather.3.cloned.1.call-start
  25.0 0.0 copy-done.2
  25.0 0.0 copy-done.3
  25.0 0.0 copy-done.4
  25.1 0.7 pad_maximum_fusion.5
  25.7 0.0 all-gather.3.cloned.1.call-update
  25.8 0.2 reduce-scatter.4.cloned.1.call-start
  26.0 52.5 %all-to-all-done = bf16[32,64,1024]{2,1,0:T(8,128)(2,1)} async-done(((bf16[32,64,1024]{2,1,0:T(8,128)(2,1)}), bf16[32,64,1024]{2,1,0:T(8,128)(2,1)}, u32[]{:S(2)}, u32[]{:S(2)}) %all-to-all-start) | async-done | bytes 4194336 | tf_op jit(solution)/shard_map/all_to_all | solution.py:55
  78.5 4.2 %fusion.24 = (bf16[32,32,1024]{2,1,0:T(8,128)(2,1)S(1)}, bf16[32,32,1024]{2,1,0:T(8,128)(2,1)}) fusion(bf16[32,64,1024]{2,1,0:T(8,128)(2,1)} %all-to-all-done), kind=kLoop, calls=%fused_computation.58 | loop fusion | bytes 8388608 | tf_op jit(solution)/shard_map/slice | solution.py:62
  82.7 23.6 %all-gather.3.cloned.1.call-done = bf16[1024,1152]{1,0:T(8,128)(2,1)} async-done(((bf16[64,1152]{1,0:T(8,128)(2,1)}), bf16[1024,1152]{1,0:T(8,128)(2,1)}) %all-gather.3.cloned.1.call-update) | async-done | bytes 2359312 | tf_op jit(solution)/shard_map/all_gather | solution.py:37
  106.3 3.5 %fusion.5 = f32[1024,768]{0,1:T(8,128)S(1)} fusion(bf16[1024,1024]{1,0:T(8,128)(2,1)S(1)} %bitcast.59, bf16[1024,1152]{1,0:T(8,128)(2,1)} %all-gather.3.cloned.1.call-done), kind=kOutput, calls=%fused_computation.20 | convolution fusion | flops 1610612736 | bytes 6815744 | tf_op jit(solution)/shard_map/dot_general | solution.py:65
  109.8 0.0 copy-done
  109.8 2.8 %multiply_convert_fusion.1 = (bf16[1024,384]{0,1:T(8,128)(2,1)S(1)}, bf16[1024,384]{0,1:T(8,128)(2,1)S(1)}, bf16[1024,384]{0,1:T(8,128)(2,1)S(1)}) fusion(f32[1024,768]{0,1:T(8,128)S(1)} %fusion.5, bf16[1024,1024]{1,0:T(8,128)(2,1)S(1)} %bitcast.61, bf16[1024,1152]{1,0:T(8,128)(2,1)} %all-gather.3.cloned.1.call-done), kind=kOutput, calls=%fused_computation.14 | convolution fusion | flops 811204608 | bytes 8388608 | tf_op jit(solution)/shard_map/dot_general | solution.py:71
  112.6 0.0 copy-start.8
  112.6 0.0 copy-start.9
  112.6 1.0 convolution_convert_fusion.4
  113.6 0.0 copy-done.8
  113.7 0.1 copy-done.9
  113.8 1.8 convolution_convert_fusion.3
  115.6 0.2 pad_maximum_fusion.1
  115.8 2.6 %copy.53 = bf16[1024,1152]{1,0:T(8,128)(2,1)} copy(bf16[1024,1152]{0,1:T(8,128)(2,1)S(1)} %pad_maximum_fusion.1) | data formatting | bytes 4718592
  118.4 0.0 reduce-scatter.4.cloned.1.call-update
  118.4 1.6 copy-done.6
  120.1 3.2 %convolution_convert_fusion.2 = bf16[1024,1024]{1,0:T(8,128)(2,1)S(1)} fusion(bf16[1024,1152]{1,0:T(8,128)(2,1)S(1)} %copy-done.6, bf16[1024,384]{0,1:T(8,128)(2,1)} %copy-done.9, bf16[1024,384]{0,1:T(8,128)(2,1)} %copy-done.8), kind=kOutput, calls=%fused_computation.10 | convolution fusion | flops 1614807040 | bytes 5242880 | tf_op jit(solution)/shard_map/dot_general | solution.py:22
  123.3 1.3 convolution_convert_fusion.1
  124.6 2.7 %pad_maximum_fusion = bf16[32,64,1024]{2,1,0:T(8,128)(2,1)} fusion(bf16[32,32,1024]{2,1,0:T(8,128)(2,1)S(1)} %bitcast.63, bf16[32,32,1024]{2,1,0:T(8,128)(2,1)S(1)} %bitcast.64), kind=kLoop, calls=%fused_computation.2 | loop fusion | flops 8388608 | bytes 8388608 | tf_op jit(solution)/shard_map/concatenate | solution.py:89
  127.3 7.7 %all-to-all-start.1 = ((bf16[32,64,1024]{2,1,0:T(8,128)(2,1)}), bf16[32,64,1024]{2,1,0:T(8,128)(2,1)}, u32[]{:S(2)}, u32[]{:S(2)}) async-start(bf16[32,64,1024]{2,1,0:T(8,128)(2,1)} %pad_maximum_fusion), calls=%async_computation.1 | async-start | bytes 8388608 | tf_op jit(solution)/shard_map/all_to_all | solution.py:96
  135.0 0.0 copy-done.1
  135.1 53.2 %all-to-all-done.1 = bf16[32,64,1024]{2,1,0:T(8,128)(2,1)} async-done(((bf16[32,64,1024]{2,1,0:T(8,128)(2,1)}), bf16[32,64,1024]{2,1,0:T(8,128)(2,1)}, u32[]{:S(2)}, u32[]{:S(2)}) %all-to-all-start.1) | async-done | bytes 4194336 | tf_op jit(solution)/shard_map/all_to_all | solution.py:96
  188.2 4.3 %gather_fusion = bf16[256,1024]{1,0:T(8,128)(2,1)S(1)} fusion(bf16[2048,1024]{1,0:T(8,128)(2,1)} %bitcast.13, s32[1024]{0:T(1024)S(1)} %pad_clamp_fusion.1), kind=kCustom, calls=%fused_computation | custom fusion | bytes 1049600 | tf_op jit(solution)/shard_map/gather | solution.py:100
  192.5 4.3 %gather_fusion.1 = bf16[256,1024]{1,0:T(8,128)(2,1)S(1)} fusion(bf16[2048,1024]{1,0:T(8,128)(2,1)} %bitcast.13, s32[1024]{0:T(1024)S(1)} %pad_clamp_fusion), kind=kCustom, calls=%fused_computation.1 | custom fusion | bytes 1049600 | tf_op jit(solution)/shard_map/gather | solution.py:101
  196.8 0.8 reduce_sum.44
  197.7 1.0 fusion.8
  198.7 0.9 fusion.25
  199.5 0.1 copy.55
  199.6 0.7 copy.50
  200.4 0.1 copy.56
  200.5 0.7 copy.51
  201.2 0.1 copy.57
  201.3 0.7 copy.52
  (14 shorter events, 0.1 us)
Async XLA Ops:
  8.2 4.2 %copy-start.5 = (f32[128,2]{0,1:T(2,128)S(1)}, f32[128,2]{0,1:T(2,128)}, u32[]{:S(2)}) copy-start(f32[128,2]{0,1:T(2,128)} %param.9) | copy-start | bytes 3076
  11.7 1.4 copy-start.7
  17.4 7.6 %copy-start.2 = (bf16[1,384,64]{1,2,0:T(8,128)(2,1)S(1)}, bf16[1,384,64]{1,2,0:T(8,128)(2,1)}, u32[]{:S(2)}) copy-start(bf16[1,384,64]{1,2,0:T(8,128)(2,1)} %param.12) | copy-start | bytes 147460
  17.4 7.7 %copy-start.3 = (bf16[1,64,384]{2,1,0:T(8,128)(2,1)S(1)}, bf16[1,64,384]{2,1,0:T(8,128)(2,1)}, u32[]{:S(2)}) copy-start(bf16[1,64,384]{2,1,0:T(8,128)(2,1)} %param.11) | copy-start | bytes 147460
  17.4 7.7 %copy-start.4 = (bf16[1,64,384]{2,1,0:T(8,128)(2,1)S(1)}, bf16[1,64,384]{2,1,0:T(8,128)(2,1)}, u32[]{:S(2)}) copy-start(bf16[1,64,384]{2,1,0:T(8,128)(2,1)} %param.10) | copy-start | bytes 147460
  17.4 61.1 %all-to-all-start = ((bf16[32,64,1024]{2,1,0:T(8,128)(2,1)}), bf16[32,64,1024]{2,1,0:T(8,128)(2,1)}, u32[]{:S(2)}, u32[]{:S(2)}) async-start(bf16[32,64,1024]{2,1,0:T(8,128)(2,1)} %bitcast.56), calls=%async_computation | async-start | bytes 8388608 | tf_op jit(solution)/shard_map/all_to_all | solution.py:55
  25.0 81.3 %all-gather.3.cloned.1.call-start = ((), (), s32[]{:S(2)}) async-start(), calls=%async_computation.3 | async-start | bytes 2506752 | tf_op jit(solution)/shard_map/all_gather | solution.py:37
  25.8 172.9 %reduce-scatter.4.cloned.1.call-start = ((), (), s32[]{:S(2)}) async-start(), calls=%async_computation.4 | async-start | bytes 2506752
  106.3 3.5 %copy-start = (bf16[32,32,1024]{2,1,0:T(8,128)(2,1)S(1)}, bf16[32,32,1024]{2,1,0:T(8,128)(2,1)}, u32[]{:S(2)}) copy-start(bf16[32,32,1024]{2,1,0:T(8,128)(2,1)} %get-tuple-element.41) | copy-start | bytes 6291460
  112.6 1.0 copy-start.8
  112.6 1.1 copy-start.9
  118.4 1.7 copy-start.6
  127.3 7.7 %copy-start.1 = (bf16[128,1024]{1,0:T(8,128)(2,1)S(1)}, bf16[128,1024]{1,0:T(8,128)(2,1)}, u32[]{:S(2)}) copy-start(bf16[128,1024]{1,0:T(8,128)(2,1)} %param.13) | copy-start | bytes 786436
  127.3 60.9 %all-to-all-start.1 = ((bf16[32,64,1024]{2,1,0:T(8,128)(2,1)}), bf16[32,64,1024]{2,1,0:T(8,128)(2,1)}, u32[]{:S(2)}, u32[]{:S(2)}) async-start(bf16[32,64,1024]{2,1,0:T(8,128)(2,1)} %pad_maximum_fusion), calls=%async_computation.1 | async-start | bytes 8388608 | tf_op jit(solution)/shard_map/all_to_all | solution.py:96
Sparse Core Ops, SparseCore 0:
  28.5 77.7 all-gather.2
  118.5 69.9 reduce-scatter.3

commit v4 on v3

--- a/solution.py
+++ b/solution.py
@@ -97,14 +97,18 @@
 
     home_flat = back_home.reshape(2 * total_rows, model_width)
     own_place = base.reshape(tok_rows, top_count).T.reshape(-1)
-    picked = home_flat[own_place].reshape(top_count, tok_rows, model_width).astype(jnp.float32)
-    back_picked = home_flat[own_place + capacity].reshape(top_count, tok_rows, model_width)
+    wanted = jnp.concatenate([own_place, own_place + capacity])
+    taker = (jnp.arange(2 * total_rows, dtype=jnp.int32)[None, :] == wanted[:, None]).astype(
+        jnp.bfloat16
+    )
+    taken = jnp.dot(taker, home_flat, preferred_element_type=jnp.float32)
+    picked = taken[: tok_rows * top_count].reshape(top_count, tok_rows, model_width)
+    back_picked = taken[tok_rows * top_count :].reshape(top_count, tok_rows, model_width)
     probs_k = route_probs.T[:, :, None]
     mixed_out = jnp.sum(probs_k * picked, axis=0).astype(jnp.bfloat16)
     grad_probs = jnp.sum(grad_wide[None] * picked, axis=2).T
     grad_tokens = jnp.sum(back_picked.astype(jnp.float32), axis=0).astype(jnp.bfloat16)
 
-    summed = summed.astype(jnp.float32).astype(jnp.bfloat16)
     grad_w_gate = summed[:, :hidden_width][None]
     grad_w_up = summed[:, hidden_width : 2 * hidden_width][None]
     grad_w_down = summed[:, 2 * hidden_width :].T[None]

time: 209 us -> 215 us (1.029)
  the two profiles are of different devices: /device:TPU:32 before, /device:TPU:10 now
where the time goes in v4:
time: 215 us
  waiting for transfers between devices  137 us (64%)
  matrix products  21.1 us (10%)
  starting transfers between devices  18.4 us (9%)
  local copies, waits for them, and re-layouts  14.8 us (7%)
  between operations  14.3 us (7%)
  other arithmetic  9.56 us (4%)
    all_to_all x1, waiting for transfers between devices, shards(): lax.all_to_all(outgoing.reshape(senders, 2 * capacity, model_width), 'exp...  48.8 us
    all_to_all x1, waiting for transfers between devices, shards(): lax.all_to_all(leaving, 'expert', split_axis=0, concat_axis=0, tiled=True)  44.3 us
    all_gather x1, waiting for transfers between devices, shards(): whole = lax.all_gather(packed[None], 'dp', axis=1, tiled=True)[0]  25.1 us
    unnamed x3, waiting for transfers between devices  18.6 us
    all_to_all x1, starting transfers between devices, shards(): lax.all_to_all(outgoing.reshape(senders, 2 * capacity, model_width), 'exp...  10.4 us
    all_to_all x1, starting transfers between devices, shards(): lax.all_to_all(leaving, 'expert', split_axis=0, concat_axis=0, tiled=True)  7.5 us
    unnamed x25, local copies, waits for them, and re-layouts  6.93 us
    dot_general x1, matrix products, shards(): taken = jnp.dot(taker, home_flat, preferred_element_type=jnp.float32)  4.56 us
  transfers between devices with their start and end apart: 4, of which 4 were waited for; matrix products, arithmetic and copies ran while one was open for 7% of the time, Pallas kernels for 0%

profile of v4, /device:TPU:10, one launch (start us, length us, event | category | flops | bytes accessed | tf_op | source)
XLA Modules:
  0.0 214.9 jit_solution(16219119264091501010)
XLA Ops:
  7.2 0.8 copy.45
  8.0 0.1 eq.86
  8.1 0.1 eq.82
  8.2 0.0 copy-start.5
  8.3 0.6 reduce-window.6
  8.9 0.2 slice_reduce_fusion
  9.1 0.1 fusion.19
  9.2 0.1 reduce_sum.41
  9.3 0.1 copy.48
  9.4 0.7 broadcast_add_fusion
  10.1 0.3 iota_compare_fusion.2
  10.5 1.2 mul.84
  11.7 0.0 copy-start.7
  11.7 0.7 mul.85
  12.4 0.0 copy-done.5
  12.4 0.1 copy.49
  12.6 0.1 mul.82
  12.7 0.2 fusion.10
  12.9 0.1 multiply_convert_fusion.3
  13.0 0.0 copy-done.7
  13.1 4.3 %convolution_convert_fusion = bf16[2048,1024]{1,0:T(8,128)(2,1)} fusion(pred[2048,256]{1,0:T(32,128)(4,1)S(1)} %iota_compare_fusion.2, pred[2048,128]{1,0:T(32,128)(4,1)S(1)} %fusion.10, bf16[256,1024]{1,0:T(8,128)(2,1)S(1)} %multiply_convert_fusion.3, bf16[128,1024]{1,0:T(8,128)(2,1)S(1)} %copy-done.7), kind=kOutput, calls=%fused_computation.3 | convolution fusion | flops 1615069184 | bytes 5767168 | tf_op jit(solution)/shard_map/dot_general | solution.py:54
  17.4 0.0 copy-start.2
  17.4 0.0 copy-start.3
  17.4 0.0 copy-start.4
  17.4 10.4 %all-to-all-start = ((bf16[32,64,1024]{2,1,0:T(8,128)(2,1)}), bf16[32,64,1024]{2,1,0:T(8,128)(2,1)}, u32[]{:S(2)}, u32[]{:S(2)}) async-start(bf16[32,64,1024]{2,1,0:T(8,128)(2,1)} %bitcast.63), calls=%async_computation | async-start | bytes 8388608 | tf_op jit(solution)/shard_map/all_to_all | solution.py:55
  27.8 0.2 all-gather.3.cloned.1.call-start
  28.0 0.0 copy-done.2
  28.0 0.0 copy-done.3
  28.1 0.0 copy-done.4
  28.1 0.7 pad_maximum_fusion.5
  28.7 0.0 all-gather.3.cloned.1.call-update
  28.8 48.8 %all-to-all-done = bf16[32,64,1024]{2,1,0:T(8,128)(2,1)} async-done(((bf16[32,64,1024]{2,1,0:T(8,128)(2,1)}), bf16[32,64,1024]{2,1,0:T(8,128)(2,1)}, u32[]{:S(2)}, u32[]{:S(2)}) %all-to-all-start) | async-done | bytes 4194336 | tf_op jit(solution)/shard_map/all_to_all | solution.py:55
  77.5 4.2 %fusion.25 = (bf16[32,32,1024]{2,1,0:T(8,128)(2,1)S(1)}, bf16[32,32,1024]{2,1,0:T(8,128)(2,1)}) fusion(bf16[32,64,1024]{2,1,0:T(8,128)(2,1)} %all-to-all-done), kind=kLoop, calls=%fused_computation.56 | loop fusion | bytes 8388608 | tf_op jit(solution)/shard_map/slice | solution.py:62
  81.8 25.1 %all-gather.3.cloned.1.call-done = bf16[1024,1152]{1,0:T(8,128)(2,1)} async-done(((bf16[64,1152]{1,0:T(8,128)(2,1)}), bf16[1024,1152]{1,0:T(8,128)(2,1)}) %all-gather.3.cloned.1.call-update) | async-done | bytes 2359312 | tf_op jit(solution)/shard_map/all_gather | solution.py:37
  106.8 0.0 copy-start
  106.8 0.0 copy-start.6
  106.8 3.4 %fusion.7 = f32[1024,768]{0,1:T(8,128)S(1)} fusion(bf16[1024,1024]{1,0:T(8,128)(2,1)S(1)} %bitcast.64, bf16[1024,1152]{1,0:T(8,128)(2,1)} %all-gather.3.cloned.1.call-done), kind=kOutput, calls=%fused_computation.21 | convolution fusion | flops 1610612736 | bytes 6815744 | tf_op jit(solution)/shard_map/dot_general | solution.py:65
  110.3 0.0 copy-done
  110.3 0.0 copy-done.6
  110.3 1.7 multiply_convert_fusion.1
  112.0 1.0 convolution_convert_fusion.4
  113.0 3.0 %convolution_convert_fusion.3 = bf16[1024,768]{0,1:T(8,128)(2,1)} fusion(bf16[1024,1024]{1,0:T(8,128)(2,1)S(1)} %bitcast.65, bf16[1024,384]{0,1:T(8,128)(2,1)S(1)} %get-tuple-element.39, bf16[1024,384]{0,1:T(8,128)(2,1)S(1)} %get-tuple-element.38), kind=kOutput, calls=%fused_computation.12 | convolution fusion | flops 1614544896 | bytes 5242880 | tf_op jit(solution)/shard_map/dot_general | solution.py:16
  116.0 1.8 convolution_convert_fusion.2
  117.9 1.3 convolution_convert_fusion.1
  119.2 2.7 %pad_maximum_fusion = bf16[32,64,1024]{2,1,0:T(8,128)(2,1)} fusion(bf16[32,32,1024]{2,1,0:T(8,128)(2,1)S(1)} %bitcast.68, bf16[32,32,1024]{2,1,0:T(8,128)(2,1)S(1)} %bitcast.69), kind=kLoop, calls=%fused_computation | loop fusion | flops 8388608 | bytes 8388608 | tf_op jit(solution)/shard_map/concatenate | solution.py:89
  121.8 7.5 %all-to-all-start.1 = ((bf16[32,64,1024]{2,1,0:T(8,128)(2,1)}), bf16[32,64,1024]{2,1,0:T(8,128)(2,1)}, u32[]{:S(2)}, u32[]{:S(2)}) async-start(bf16[32,64,1024]{2,1,0:T(8,128)(2,1)} %pad_maximum_fusion), calls=%async_computation.1 | async-start | bytes 8388608 | tf_op jit(solution)/shard_map/all_to_all | solution.py:96
  129.4 0.3 reduce-scatter.4.cloned.1.call-start
  129.6 1.6 pad_maximum_fusion.1
  131.2 2.5 %copy.53 = bf16[1024,1152]{1,0:T(8,128)(2,1)} copy(bf16[1024,1152]{0,1:T(8,128)(2,1)S(1)} %pad_maximum_fusion.1) | data formatting | bytes 4718592
  133.8 0.0 reduce-scatter.4.cloned.1.call-update
  133.8 0.9 copy-done.1
  134.8 44.3 %all-to-all-done.1 = bf16[32,64,1024]{2,1,0:T(8,128)(2,1)} async-done(((bf16[32,64,1024]{2,1,0:T(8,128)(2,1)}), bf16[32,64,1024]{2,1,0:T(8,128)(2,1)}, u32[]{:S(2)}, u32[]{:S(2)}) %all-to-all-start.1) | async-done | bytes 4194336 | tf_op jit(solution)/shard_map/all_to_all | solution.py:96
  179.1 4.6 %fusion = f32[512,1024]{1,0:T(8,128)S(1)} fusion(bf16[2048,1024]{1,0:T(8,128)(2,1)} %bitcast.16, s32[512]{0:T(512)S(1)} %pad_add_fusion), kind=kOutput, calls=%fused_computation.2 | convolution fusion | flops 2148532224 | bytes 6293504 | tf_op jit(solution)/shard_map/dot_general | solution.py:104
  183.7 0.8 fusion.9
  184.4 0.8 reduce_sum.43
  185.3 0.8 multiply_reduce_fusion
  186.1 18.6 %reduce-scatter.4.cloned.1.call-done = bf16[64,1152]{1,0:T(8,128)(2,1)} async-done(((bf16[1024,1152]{1,0:T(8,128)(2,1)}), bf16[64,1152]{1,0:T(8,128)(2,1)}) %reduce-scatter.4.cloned.1.call-update) | async-done | bytes 147472
  204.7 0.9 fusion.26
  205.5 0.1 copy.55
  205.7 0.7 copy.50
  206.4 0.1 copy.56
  206.5 0.7 copy.51
  207.2 0.1 copy.57
  207.4 0.7 copy.52
  (8 shorter events, 0.1 us)
Async XLA Ops:
  8.2 4.2 %copy-start.5 = (f32[128,2]{0,1:T(2,128)S(1)}, f32[128,2]{0,1:T(2,128)}, u32[]{:S(2)}) copy-start(f32[128,2]{0,1:T(2,128)} %param.9) | copy-start | bytes 3076
  11.7 1.4 copy-start.7
  17.4 10.7 %copy-start.2 = (bf16[1,384,64]{1,2,0:T(8,128)(2,1)S(1)}, bf16[1,384,64]{1,2,0:T(8,128)(2,1)}, u32[]{:S(2)}) copy-start(bf16[1,384,64]{1,2,0:T(8,128)(2,1)} %param.12) | copy-start | bytes 147460
  17.4 10.7 %copy-start.3 = (bf16[1,64,384]{2,1,0:T(8,128)(2,1)S(1)}, bf16[1,64,384]{2,1,0:T(8,128)(2,1)}, u32[]{:S(2)}) copy-start(bf16[1,64,384]{2,1,0:T(8,128)(2,1)} %param.11) | copy-start | bytes 147460
  17.4 10.7 %copy-start.4 = (bf16[1,64,384]{2,1,0:T(8,128)(2,1)S(1)}, bf16[1,64,384]{2,1,0:T(8,128)(2,1)}, u32[]{:S(2)}) copy-start(bf16[1,64,384]{2,1,0:T(8,128)(2,1)} %param.10) | copy-start | bytes 147460
  17.4 60.2 %all-to-all-start = ((bf16[32,64,1024]{2,1,0:T(8,128)(2,1)}), bf16[32,64,1024]{2,1,0:T(8,128)(2,1)}, u32[]{:S(2)}, u32[]{:S(2)}) async-start(bf16[32,64,1024]{2,1,0:T(8,128)(2,1)} %bitcast.63), calls=%async_computation | async-start | bytes 8388608 | tf_op jit(solution)/shard_map/all_to_all | solution.py:55
  27.8 79.0 %all-gather.3.cloned.1.call-start = ((), (), s32[]{:S(2)}) async-start(), calls=%async_computation.3 | async-start | bytes 2506752 | tf_op jit(solution)/shard_map/all_gather | solution.py:37
  106.8 3.4 %copy-start = (bf16[32,32,1024]{2,1,0:T(8,128)(2,1)S(1)}, bf16[32,32,1024]{2,1,0:T(8,128)(2,1)}, u32[]{:S(2)}) copy-start(bf16[32,32,1024]{2,1,0:T(8,128)(2,1)} %get-tuple-element.41) | copy-start | bytes 6291460
  106.8 3.5 %copy-start.6 = (bf16[1024,1152]{1,0:T(8,128)(2,1)S(1)}, bf16[1024,1152]{1,0:T(8,128)(2,1)}, u32[]{:S(2)}) copy-start(bf16[1024,1152]{1,0:T(8,128)(2,1)} %all-gather.3.cloned.1.call-done) | copy-start | bytes 7077892
  121.8 57.3 %all-to-all-start.1 = ((bf16[32,64,1024]{2,1,0:T(8,128)(2,1)}), bf16[32,64,1024]{2,1,0:T(8,128)(2,1)}, u32[]{:S(2)}, u32[]{:S(2)}) async-start(bf16[32,64,1024]{2,1,0:T(8,128)(2,1)} %pad_maximum_fusion), calls=%async_computation.1 | async-start | bytes 8388608 | tf_op jit(solution)/shard_map/all_to_all | solution.py:96
  129.4 75.3 %reduce-scatter.4.cloned.1.call-start = ((), (), s32[]{:S(2)}) async-start(), calls=%async_computation.4 | async-start | bytes 2506752
  133.8 0.9 copy-start.1
Sparse Core Ops, SparseCore 0:
  31.3 75.4 all-gather.2
  133.9 70.7 reduce-scatter.3

commit v5 on v4

--- a/solution.py
+++ b/solution.py
@@ -95,6 +95,7 @@
     )
     back_home = lax.all_to_all(leaving, "expert", split_axis=0, concat_axis=0, tiled=True)
 
+    back_home, summed = lax.optimization_barrier((back_home, summed))
     home_flat = back_home.reshape(2 * total_rows, model_width)
     own_place = base.reshape(tok_rows, top_count).T.reshape(-1)
     wanted = jnp.concatenate([own_place, own_place + capacity])

time: 215 us -> 207 us (0.963)
  the two profiles are of different devices: /device:TPU:10 before, /device:TPU:2 now
where the time goes in v5:
time: 207 us
  waiting for transfers between devices  129 us (62%)
  matrix products  21.1 us (10%)
  starting transfers between devices  18.2 us (9%)
  local copies, waits for them, and re-layouts  15.5 us (7%)
  between operations  14.3 us (7%)
  other arithmetic  8.13 us (4%)
    unnamed x3, waiting for transfers between devices  55.2 us
    all_to_all x1, waiting for transfers between devices, shards(): lax.all_to_all(outgoing.reshape(senders, 2 * capacity, model_width), 'exp...  50.5 us
    all_gather x1, waiting for transfers between devices, shards(): whole = lax.all_gather(packed[None], 'dp', axis=1, tiled=True)[0]  23.6 us
    all_to_all x1, starting transfers between devices, shards(): lax.all_to_all(outgoing.reshape(senders, 2 * capacity, model_width), 'exp...  10.5 us
    all_to_all x1, starting transfers between devices, shards(): lax.all_to_all(leaving, 'expert', split_axis=0, concat_axis=0, tiled=True)  7.48 us
    unnamed x30, local copies, waits for them, and re-layouts  7.44 us
    dot_general x1, matrix products, shards(): taken = jnp.dot(taker, home_flat, preferred_element_type=jnp.float32)  4.55 us
    dot_general x1, matrix products, shards(): jnp.dot(chooser, sources, preferred_element_type=jnp.float32)  4.31 us
  transfers between devices with their start and end apart: 4, of which 3 were waited for; matrix products, arithmetic and copies ran while one was open for 6% of the time, Pallas kernels for 0%

profile of v5, /device:TPU:2, one launch (start us, length us, event | category | flops | bytes accessed | tf_op | source)
XLA Modules:
  0.0 206.6 jit_solution(14948336016779176038)
XLA Ops:
  7.2 0.8 copy.45
  8.0 0.1 eq.86
  8.1 0.1 eq.82
  8.2 0.0 copy-start.5
  8.3 0.6 reduce-window.6
  8.9 0.2 slice_reduce_fusion
  9.1 0.1 fusion.19
  9.2 0.1 reduce_sum.41
  9.3 0.1 copy.48
  9.4 0.7 broadcast_add_fusion
  10.1 0.3 iota_compare_fusion.2
  10.5 1.2 mul.84
  11.7 0.0 copy-start.7
  11.7 0.7 mul.85
  12.4 0.0 copy-done.5
  12.4 0.1 copy.49
  12.6 0.1 mul.82
  12.7 0.2 fusion.10
  12.9 0.1 multiply_convert_fusion.3
  13.0 0.0 copy-done.7
  13.1 4.3 %convolution_convert_fusion = bf16[2048,1024]{1,0:T(8,128)(2,1)} fusion(pred[2048,256]{1,0:T(32,128)(4,1)S(1)} %iota_compare_fusion.2, pred[2048,128]{1,0:T(32,128)(4,1)S(1)} %fusion.10, bf16[256,1024]{1,0:T(8,128)(2,1)S(1)} %multiply_convert_fusion.3, bf16[128,1024]{1,0:T(8,128)(2,1)S(1)} %copy-done.7), kind=kOutput, calls=%fused_computation.3 | convolution fusion | flops 1615069184 | bytes 5767168 | tf_op jit(solution)/shard_map/dot_general | solution.py:54
  17.4 0.0 copy-start.2
  17.4 0.0 copy-start.3
  17.4 10.5 %all-to-all-start = ((bf16[32,64,1024]{2,1,0:T(8,128)(2,1)}), bf16[32,64,1024]{2,1,0:T(8,128)(2,1)}, u32[]{:S(2)}, u32[]{:S(2)}) async-start(bf16[32,64,1024]{2,1,0:T(8,128)(2,1)} %bitcast.66), calls=%async_computation | async-start | bytes 8388608 | tf_op jit(solution)/shard_map/all_to_all | solution.py:55
  27.9 0.0 all-gather.3.cloned.1.call-start
  27.9 0.0 copy-done.2
  27.9 0.0 copy-done.3
  27.9 0.0 copy-done.4
  28.0 0.7 pad_maximum_fusion.5
  28.6 0.0 all-gather.3.cloned.1.call-update
  28.7 0.2 reduce-scatter.4.cloned.1.call-start
  28.9 50.5 %all-to-all-done = bf16[32,64,1024]{2,1,0:T(8,128)(2,1)} async-done(((bf16[32,64,1024]{2,1,0:T(8,128)(2,1)}), bf16[32,64,1024]{2,1,0:T(8,128)(2,1)}, u32[]{:S(2)}, u32[]{:S(2)}) %all-to-all-start) | async-done | bytes 4194336 | tf_op jit(solution)/shard_map/all_to_all | solution.py:55
  79.3 4.2 %fusion.25 = (bf16[32,32,1024]{2,1,0:T(8,128)(2,1)S(1)}, bf16[32,32,1024]{2,1,0:T(8,128)(2,1)}) fusion(bf16[32,64,1024]{2,1,0:T(8,128)(2,1)} %all-to-all-done), kind=kLoop, calls=%fused_computation.59 | loop fusion | bytes 8388608 | tf_op jit(solution)/shard_map/slice | solution.py:62
  83.5 23.6 %all-gather.3.cloned.1.call-done = bf16[1024,1152]{1,0:T(8,128)(2,1)} async-done(((bf16[64,1152]{1,0:T(8,128)(2,1)}), bf16[1024,1152]{1,0:T(8,128)(2,1)}) %all-gather.3.cloned.1.call-update) | async-done | bytes 2359312 | tf_op jit(solution)/shard_map/all_gather | solution.py:37
  107.1 3.5 %fusion.7 = f32[1024,768]{0,1:T(8,128)S(1)} fusion(bf16[1024,1024]{1,0:T(8,128)(2,1)S(1)} %bitcast.67, bf16[1024,1152]{1,0:T(8,128)(2,1)} %all-gather.3.cloned.1.call-done), kind=kOutput, calls=%fused_computation.21 | convolution fusion | flops 1610612736 | bytes 6815744 | tf_op jit(solution)/shard_map/dot_general | solution.py:65
  110.6 0.0 copy-done
  110.6 2.8 %multiply_convert_fusion.1 = (bf16[1024,384]{0,1:T(8,128)(2,1)S(1)}, bf16[1024,384]{0,1:T(8,128)(2,1)S(1)}, bf16[1024,384]{0,1:T(8,128)(2,1)S(1)}) fusion(f32[1024,768]{0,1:T(8,128)S(1)} %fusion.7, bf16[1024,1024]{1,0:T(8,128)(2,1)S(1)} %bitcast.69, bf16[1024,1152]{1,0:T(8,128)(2,1)} %all-gather.3.cloned.1.call-done), kind=kOutput, calls=%fused_computation.15 | convolution fusion | flops 811204608 | bytes 8388608 | tf_op jit(solution)/shard_map/dot_general | solution.py:71
  113.4 0.0 copy-start.8
  113.4 0.0 copy-start.10
  113.4 1.0 convolution_convert_fusion.4
  114.4 0.0 copy-done.8
  114.4 0.1 copy-done.10
  114.6 1.8 convolution_convert_fusion.3
  116.4 0.2 pad_maximum_fusion.1
  116.6 2.6 %copy.53 = bf16[1024,1152]{1,0:T(8,128)(2,1)} copy(bf16[1024,1152]{0,1:T(8,128)(2,1)S(1)} %pad_maximum_fusion.1) | data formatting | bytes 4718592
  119.2 0.0 reduce-scatter.4.cloned.1.call-update
  119.2 1.6 copy-done.6
  120.8 1.3 convolution_convert_fusion.1
  122.1 0.0 copy-done.9
  122.2 0.0 copy-done.11
  122.2 1.8 convolution_convert_fusion.2
  124.1 2.7 %pad_maximum_fusion = bf16[32,64,1024]{2,1,0:T(8,128)(2,1)} fusion(bf16[32,32,1024]{2,1,0:T(8,128)(2,1)S(1)} %bitcast.72, bf16[32,32,1024]{2,1,0:T(8,128)(2,1)S(1)} %bitcast.71), kind=kLoop, calls=%fused_computation | loop fusion | flops 8388608 | bytes 8388608 | tf_op jit(solution)/shard_map/concatenate | solution.py:89
  126.7 7.5 %all-to-all-start.1 = ((bf16[32,64,1024]{2,1,0:T(8,128)(2,1)}), bf16[32,64,1024]{2,1,0:T(8,128)(2,1)}, u32[]{:S(2)}, u32[]{:S(2)}) async-start(bf16[32,64,1024]{2,1,0:T(8,128)(2,1)} %pad_maximum_fusion), calls=%async_computation.1 | async-start | bytes 8388608 | tf_op jit(solution)/shard_map/all_to_all | solution.py:96
  134.2 0.0 copy-done.1
  134.3 55.2 %reduce-scatter.4.cloned.1.call-done = bf16[64,1152]{1,0:T(8,128)(2,1)} async-done(((bf16[1024,1152]{1,0:T(8,128)(2,1)}), bf16[64,1152]{1,0:T(8,128)(2,1)}) %reduce-scatter.4.cloned.1.call-update) | async-done | bytes 147472
  189.5 1.1 copy.54
  190.6 0.0 all-to-all-done.1
  190.7 0.7 copy.50
  191.4 0.7 copy.51
  192.1 0.7 copy.52
  192.8 4.6 %fusion = f32[512,1024]{1,0:T(8,128)S(1)} fusion(bf16[2048,1024]{1,0:T(8,128)(2,1)} %bitcast.16, s32[512]{0:T(512)S(1)} %pad_add_fusion), kind=kOutput, calls=%fused_computation.2 | convolution fusion | flops 2148532224 | bytes 6293504 | tf_op jit(solution)/shard_map/dot_general | solution.py:105
  197.4 0.7 fusion.9
  198.1 0.8 multiply_reduce_fusion
  198.9 0.8 reduce_sum.43
  (14 shorter events, 0.1 us)
Async XLA Ops:
  8.2 4.2 %copy-start.5 = (f32[128,2]{0,1:T(2,128)S(1)}, f32[128,2]{0,1:T(2,128)}, u32[]{:S(2)}) copy-start(f32[128,2]{0,1:T(2,128)} %param.9) | copy-start | bytes 3076
  11.7 1.4 copy-start.7
  17.4 10.6 %copy-start.2 = (bf16[1,384,64]{1,2,0:T(8,128)(2,1)S(1)}, bf16[1,384,64]{1,2,0:T(8,128)(2,1)}, u32[]{:S(2)}) copy-start(bf16[1,384,64]{1,2,0:T(8,128)(2,1)} %param.12) | copy-start | bytes 147460
  17.4 10.6 %copy-start.3 = (bf16[1,64,384]{2,1,0:T(8,128)(2,1)S(1)}, bf16[1,64,384]{2,1,0:T(8,128)(2,1)}, u32[]{:S(2)}) copy-start(bf16[1,64,384]{2,1,0:T(8,128)(2,1)} %param.11) | copy-start | bytes 147460
  17.4 10.6 %copy-start.4 = (bf16[1,64,384]{2,1,0:T(8,128)(2,1)S(1)}, bf16[1,64,384]{2,1,0:T(8,128)(2,1)}, u32[]{:S(2)}) copy-start(bf16[1,64,384]{2,1,0:T(8,128)(2,1)} %param.10) | copy-start | bytes 147460
  17.4 62.0 %all-to-all-start = ((bf16[32,64,1024]{2,1,0:T(8,128)(2,1)}), bf16[32,64,1024]{2,1,0:T(8,128)(2,1)}, u32[]{:S(2)}, u32[]{:S(2)}) async-start(bf16[32,64,1024]{2,1,0:T(8,128)(2,1)} %bitcast.66), calls=%async_computation | async-start | bytes 8388608 | tf_op jit(solution)/shard_map/all_to_all | solution.py:55
  27.9 79.2 %all-gather.3.cloned.1.call-start = ((), (), s32[]{:S(2)}) async-start(), calls=%async_computation.3 | async-start | bytes 2506752 | tf_op jit(solution)/shard_map/all_gather | solution.py:37
  28.7 160.9 %reduce-scatter.4.cloned.1.call-start = ((), (), s32[]{:S(2)}) async-start(), calls=%async_computation.4 | async-start | bytes 2506752
  107.1 3.5 %copy-start = (bf16[32,32,1024]{2,1,0:T(8,128)(2,1)S(1)}, bf16[32,32,1024]{2,1,0:T(8,128)(2,1)}, u32[]{:S(2)}) copy-start(bf16[32,32,1024]{2,1,0:T(8,128)(2,1)} %get-tuple-element.45) | copy-start | bytes 6291460
  113.4 1.0 copy-start.8
  113.4 1.1 copy-start.10
  119.2 1.7 copy-start.6
  120.8 1.3 copy-start.9
  120.8 1.4 copy-start.11
  126.7 7.5 %copy-start.1 = (bf16[128,1024]{1,0:T(8,128)(2,1)S(1)}, bf16[128,1024]{1,0:T(8,128)(2,1)}, u32[]{:S(2)}) copy-start(bf16[128,1024]{1,0:T(8,128)(2,1)} %param.13) | copy-start | bytes 786436
  126.7 63.9 %all-to-all-start.1 = ((bf16[32,64,1024]{2,1,0:T(8,128)(2,1)}), bf16[32,64,1024]{2,1,0:T(8,128)(2,1)}, u32[]{:S(2)}, u32[]{:S(2)}) async-start(bf16[32,64,1024]{2,1,0:T(8,128)(2,1)} %pad_maximum_fusion), calls=%async_computation.1 | async-start | bytes 8388608 | tf_op jit(solution)/shard_map/all_to_all | solution.py:96
Sparse Core Ops, SparseCore 0:
  31.4 75.6 all-gather.2
  119.3 70.1 reduce-scatter.3

commit v6 on v5

--- a/solution.py
+++ b/solution.py
@@ -40,7 +40,7 @@
 
     grad_wide = grad_out.astype(jnp.float32)
     scaled = (
-        (route_probs[:, :, None] * grad_wide[:, None, :])
+        (route_probs.T[:, :, None] * grad_wide[None])
         .astype(jnp.bfloat16)
         .reshape(tok_rows * top_count, model_width)
     )
@@ -48,7 +48,7 @@
     slots = jnp.arange(2 * total_rows, dtype=jnp.int32)[:, None]
     pairs = base.reshape(tok_rows, top_count)
     pick_tok = (slots == pairs[None, :, 0]) | (slots == pairs[None, :, 1])
-    pick_grad = slots == (base + capacity)[None, :]
+    pick_grad = slots == (pairs.T.reshape(-1) + capacity)[None, :]
     chooser = jnp.concatenate([pick_tok, pick_grad], axis=1).astype(jnp.bfloat16)
     sources = jnp.concatenate([tokens, scaled], axis=0)
     outgoing = jnp.dot(chooser, sources, preferred_element_type=jnp.float32).astype(jnp.bfloat16)
@@ -59,6 +59,7 @@
         concat_axis=0,
         tiled=True,
     )
+    arrived, whole = lax.optimization_barrier((arrived, whole))
     slot_rows = arrived[:, :capacity].reshape(total_rows, model_width)
     grad_in = arrived[:, capacity:].reshape(total_rows, model_width)
 

time: 207 us -> 189 us (0.913)
  the two profiles are of different devices: /device:TPU:2 before, /device:TPU:12 now
where the time goes in v6:
time: 189 us
  waiting for transfers between devices  70 us (37%)
  blocking collectives  57.4 us (30%)
  matrix products  17.6 us (9%)
  between operations  14.3 us (8%)
  local copies, waits for them, and re-layouts  12.2 us (6%)
  other arithmetic  9.97 us (5%)
  starting transfers between devices  7.53 us (4%)
    all_to_all x1, blocking collectives, shards(): lax.all_to_all(outgoing.reshape(senders, 2 * capacity, model_width), 'exp...  57.4 us
    unnamed x3, waiting for transfers between devices  54.1 us
    all_gather x1, waiting for transfers between devices, shards(): whole = lax.all_gather(packed[None], 'dp', axis=1, tiled=True)[0]  15.8 us
    unnamed x23, local copies, waits for them, and re-layouts  7.61 us
    all_to_all x1, starting transfers between devices, shards(): lax.all_to_all(leaving, 'expert', split_axis=0, concat_axis=0, tiled=True)  7.45 us
    dot_general x1, matrix products, shards(): taken = jnp.dot(taker, home_flat, preferred_element_type=jnp.float32)  4.56 us
    dot_general x2, matrix products, contract_cols(): lax.dot_general(left_op, right_op, (((1,), (1,)), ((), ())), preferred_el...  4.41 us
  transfers between devices with their start and end apart: 3, of which 2 were waited for; matrix products, arithmetic and copies ran while one was open for 8% of the time, Pallas kernels for 0%

profile of v6, /device:TPU:12, one launch (start us, length us, event | category | flops | bytes accessed | tf_op | source)
XLA Modules:
  0.0 189.0 jit_solution(16406442462077537745)
XLA Ops:
  7.2 0.0 copy-start
  7.2 0.0 copy-start.3
  7.2 0.0 all-gather.3.cloned.1.call-start
  7.2 1.6 pad_maximum_fusion.5
  8.8 0.0 all-gather.3.cloned.1.call-update
  8.8 0.0 reduce-scatter.4.cloned.1.call-start
  8.9 0.8 copy.42
  9.7 0.1 eq.86
  9.8 0.1 eq.82
  9.9 0.6 reduce-window.6
  10.5 0.2 slice_reduce_fusion
  10.8 0.1 fusion.20
  10.9 0.1 reduce_sum.41
  11.0 0.1 copy.45
  11.1 0.7 broadcast_add_fusion
  11.8 0.3 iota_compare_fusion.2
  12.1 0.2 fusion.11
  12.4 1.0 convert_element_type.48
  13.4 0.0 copy-done
  13.4 0.1 fusion.9
  13.5 0.0 copy-done.3
  13.5 2.3 %convolution_convert_fusion = bf16[2048,1024]{1,0:T(8,128)(2,1)S(1)} fusion(pred[2048,256]{1,0:T(32,128)(4,1)S(1)} %iota_compare_fusion.2, pred[2048,128]{1,0:T(32,128)(4,1)S(1)} %fusion.11, bf16[256,1024]{1,0:T(8,128)(2,1)S(1)} %fusion.9, bf16[128,1024]{1,0:T(8,128)(2,1)S(1)} %copy-done.3), kind=kOutput, calls=%fused_computation.3 | convolution fusion | flops 1615069184 | bytes 5767168 | tf_op jit(solution)/shard_map/dot_general | solution.py:54
  15.9 57.4 %all_to_all.10 = bf16[32,64,1024]{2,1,0:T(8,128)(2,1)} all-to-all(bf16[32,64,1024]{2,1,0:T(8,128)(2,1)S(1)} %bitcast.71), channel_id=1, replica_groups=mesh['dp'=16,'expert'=32] {'expert'}, dimensions={0} | all-to-all | bytes 8388608 | tf_op jit(solution)/shard_map/all_to_all | solution.py:55
  73.3 15.8 %all-gather.3.cloned.1.call-done = bf16[1024,1152]{1,0:T(8,128)(2,1)} async-done(((bf16[64,1152]{1,0:T(8,128)(2,1)}), bf16[1024,1152]{1,0:T(8,128)(2,1)}) %all-gather.3.cloned.1.call-update) | async-done | bytes 2359312 | tf_op jit(solution)/shard_map/all_gather | solution.py:37
  89.1 0.0 copy-start.1
  89.1 2.8 %fusion.26 = (bf16[32,32,1024]{2,1,0:T(8,128)(2,1)S(1)}, bf16[32,32,1024]{2,1,0:T(8,128)(2,1)S(1)}) fusion(bf16[32,64,1024]{2,1,0:T(8,128)(2,1)} %all_to_all.10), kind=kLoop, calls=%fused_computation.59 | loop fusion | bytes 8388608 | tf_op jit(solution)/shard_map/slice | solution.py:63
  92.0 0.1 copy-done.1
  92.1 1.9 fusion.7
  93.9 1.7 multiply_convert_fusion.1
  95.6 0.0 copy-start.4
  95.6 0.0 copy-start.5
  95.6 0.0 copy-start.7
  95.6 1.0 convolution_convert_fusion.4
  96.6 0.0 copy-done.4
  96.6 0.1 copy-done.5
  96.7 0.3 copy-done.7
  97.0 1.8 convolution_convert_fusion.3
  98.8 0.2 pad_maximum_fusion.1
  99.0 2.5 %copy.49 = bf16[1024,1152]{1,0:T(8,128)(2,1)} copy(bf16[1024,1152]{0,1:T(8,128)(2,1)S(1)} %pad_maximum_fusion.1) | data formatting | bytes 4718592
  101.6 0.0 copy-start.2
  101.6 0.0 reduce-scatter.4.cloned.1.call-update
  101.6 1.6 copy-done.2
  103.2 0.0 copy-start.6
  103.2 0.0 copy-start.8
  103.2 2.6 %convolution_convert_fusion.1 = bf16[1024,1024]{1,0:T(8,128)(2,1)S(1)} fusion(bf16[1024,384]{0,1:T(8,128)(2,1)} %copy-done.4, bf16[1024,1152]{1,0:T(8,128)(2,1)S(1)} %copy-done.2), kind=kOutput, calls=%fused_computation.10 | convolution fusion | flops 806354944 | bytes 3670016 | tf_op jit(solution)/shard_map/dot_general | solution.py:22
  105.8 0.0 copy-done.6
  105.8 0.0 copy-done.8
  105.8 1.9 convolution_convert_fusion.2
  107.7 2.7 %pad_maximum_fusion = bf16[32,64,1024]{2,1,0:T(8,128)(2,1)} fusion(bf16[32,32,1024]{2,1,0:T(8,128)(2,1)S(1)} %bitcast.77, bf16[32,32,1024]{2,1,0:T(8,128)(2,1)S(1)} %bitcast.76), kind=kLoop, calls=%fused_computation | loop fusion | flops 8388608 | bytes 8388608 | tf_op jit(solution)/shard_map/concatenate | solution.py:90
  110.4 7.4 %all-to-all-start.1 = ((bf16[32,64,1024]{2,1,0:T(8,128)(2,1)}), bf16[32,64,1024]{2,1,0:T(8,128)(2,1)}, u32[]{:S(2)}, u32[]{:S(2)}) async-start(bf16[32,64,1024]{2,1,0:T(8,128)(2,1)} %pad_maximum_fusion), calls=%async_computation.1 | async-start | bytes 8388608 | tf_op jit(solution)/shard_map/all_to_all | solution.py:97
  117.8 54.1 %reduce-scatter.4.cloned.1.call-done = bf16[64,1152]{1,0:T(8,128)(2,1)} async-done(((bf16[1024,1152]{1,0:T(8,128)(2,1)}), bf16[64,1152]{1,0:T(8,128)(2,1)}) %reduce-scatter.4.cloned.1.call-update) | async-done | bytes 147472
  171.9 1.1 copy.50
  173.1 0.0 all-to-all-done.1
  173.1 4.6 %fusion = f32[512,1024]{1,0:T(8,128)S(1)} fusion(bf16[2048,1024]{1,0:T(8,128)(2,1)} %bitcast.18, s32[512]{0:T(512)S(1)} %pad_add_fusion), kind=kOutput, calls=%fused_computation.2 | convolution fusion | flops 2148532224 | bytes 6293504 | tf_op jit(solution)/shard_map/dot_general | solution.py:106
  177.6 0.7 fusion.10
  178.4 0.7 copy.48
  179.1 0.7 copy.47
  179.8 0.7 copy.46
  180.5 0.8 reduce_sum.43
  181.4 0.8 multiply_reduce_fusion
  (6 shorter events, 0.1 us)
Async XLA Ops:
  7.2 6.2 %copy-start = (f32[128,2]{0,1:T(2,128)S(1)}, f32[128,2]{0,1:T(2,128)}, u32[]{:S(2)}) copy-start(f32[128,2]{0,1:T(2,128)} %param.9) | copy-start | bytes 3076
  7.2 6.3 %copy-start.3 = (bf16[128,1024]{1,0:T(8,128)(2,1)S(1)}, bf16[128,1024]{1,0:T(8,128)(2,1)}, u32[]{:S(2)}) copy-start(bf16[128,1024]{1,0:T(8,128)(2,1)} %param.7) | copy-start | bytes 786436
  7.2 81.9 %all-gather.3.cloned.1.call-start = ((), (), s32[]{:S(2)}) async-start(), calls=%async_computation.3 | async-start | bytes 2506752 | tf_op jit(solution)/shard_map/all_gather | solution.py:37
  8.8 163.1 %reduce-scatter.4.cloned.1.call-start = ((), (), s32[]{:S(2)}) async-start(), calls=%async_computation.4 | async-start | bytes 2506752
  89.1 2.9 %copy-start.1 = (bf16[1024,1152]{1,0:T(8,128)(2,1)S(1)}, bf16[1024,1152]{1,0:T(8,128)(2,1)}, u32[]{:S(2)}) copy-start(bf16[1024,1152]{1,0:T(8,128)(2,1)} %all-gather.3.cloned.1.call-done) | copy-start | bytes 7077892
  95.6 1.0 copy-start.4
  95.6 1.1 copy-start.5
  95.6 1.4 copy-start.7
  101.6 1.7 copy-start.2
  103.2 2.6 %copy-start.6 = (bf16[1024,384]{0,1:T(8,128)(2,1)S(1)}, bf16[1024,384]{0,1:T(8,128)(2,1)}, u32[]{:S(2)}) copy-start(bf16[1024,384]{0,1:T(8,128)(2,1)} %copy-done.5) | copy-start | bytes 2359300
  103.2 2.6 %copy-start.8 = (bf16[1024,384]{0,1:T(8,128)(2,1)S(1)}, bf16[1024,384]{0,1:T(8,128)(2,1)}, u32[]{:S(2)}) copy-start(bf16[1024,384]{0,1:T(8,128)(2,1)} %copy-done.7) | copy-start | bytes 2359300
  110.4 62.7 %all-to-all-start.1 = ((bf16[32,64,1024]{2,1,0:T(8,128)(2,1)}), bf16[32,64,1024]{2,1,0:T(8,128)(2,1)}, u32[]{:S(2)}, u32[]{:S(2)}) async-start(bf16[32,64,1024]{2,1,0:T(8,128)(2,1)} %pad_maximum_fusion), calls=%async_computation.1 | async-start | bytes 8388608 | tf_op jit(solution)/shard_map/all_to_all | solution.py:97
Sparse Core Ops, SparseCore 0:
  10.7 78.4 all-gather.2
  101.7 70.1 reduce-scatter.3

commit v7 on v6

--- a/solution.py
+++ b/solution.py
@@ -35,9 +35,6 @@
 
     packed = jnp.concatenate([w_gate[0], w_up[0], w_down[0].T], axis=1)
     whole = lax.all_gather(packed[None], "dp", axis=1, tiled=True)[0]
-    gate_up = whole[:, : 2 * hidden_width]
-    down_t = whole[:, 2 * hidden_width :]
-
     grad_wide = grad_out.astype(jnp.float32)
     scaled = (
         (route_probs.T[:, :, None] * grad_wide[None])
@@ -45,23 +42,26 @@
         .reshape(tok_rows * top_count, model_width)
     )
     base = flat_ids * (2 * capacity) + slot_of
-    slots = jnp.arange(2 * total_rows, dtype=jnp.int32)[:, None]
-    pairs = base.reshape(tok_rows, top_count)
-    pick_tok = (slots == pairs[None, :, 0]) | (slots == pairs[None, :, 1])
-    pick_grad = slots == (pairs.T.reshape(-1) + capacity)[None, :]
-    chooser = jnp.concatenate([pick_tok, pick_grad], axis=1).astype(jnp.bfloat16)
-    sources = jnp.concatenate([tokens, scaled], axis=0)
-    outgoing = jnp.dot(chooser, sources, preferred_element_type=jnp.float32).astype(jnp.bfloat16)
-    arrived = lax.all_to_all(
-        outgoing.reshape(senders, 2 * capacity, model_width),
-        "expert",
-        split_axis=0,
-        concat_axis=0,
-        tiled=True,
+    place = flat_ids * capacity + slot_of
+    slots = jnp.arange(total_rows, dtype=jnp.int32)[:, None]
+    pairs = place.reshape(tok_rows, top_count)
+    pick_tok = ((slots == pairs[None, :, 0]) | (slots == pairs[None, :, 1])).astype(jnp.bfloat16)
+    pick_grad = (slots == pairs.T.reshape(-1)[None, :]).astype(jnp.bfloat16)
+    tok_send = jnp.dot(pick_tok, tokens, preferred_element_type=jnp.float32).astype(jnp.bfloat16)
+    grad_send = jnp.dot(pick_grad, scaled, preferred_element_type=jnp.float32).astype(jnp.bfloat16)
+    slot_rows, grad_in = (
+        lax.all_to_all(
+            sent.reshape(senders, capacity, model_width),
+            "expert",
+            split_axis=0,
+            concat_axis=0,
+            tiled=True,
+        ).reshape(total_rows, model_width)
+        for sent in (tok_send, grad_send)
     )
-    arrived, whole = lax.optimization_barrier((arrived, whole))
-    slot_rows = arrived[:, :capacity].reshape(total_rows, model_width)
-    grad_in = arrived[:, capacity:].reshape(total_rows, model_width)
+    slot_rows, grad_in, whole = lax.optimization_barrier((slot_rows, grad_in, whole))
+    gate_up = whole[:, : 2 * hidden_width]
+    down_t = whole[:, 2 * hidden_width :]
 
     both_pre = jnp.dot(slot_rows, gate_up, preferred_element_type=jnp.float32)
     gate_pre = both_pre[:, :hidden_width]

time: 189 us -> 192 us (1.016)
  the two profiles are of different devices: /device:TPU:12 before, /device:TPU:2 now
where the time goes in v7:
time: 192 us; the launch traced here: 191 us
  waiting for transfers between devices  84.8 us (44%)
  blocking collectives  33.2 us (17%)
  matrix products  22.9 us (12%)
  starting transfers between devices  18.1 us (9%)
  between operations  14.3 us (7%)
  local copies, waits for them, and re-layouts  9.33 us (5%)
  other arithmetic  8.48 us (4%)
    unnamed x3, waiting for transfers between devices  53.9 us
    all_to_all x1, blocking collectives, shards(): lax.all_to_all(sent.reshape(senders, capacity, model_width), 'expert', sp...  33.2 us
    all_to_all x1, waiting for transfers between devices, shards(): lax.all_to_all(sent.reshape(senders, capacity, model_width), 'expert', sp...  27 us
    all_to_all x1, starting transfers between devices, shards(): lax.all_to_all(sent.reshape(senders, capacity, model_width), 'expert', sp...  10.4 us
    all_to_all x1, starting transfers between devices, shards(): lax.all_to_all(leaving, 'expert', split_axis=0, concat_axis=0, tiled=True)  7.61 us
    unnamed x27, local copies, waits for them, and re-layouts  7.52 us
    dot_general x1, matrix products, shards(): taken = jnp.dot(taker, home_flat, preferred_element_type=jnp.float32)  4.56 us
    dot_general x2, matrix products, contract_cols(): lax.dot_general(left_op, right_op, (((1,), (1,)), ((), ())), preferred_el...  4.41 us
  transfers between devices with their start and end apart: 4, of which 3 were waited for; matrix products, arithmetic and copies ran while one was open for 7% of the time, Pallas kernels for 0%

profile of v7, /device:TPU:2, one launch (start us, length us, event | category | flops | bytes accessed | tf_op | source)
XLA Modules:
  0.0 191.0 jit_solution(10893639472220600248)
XLA Ops:
  7.2 0.0 copy-start
  7.2 0.0 all-gather.3.cloned.1.call-start
  7.2 1.6 pad_maximum_fusion.5
  8.8 0.0 all-gather.3.cloned.1.call-update
  8.8 0.8 copy.50
  9.6 0.1 eq.88
  9.7 0.1 eq.84
  9.9 0.6 reduce-window.6
  10.5 0.2 slice_reduce_fusion
  10.7 0.1 fusion.18
  10.8 0.1 reduce_sum.41
  11.0 0.1 copy.53
  11.0 0.7 multiply_add_fusion
  11.7 0.0 copy-done
  11.7 2.1 %convolution_convert_fusion.2 = bf16[1024,1024]{1,0:T(8,128)(2,1)} fusion(bf16[128,1024]{1,0:T(8,128)(2,1)S(1)} %copy-done, s32[128]{0:T(128)S(1)} %get-tuple-element.58, s32[128]{0:T(128)S(1)} %get-tuple-element.57), kind=kOutput, calls=%fused_computation.7 | convolution fusion | flops 269877248 | bytes 2360320 | tf_op jit(solution)/shard_map/dot_general | solution.py:50
  13.8 0.0 copy-start.2
  13.8 0.0 copy-start.4
  13.8 10.4 %all-to-all-start = ((bf16[32,32,1024]{2,1,0:T(8,128)(2,1)}), bf16[32,32,1024]{2,1,0:T(8,128)(2,1)}, u32[]{:S(2)}, u32[]{:S(2)}) async-start(bf16[32,32,1024]{2,1,0:T(8,128)(2,1)} %bitcast.7), calls=%async_computation | async-start | bytes 4194304 | tf_op jit(solution)/shard_map/all_to_all | solution.py:53
  24.2 0.0 reduce-scatter.4.cloned.1.call-start
  24.3 0.0 copy-done.2
  24.3 0.0 copy-done.4
  24.3 0.1 fusion.6
  24.5 0.7 convolution_convert_fusion.1
  25.2 27.0 %all-to-all-done = bf16[32,32,1024]{2,1,0:T(8,128)(2,1)} async-done(((bf16[32,32,1024]{2,1,0:T(8,128)(2,1)}), bf16[32,32,1024]{2,1,0:T(8,128)(2,1)}, u32[]{:S(2)}, u32[]{:S(2)}) %all-to-all-start) | async-done | bytes 2097184 | tf_op jit(solution)/shard_map/all_to_all | solution.py:53
  52.2 33.2 %all_to_all.15 = bf16[32,32,1024]{2,1,0:T(8,128)(2,1)} all-to-all(bf16[32,32,1024]{2,1,0:T(8,128)(2,1)S(1)} %bitcast.76), channel_id=1, replica_groups=mesh['dp'=16,'expert'=32] {'expert'}, dimensions={0} | all-to-all | bytes 4194304 | tf_op jit(solution)/shard_map/all_to_all | solution.py:53
  85.4 3.9 %all-gather.3.cloned.1.call-done = bf16[1024,1152]{1,0:T(8,128)(2,1)} async-done(((bf16[64,1152]{1,0:T(8,128)(2,1)}), bf16[1024,1152]{1,0:T(8,128)(2,1)}) %all-gather.3.cloned.1.call-update) | async-done | bytes 2359312 | tf_op jit(solution)/shard_map/all_gather | solution.py:37
  89.3 0.0 copy-start.1
  89.3 4.0 %fusion.4 = f32[1024,768]{0,1:T(8,128)S(1)} fusion(bf16[1024,1024]{1,0:T(8,128)(2,1)} %bitcast.8, bf16[1024,1152]{1,0:T(8,128)(2,1)} %all-gather.3.cloned.1.call-done), kind=kOutput, calls=%fused_computation.20 | convolution fusion | flops 1610612736 | bytes 6815744 | tf_op jit(solution)/shard_map/dot_general | solution.py:66
  93.3 0.0 copy-done.1
  93.3 2.7 %multiply_convert_fusion.1 = (bf16[1024,384]{0,1:T(8,128)(2,1)S(1)}, bf16[1024,384]{0,1:T(8,128)(2,1)S(1)}, bf16[1024,384]{0,1:T(8,128)(2,1)S(1)}) fusion(f32[1024,768]{0,1:T(8,128)S(1)} %fusion.4, bf16[1024,1024]{1,0:T(8,128)(2,1)S(1)} %bitcast.79, bf16[1024,1152]{1,0:T(8,128)(2,1)} %all-gather.3.cloned.1.call-done), kind=kOutput, calls=%fused_computation.14 | convolution fusion | flops 811204608 | bytes 8388608 | tf_op jit(solution)/shard_map/dot_general | solution.py:72
  96.0 0.0 copy-start.6
  96.1 0.0 copy-start.7
  96.1 0.0 copy-start.9
  96.1 1.0 convolution_convert_fusion.5
  97.1 0.0 copy-done.6
  97.1 0.2 copy-done.7
  97.2 0.2 copy-done.9
  97.5 3.4 %convolution_convert_fusion.4 = bf16[1024,768]{0,1:T(8,128)(2,1)S(1)} fusion(bf16[1024,1024]{1,0:T(8,128)(2,1)} %bitcast.8, bf16[1024,384]{0,1:T(8,128)(2,1)S(1)} %get-tuple-element.49, bf16[1024,384]{0,1:T(8,128)(2,1)S(1)} %get-tuple-element.48), kind=kOutput, calls=%fused_computation.9 | convolution fusion | flops 1614544896 | bytes 5242880 | tf_op jit(solution)/shard_map/dot_general | solution.py:16
  100.9 0.2 pad_maximum_fusion.1
  101.1 2.5 %copy.58 = bf16[1024,1152]{1,0:T(8,128)(2,1)} copy(bf16[1024,1152]{0,1:T(8,128)(2,1)S(1)} %pad_maximum_fusion.1) | data formatting | bytes 4718592
  103.6 0.0 copy-start.5
  103.6 0.0 reduce-scatter.4.cloned.1.call-update
  103.6 1.6 copy-done.5
  105.3 0.0 copy-start.8
  105.3 0.0 copy-start.10
  105.3 2.6 %convolution_convert_fusion = bf16[1024,1024]{1,0:T(8,128)(2,1)S(1)} fusion(bf16[1024,384]{0,1:T(8,128)(2,1)} %copy-done.6, bf16[1024,1152]{1,0:T(8,128)(2,1)S(1)} %copy-done.5), kind=kOutput, calls=%fused_computation.5 | convolution fusion | flops 806354944 | bytes 3670016 | tf_op jit(solution)/shard_map/dot_general | solution.py:22
  107.8 0.0 copy-done.8
  107.9 0.0 copy-done.10
  107.9 1.9 convolution_convert_fusion.3
  109.7 2.7 %pad_maximum_fusion = bf16[32,64,1024]{2,1,0:T(8,128)(2,1)} fusion(bf16[32,32,1024]{2,1,0:T(8,128)(2,1)S(1)} %bitcast.82, bf16[32,32,1024]{2,1,0:T(8,128)(2,1)S(1)} %bitcast.81), kind=kLoop, calls=%fused_computation | loop fusion | flops 8388608 | bytes 8388608 | tf_op jit(solution)/shard_map/concatenate | solution.py:90
  112.4 0.0 copy-start.3
  112.4 7.6 %all-to-all-start.2 = ((bf16[32,64,1024]{2,1,0:T(8,128)(2,1)}), bf16[32,64,1024]{2,1,0:T(8,128)(2,1)}, u32[]{:S(2)}, u32[]{:S(2)}) async-start(bf16[32,64,1024]{2,1,0:T(8,128)(2,1)} %pad_maximum_fusion), calls=%async_computation.2 | async-start | bytes 8388608 | tf_op jit(solution)/shard_map/all_to_all | solution.py:97
  120.0 0.0 copy-done.3
  120.1 53.8 %reduce-scatter.4.cloned.1.call-done = bf16[64,1152]{1,0:T(8,128)(2,1)} async-done(((bf16[1024,1152]{1,0:T(8,128)(2,1)}), bf16[64,1152]{1,0:T(8,128)(2,1)}) %reduce-scatter.4.cloned.1.call-update) | async-done | bytes 147472
  173.9 1.1 copy.59
  175.0 0.0 all-to-all-done.2
  175.0 4.6 %fusion = f32[512,1024]{1,0:T(8,128)S(1)} fusion(bf16[2048,1024]{1,0:T(8,128)(2,1)} %bitcast.21, s32[512]{0:T(512)S(1)} %pad_add_fusion), kind=kOutput, calls=%fused_computation.2 | convolution fusion | flops 2148532224 | bytes 6293504 | tf_op jit(solution)/shard_map/dot_general | solution.py:106
  179.6 0.7 fusion.7
  180.4 0.7 copy.55
  181.1 0.7 copy.56
  181.8 0.7 copy.57
  182.5 0.8 multiply_reduce_fusion
  183.4 0.8 reduce_sum.43
  (8 shorter events, 0.1 us)
Async XLA Ops:
  7.2 4.6 %copy-start = (bf16[128,1024]{1,0:T(8,128)(2,1)S(1)}, bf16[128,1024]{1,0:T(8,128)(2,1)}, u32[]{:S(2)}) copy-start(bf16[128,1024]{1,0:T(8,128)(2,1)} %param.7) | copy-start | bytes 786436
  7.2 82.1 %all-gather.3.cloned.1.call-start = ((), (), s32[]{:S(2)}) async-start(), calls=%async_computation.4 | async-start | bytes 2506752 | tf_op jit(solution)/shard_map/all_gather | solution.py:37
  13.8 10.5 %copy-start.2 = (bf16[128,1024]{1,0:T(8,128)(2,1)S(1)}, bf16[128,1024]{1,0:T(8,128)(2,1)}, u32[]{:S(2)}) copy-start(bf16[128,1024]{1,0:T(8,128)(2,1)} %param.13) | copy-start | bytes 786436
  13.8 10.5 %copy-start.4 = (f32[128,2]{0,1:T(2,128)S(1)}, f32[128,2]{0,1:T(2,128)}, u32[]{:S(2)}) copy-start(f32[128,2]{0,1:T(2,128)} %param.9) | copy-start | bytes 3076
  13.8 38.4 %all-to-all-start = ((bf16[32,32,1024]{2,1,0:T(8,128)(2,1)}), bf16[32,32,1024]{2,1,0:T(8,128)(2,1)}, u32[]{:S(2)}, u32[]{:S(2)}) async-start(bf16[32,32,1024]{2,1,0:T(8,128)(2,1)} %bitcast.7), calls=%async_computation | async-start | bytes 4194304 | tf_op jit(solution)/shard_map/all_to_all | solution.py:53
  24.2 149.7 %reduce-scatter.4.cloned.1.call-start = ((), (), s32[]{:S(2)}) async-start(), calls=%async_computation.5 | async-start | bytes 2506752
  89.3 4.0 %copy-start.1 = (bf16[32,32,1024]{2,1,0:T(8,128)(2,1)S(1)}, bf16[32,32,1024]{2,1,0:T(8,128)(2,1)}, u32[]{:S(2)}) copy-start(bf16[32,32,1024]{2,1,0:T(8,128)(2,1)} %all_to_all.15) | copy-start | bytes 6291460
  96.0 1.0 copy-start.6
  96.1 1.2 copy-start.7
  96.1 1.4 copy-start.9
  103.6 1.7 copy-start.5
  105.3 2.6 %copy-start.8 = (bf16[1024,384]{0,1:T(8,128)(2,1)S(1)}, bf16[1024,384]{0,1:T(8,128)(2,1)}, u32[]{:S(2)}) copy-start(bf16[1024,384]{0,1:T(8,128)(2,1)} %copy-done.7) | copy-start | bytes 2359300
  105.3 2.6 %copy-start.10 = (bf16[1024,384]{0,1:T(8,128)(2,1)S(1)}, bf16[1024,384]{0,1:T(8,128)(2,1)}, u32[]{:S(2)}) copy-start(bf16[1024,384]{0,1:T(8,128)(2,1)} %copy-done.9) | copy-start | bytes 2359300
  112.4 7.6 %copy-start.3 = (s32[128,2]{0,1:T(2,128)S(1)}, s32[128,2]{0,1:T(2,128)}, u32[]{:S(2)}) copy-start(s32[128,2]{0,1:T(2,128)} %param.8) | copy-start | bytes 3076
  112.4 62.6 %all-to-all-start.2 = ((bf16[32,64,1024]{2,1,0:T(8,128)(2,1)}), bf16[32,64,1024]{2,1,0:T(8,128)(2,1)}, u32[]{:S(2)}, u32[]{:S(2)}) async-start(bf16[32,64,1024]{2,1,0:T(8,128)(2,1)} %pad_maximum_fusion), calls=%async_computation.2 | async-start | bytes 8388608 | tf_op jit(solution)/shard_map/all_to_all | solution.py:97
Sparse Core Ops, SparseCore 0:
  10.7 78.5 all-gather.2
  103.8 70.1 reduce-scatter.3

commit v8 on v6

--- a/solution.py
+++ b/solution.py
@@ -97,15 +97,19 @@
     back_home = lax.all_to_all(leaving, "expert", split_axis=0, concat_axis=0, tiled=True)
 
     back_home, summed = lax.optimization_barrier((back_home, summed))
-    home_flat = back_home.reshape(2 * total_rows, model_width)
-    own_place = base.reshape(tok_rows, top_count).T.reshape(-1)
-    wanted = jnp.concatenate([own_place, own_place + capacity])
-    taker = (jnp.arange(2 * total_rows, dtype=jnp.int32)[None, :] == wanted[:, None]).astype(
+    own_place = (flat_ids * capacity + slot_of).reshape(tok_rows, top_count).T.reshape(-1)
+    taker = (jnp.arange(total_rows, dtype=jnp.int32)[None, :] == own_place[:, None]).astype(
         jnp.bfloat16
+    ).reshape(tok_rows * top_count, senders, capacity)
+    picked, back_picked = (
+        lax.dot_general(
+            taker,
+            back_home[:, half * capacity : (half + 1) * capacity],
+            (((1, 2), (0, 1)), ((), ())),
+            preferred_element_type=jnp.float32,
+        ).reshape(top_count, tok_rows, model_width)
+        for half in (0, 1)
     )
-    taken = jnp.dot(taker, home_flat, preferred_element_type=jnp.float32)
-    picked = taken[: tok_rows * top_count].reshape(top_count, tok_rows, model_width)
-    back_picked = taken[tok_rows * top_count :].reshape(top_count, tok_rows, model_width)
     probs_k = route_probs.T[:, :, None]
     mixed_out = jnp.sum(probs_k * picked, axis=0).astype(jnp.bfloat16)
     grad_probs = jnp.sum(grad_wide[None] * picked, axis=2).T

time: 189 us -> 189 us (level)
  the two profiles are of different devices: /device:TPU:12 before, /device:TPU:20 now
where the time goes in v8:
time: 189 us
  waiting for transfers between devices  71.4 us (38%)
  blocking collectives  56.1 us (30%)
  matrix products  19.9 us (11%)
  between operations  14.3 us (8%)
  local copies, waits for them, and re-layouts  12.2 us (6%)
  other arithmetic  7.57 us (4%)
  starting transfers between devices  7.52 us (4%)
    all_to_all x1, blocking collectives, shards(): lax.all_to_all(outgoing.reshape(senders, 2 * capacity, model_width), 'exp...  56.1 us
    unnamed x3, waiting for transfers between devices  54.3 us
    all_gather x1, waiting for transfers between devices, shards(): whole = lax.all_gather(packed[None], 'dp', axis=1, tiled=True)[0]  17.1 us
    unnamed x23, local copies, waits for them, and re-layouts  7.6 us
    all_to_all x1, starting transfers between devices, shards(): lax.all_to_all(leaving, 'expert', split_axis=0, concat_axis=0, tiled=True)  7.44 us
    dot_general x2, matrix products, shards(): lax.dot_general(taker, back_home[:, half * capacity:(half + 1) * capacity...  6.76 us
    dot_general x2, matrix products, contract_cols(): lax.dot_general(left_op, right_op, (((1,), (1,)), ((), ())), preferred_el...  4.42 us
  transfers between devices with their start and end apart: 3, of which 2 were waited for; matrix products, arithmetic and copies ran while one was open for 8% of the time, Pallas kernels for 0%

profile of v8, /device:TPU:20, one launch (start us, length us, event | category | flops | bytes accessed | tf_op | source)
XLA Modules:
  0.0 189.0 jit_solution(14123776317597047402)
XLA Ops:
  7.2 0.0 copy-start
  7.2 0.0 copy-start.3
  7.2 0.0 all-gather.3.cloned.1.call-start
  7.2 1.6 pad_maximum_fusion.5
  8.8 0.0 all-gather.3.cloned.1.call-update
  8.8 0.0 reduce-scatter.4.cloned.1.call-start
  8.9 0.8 copy.51
  9.7 0.1 eq.98
  9.8 0.1 eq.94
  9.9 0.6 reduce-window.6
  10.5 0.2 slice_reduce_fusion
  10.8 0.1 fusion.40
  10.9 0.1 reduce_sum.39
  11.0 0.1 copy.54
  11.1 0.7 add_bitcast_fusion.1
  11.8 0.3 iota_compare_fusion
  12.1 0.2 fusion.27
  12.4 1.0 convert_element_type.48
  13.4 0.0 copy-done
  13.4 0.1 fusion.26
  13.5 0.0 copy-done.3
  13.5 2.3 %convolution_convert_fusion = bf16[2048,1024]{1,0:T(8,128)(2,1)S(1)} fusion(pred[2048,256]{1,0:T(32,128)(4,1)S(1)} %iota_compare_fusion, pred[2048,128]{1,0:T(32,128)(4,1)S(1)} %fusion.27, bf16[256,1024]{1,0:T(8,128)(2,1)S(1)} %fusion.26, bf16[128,1024]{1,0:T(8,128)(2,1)S(1)} %copy-done.3), kind=kOutput, calls=%fused_computation.1 | convolution fusion | flops 1615069184 | bytes 5767168 | tf_op jit(solution)/shard_map/dot_general | solution.py:54
  15.9 56.1 %all_to_all.10 = bf16[32,64,1024]{2,1,0:T(8,128)(2,1)} all-to-all(bf16[32,64,1024]{2,1,0:T(8,128)(2,1)S(1)} %bitcast.84), channel_id=1, replica_groups=mesh['dp'=16,'expert'=32] {'expert'}, dimensions={0} | all-to-all | bytes 8388608 | tf_op jit(solution)/shard_map/all_to_all | solution.py:55
  72.0 17.1 %all-gather.3.cloned.1.call-done = bf16[1024,1152]{1,0:T(8,128)(2,1)} async-done(((bf16[64,1152]{1,0:T(8,128)(2,1)}), bf16[1024,1152]{1,0:T(8,128)(2,1)}) %all-gather.3.cloned.1.call-update) | async-done | bytes 2359312 | tf_op jit(solution)/shard_map/all_gather | solution.py:37
  89.0 0.0 copy-start.1
  89.0 2.8 %fusion.46 = (bf16[32,32,1024]{2,1,0:T(8,128)(2,1)S(1)}, bf16[32,32,1024]{2,1,0:T(8,128)(2,1)S(1)}) fusion(bf16[32,64,1024]{2,1,0:T(8,128)(2,1)} %all_to_all.10), kind=kLoop, calls=%fused_computation.71 | loop fusion | bytes 8388608 | tf_op jit(solution)/shard_map/slice | solution.py:63
  91.9 0.1 copy-done.1
  92.0 1.9 %fusion.11 = f32[1024,768]{0,1:T(8,128)S(1)} fusion(bf16[1024,1024]{1,0:T(8,128)(2,1)S(1)} %bitcast.85, bf16[1024,1152]{1,0:T(8,128)(2,1)S(1)} %copy-done.1), kind=kOutput, calls=%fused_computation.24 | convolution fusion | flops 1610612736 | bytes 6815744 | tf_op jit(solution)/shard_map/dot_general | solution.py:66
  93.9 1.7 multiply_convert_fusion.1
  95.6 0.0 copy-start.4
  95.6 0.0 copy-start.5
  95.6 0.0 copy-start.7
  95.6 1.0 convolution_convert_fusion.4
  96.6 0.0 copy-done.4
  96.6 0.1 copy-done.5
  96.7 0.3 copy-done.7
  97.0 1.8 convolution_convert_fusion.3
  98.8 0.2 pad_maximum_fusion.1
  99.0 2.5 %copy.61 = bf16[1024,1152]{1,0:T(8,128)(2,1)} copy(bf16[1024,1152]{0,1:T(8,128)(2,1)S(1)} %pad_maximum_fusion.1) | data formatting | bytes 4718592
  101.5 0.0 copy-start.2
  101.5 0.0 reduce-scatter.4.cloned.1.call-update
  101.6 1.6 copy-done.2
  103.2 0.0 copy-start.6
  103.2 0.0 copy-start.8
  103.2 2.6 %convolution_convert_fusion.1 = bf16[1024,1024]{1,0:T(8,128)(2,1)S(1)} fusion(bf16[1024,384]{0,1:T(8,128)(2,1)} %copy-done.4, bf16[1024,1152]{1,0:T(8,128)(2,1)S(1)} %copy-done.2), kind=kOutput, calls=%fused_computation.13 | convolution fusion | flops 806354944 | bytes 3670016 | tf_op jit(solution)/shard_map/dot_general | solution.py:22
  105.8 0.0 copy-done.6
  105.8 0.0 copy-done.8
  105.8 1.9 convolution_convert_fusion.2
  107.7 2.7 %pad_maximum_fusion = bf16[32,64,1024]{2,1,0:T(8,128)(2,1)} fusion(bf16[32,32,1024]{2,1,0:T(8,128)(2,1)S(1)} %bitcast.90, bf16[32,32,1024]{2,1,0:T(8,128)(2,1)S(1)} %bitcast.89), kind=kLoop, calls=%fused_computation | loop fusion | flops 8388608 | bytes 8388608 | tf_op jit(solution)/shard_map/concatenate | solution.py:90
  110.4 7.4 %all-to-all-start.1 = ((bf16[32,64,1024]{2,1,0:T(8,128)(2,1)}), bf16[32,64,1024]{2,1,0:T(8,128)(2,1)}, u32[]{:S(2)}, u32[]{:S(2)}) async-start(bf16[32,64,1024]{2,1,0:T(8,128)(2,1)} %pad_maximum_fusion), calls=%async_computation.1 | async-start | bytes 8388608 | tf_op jit(solution)/shard_map/all_to_all | solution.py:97
  117.8 54.2 %reduce-scatter.4.cloned.1.call-done = bf16[64,1152]{1,0:T(8,128)(2,1)} async-done(((bf16[1024,1152]{1,0:T(8,128)(2,1)}), bf16[64,1152]{1,0:T(8,128)(2,1)}) %reduce-scatter.4.cloned.1.call-update) | async-done | bytes 147472
  172.0 1.1 copy.62
  173.2 0.0 all-to-all-done.1
  173.2 0.7 copy.56
  173.9 0.7 copy.57
  174.6 0.7 copy.58
  175.4 3.3 %fusion.21 = bf16[128,1024]{1,0:T(8,128)(2,1)} fusion(bf16[32,64,1024]{2,1,0:T(8,128)(2,1)} %all-to-all-done.1, s32[2,128]{1,0:T(2,128)S(1)} %get-tuple-element.54, s32[32,32]{1,0:T(8,128)S(1)} %multiply_add_fusion), kind=kOutput, calls=%fused_computation.30 | convolution fusion | flops 537264128 | bytes 2364416 | tf_op jit(solution)/shard_map/dot_general | solution.py:105
  178.7 3.4 %multiply_reduce_fusion = (f32[2,128]{1,0:T(2,128)}, bf16[128,1024]{1,0:T(8,128)(2,1)}) fusion(f32[128,1024]{1,0:T(8,128)S(1)} %convert_element_type.48, f32[2,128]{1,0:T(2,128)S(1)} %bitcast.95, bf16[32,64,1024]{2,1,0:T(8,128)(2,1)} %all-to-all-done.1, s32[2,128]{1,0:T(2,128)S(1)} %get-tuple-element.54, s32[32,32]{1,0:T(8,128)S(1)} %multiply_add_fusion), kind=kOutput, calls=%fused_computation.33 | convolution fusion | flops 538050304 | bytes 2890752 | tf_op jit(solution)/shard_map/dot_general | solution.py:105
  (6 shorter events, 0.1 us)
Async XLA Ops:
  7.2 6.2 %copy-start = (f32[128,2]{0,1:T(2,128)S(1)}, f32[128,2]{0,1:T(2,128)}, u32[]{:S(2)}) copy-start(f32[128,2]{0,1:T(2,128)} %param.9) | copy-start | bytes 3076
  7.2 6.3 %copy-start.3 = (bf16[128,1024]{1,0:T(8,128)(2,1)S(1)}, bf16[128,1024]{1,0:T(8,128)(2,1)}, u32[]{:S(2)}) copy-start(bf16[128,1024]{1,0:T(8,128)(2,1)} %param.7) | copy-start | bytes 786436
  7.2 81.8 %all-gather.3.cloned.1.call-start = ((), (), s32[]{:S(2)}) async-start(), calls=%async_computation.3 | async-start | bytes 2506752 | tf_op jit(solution)/shard_map/all_gather | solution.py:37
  8.8 163.2 %reduce-scatter.4.cloned.1.call-start = ((), (), s32[]{:S(2)}) async-start(), calls=%async_computation.4 | async-start | bytes 2506752
  89.0 2.9 %copy-start.1 = (bf16[1024,1152]{1,0:T(8,128)(2,1)S(1)}, bf16[1024,1152]{1,0:T(8,128)(2,1)}, u32[]{:S(2)}) copy-start(bf16[1024,1152]{1,0:T(8,128)(2,1)} %all-gather.3.cloned.1.call-done) | copy-start | bytes 7077892
  95.6 1.0 copy-start.4
  95.6 1.1 copy-start.5
  95.6 1.4 copy-start.7
  101.5 1.7 copy-start.2
  103.2 2.6 %copy-start.6 = (bf16[1024,384]{0,1:T(8,128)(2,1)S(1)}, bf16[1024,384]{0,1:T(8,128)(2,1)}, u32[]{:S(2)}) copy-start(bf16[1024,384]{0,1:T(8,128)(2,1)} %copy-done.5) | copy-start | bytes 2359300
  103.2 2.6 %copy-start.8 = (bf16[1024,384]{0,1:T(8,128)(2,1)S(1)}, bf16[1024,384]{0,1:T(8,128)(2,1)}, u32[]{:S(2)}) copy-start(bf16[1024,384]{0,1:T(8,128)(2,1)} %copy-done.7) | copy-start | bytes 2359300
  110.4 62.8 %all-to-all-start.1 = ((bf16[32,64,1024]{2,1,0:T(8,128)(2,1)}), bf16[32,64,1024]{2,1,0:T(8,128)(2,1)}, u32[]{:S(2)}, u32[]{:S(2)}) async-start(bf16[32,64,1024]{2,1,0:T(8,128)(2,1)} %pad_maximum_fusion), calls=%async_computation.1 | async-start | bytes 8388608 | tf_op jit(solution)/shard_map/all_to_all | solution.py:97
Sparse Core Ops, SparseCore 0:
  10.7 78.3 all-gather.2
  101.7 70.3 reduce-scatter.3

commit v9 on v8

--- a/solution.py
+++ b/solution.py
@@ -96,7 +96,14 @@
     )
     back_home = lax.all_to_all(leaving, "expert", split_axis=0, concat_axis=0, tiled=True)
 
-    back_home, summed = lax.optimization_barrier((back_home, summed))
+    back_home, gate_sum, up_sum, down_sum = lax.optimization_barrier(
+        (
+            back_home,
+            summed[:, :hidden_width],
+            summed[:, hidden_width : 2 * hidden_width],
+            summed[:, 2 * hidden_width :],
+        )
+    )
     own_place = (flat_ids * capacity + slot_of).reshape(tok_rows, top_count).T.reshape(-1)
     taker = (jnp.arange(total_rows, dtype=jnp.int32)[None, :] == own_place[:, None]).astype(
         jnp.bfloat16
@@ -115,9 +122,9 @@
     grad_probs = jnp.sum(grad_wide[None] * picked, axis=2).T
     grad_tokens = jnp.sum(back_picked.astype(jnp.float32), axis=0).astype(jnp.bfloat16)
 
-    grad_w_gate = summed[:, :hidden_width][None]
-    grad_w_up = summed[:, hidden_width : 2 * hidden_width][None]
-    grad_w_down = summed[:, 2 * hidden_width :].T[None]
+    grad_w_gate = gate_sum[None]
+    grad_w_up = up_sum[None]
+    grad_w_down = down_sum.T[None]
     return (mixed_out, grad_tokens, grad_probs, grad_w_gate, grad_w_up, grad_w_down)
 
 

time: 189 us -> 189 us (level)
  no operation moved by 1% of the time
where the time goes in v9:
time: 189 us
  waiting for transfers between devices  71.4 us (38%)
  blocking collectives  56.1 us (30%)
  matrix products  19.9 us (11%)
  between operations  14.3 us (8%)
  local copies, waits for them, and re-layouts  12.3 us (7%)
  other arithmetic  7.57 us (4%)
  starting transfers between devices  7.52 us (4%)
    all_to_all x1, blocking collectives, shards(): lax.all_to_all(outgoing.reshape(senders, 2 * capacity, model_width), 'exp...  56.1 us
    unnamed x3, waiting for transfers between devices  54.3 us
    all_gather x1, waiting for transfers between devices, shards(): whole = lax.all_gather(packed[None], 'dp', axis=1, tiled=True)[0]  17.1 us
    unnamed x23, local copies, waits for them, and re-layouts  7.6 us
    all_to_all x1, starting transfers between devices, shards(): lax.all_to_all(leaving, 'expert', split_axis=0, concat_axis=0, tiled=True)  7.44 us
    dot_general x2, matrix products, shards(): lax.dot_general(taker, back_home[:, half * capacity:(half + 1) * capacity...  6.76 us
    dot_general x2, matrix products, contract_cols(): lax.dot_general(left_op, right_op, (((1,), (1,)), ((), ())), preferred_el...  4.42 us
  transfers between devices with their start and end apart: 3, of which 2 were waited for; matrix products, arithmetic and copies ran while one was open for 8% of the time, Pallas kernels for 0%

profile of v9, /device:TPU:20, one launch (start us, length us, event | category | flops | bytes accessed | tf_op | source)
XLA Modules:
  0.0 189.0 jit_solution(11774554846974863676)
XLA Ops:
  7.2 0.0 copy-start
  7.2 0.0 copy-start.3
  7.2 0.0 all-gather.3.cloned.1.call-start
  7.2 1.6 pad_maximum_fusion.5
  8.8 0.0 all-gather.3.cloned.1.call-update
  8.8 0.0 reduce-scatter.4.cloned.1.call-start
  8.9 0.8 copy.51
  9.7 0.1 eq.98
  9.8 0.1 eq.94
  9.9 0.6 reduce-window.6
  10.5 0.2 slice_reduce_fusion
  10.8 0.1 fusion.40
  10.9 0.1 reduce_sum.39
  11.0 0.1 copy.54
  11.1 0.7 add_bitcast_fusion.1
  11.8 0.3 iota_compare_fusion
  12.1 0.2 fusion.27
  12.4 1.0 convert_element_type.48
  13.4 0.0 copy-done
  13.4 0.1 fusion.26
  13.5 0.0 copy-done.3
  13.5 2.3 %convolution_convert_fusion = bf16[2048,1024]{1,0:T(8,128)(2,1)S(1)} fusion(pred[2048,256]{1,0:T(32,128)(4,1)S(1)} %iota_compare_fusion, pred[2048,128]{1,0:T(32,128)(4,1)S(1)} %fusion.27, bf16[256,1024]{1,0:T(8,128)(2,1)S(1)} %fusion.26, bf16[128,1024]{1,0:T(8,128)(2,1)S(1)} %copy-done.3), kind=kOutput, calls=%fused_computation.1 | convolution fusion | flops 1615069184 | bytes 5767168 | tf_op jit(solution)/shard_map/dot_general | solution.py:54
  15.9 56.1 %all_to_all.10 = bf16[32,64,1024]{2,1,0:T(8,128)(2,1)} all-to-all(bf16[32,64,1024]{2,1,0:T(8,128)(2,1)S(1)} %bitcast.81), channel_id=1, replica_groups=mesh['dp'=16,'expert'=32] {'expert'}, dimensions={0} | all-to-all | bytes 8388608 | tf_op jit(solution)/shard_map/all_to_all | solution.py:55
  72.0 17.1 %all-gather.3.cloned.1.call-done = bf16[1024,1152]{1,0:T(8,128)(2,1)} async-done(((bf16[64,1152]{1,0:T(8,128)(2,1)}), bf16[1024,1152]{1,0:T(8,128)(2,1)}) %all-gather.3.cloned.1.call-update) | async-done | bytes 2359312 | tf_op jit(solution)/shard_map/all_gather | solution.py:37
  89.0 0.0 copy-start.1
  89.0 2.8 %fusion.46 = (bf16[32,32,1024]{2,1,0:T(8,128)(2,1)S(1)}, bf16[32,32,1024]{2,1,0:T(8,128)(2,1)S(1)}) fusion(bf16[32,64,1024]{2,1,0:T(8,128)(2,1)} %all_to_all.10), kind=kLoop, calls=%fused_computation.68 | loop fusion | bytes 8388608 | tf_op jit(solution)/shard_map/slice | solution.py:63
  91.9 0.1 copy-done.1
  92.0 1.9 %fusion.11 = f32[1024,768]{0,1:T(8,128)S(1)} fusion(bf16[1024,1024]{1,0:T(8,128)(2,1)S(1)} %bitcast.82, bf16[1024,1152]{1,0:T(8,128)(2,1)S(1)} %copy-done.1), kind=kOutput, calls=%fused_computation.24 | convolution fusion | flops 1610612736 | bytes 6815744 | tf_op jit(solution)/shard_map/dot_general | solution.py:66
  93.9 1.7 multiply_convert_fusion.1
  95.6 0.0 copy-start.4
  95.6 0.0 copy-start.5
  95.6 0.0 copy-start.7
  95.6 1.0 convolution_convert_fusion.4
  96.6 0.0 copy-done.4
  96.6 0.1 copy-done.5
  96.7 0.3 copy-done.7
  97.0 1.8 convolution_convert_fusion.3
  98.8 0.2 pad_maximum_fusion.1
  99.0 2.5 %copy.61 = bf16[1024,1152]{1,0:T(8,128)(2,1)} copy(bf16[1024,1152]{0,1:T(8,128)(2,1)S(1)} %pad_maximum_fusion.1) | data formatting | bytes 4718592
  101.5 0.0 copy-start.2
  101.5 0.0 reduce-scatter.4.cloned.1.call-update
  101.6 1.6 copy-done.2
  103.2 0.0 copy-start.6
  103.2 0.0 copy-start.8
  103.2 2.6 %convolution_convert_fusion.1 = bf16[1024,1024]{1,0:T(8,128)(2,1)S(1)} fusion(bf16[1024,384]{0,1:T(8,128)(2,1)} %copy-done.4, bf16[1024,1152]{1,0:T(8,128)(2,1)S(1)} %copy-done.2), kind=kOutput, calls=%fused_computation.13 | convolution fusion | flops 806354944 | bytes 3670016 | tf_op jit(solution)/shard_map/dot_general | solution.py:22
  105.8 0.0 copy-done.6
  105.8 0.0 copy-done.8
  105.8 1.9 convolution_convert_fusion.2
  107.7 2.7 %pad_maximum_fusion = bf16[32,64,1024]{2,1,0:T(8,128)(2,1)} fusion(bf16[32,32,1024]{2,1,0:T(8,128)(2,1)S(1)} %bitcast.87, bf16[32,32,1024]{2,1,0:T(8,128)(2,1)S(1)} %bitcast.86), kind=kLoop, calls=%fused_computation | loop fusion | flops 8388608 | bytes 8388608 | tf_op jit(solution)/shard_map/concatenate | solution.py:90
  110.4 7.4 %all-to-all-start.1 = ((bf16[32,64,1024]{2,1,0:T(8,128)(2,1)}), bf16[32,64,1024]{2,1,0:T(8,128)(2,1)}, u32[]{:S(2)}, u32[]{:S(2)}) async-start(bf16[32,64,1024]{2,1,0:T(8,128)(2,1)} %pad_maximum_fusion), calls=%async_computation.1 | async-start | bytes 8388608 | tf_op jit(solution)/shard_map/all_to_all | solution.py:97
  117.8 54.2 %reduce-scatter.4.cloned.1.call-done = bf16[64,1152]{1,0:T(8,128)(2,1)} async-done(((bf16[1024,1152]{1,0:T(8,128)(2,1)}), bf16[64,1152]{1,0:T(8,128)(2,1)}) %reduce-scatter.4.cloned.1.call-update) | async-done | bytes 147472
  172.0 0.9 fusion.47
  172.9 0.1 copy.63
  173.0 0.1 copy.64
  173.2 0.1 copy.65
  173.3 0.0 all-to-all-done.1
  173.3 3.3 %fusion.21 = bf16[128,1024]{1,0:T(8,128)(2,1)} fusion(bf16[32,64,1024]{2,1,0:T(8,128)(2,1)} %all-to-all-done.1, s32[2,128]{1,0:T(2,128)S(1)} %get-tuple-element.58, s32[32,32]{1,0:T(8,128)S(1)} %multiply_add_fusion), kind=kOutput, calls=%fused_computation.30 | convolution fusion | flops 537264128 | bytes 2364416 | tf_op jit(solution)/shard_map/dot_general | solution.py:112
  176.6 3.4 %multiply_reduce_fusion = (f32[2,128]{1,0:T(2,128)}, bf16[128,1024]{1,0:T(8,128)(2,1)}) fusion(f32[128,1024]{1,0:T(8,128)S(1)} %convert_element_type.48, f32[2,128]{1,0:T(2,128)S(1)} %bitcast.95, bf16[32,64,1024]{2,1,0:T(8,128)(2,1)} %all-to-all-done.1, s32[2,128]{1,0:T(2,128)S(1)} %get-tuple-element.58, s32[32,32]{1,0:T(8,128)S(1)} %multiply_add_fusion), kind=kOutput, calls=%fused_computation.33 | convolution fusion | flops 538050304 | bytes 2890752 | tf_op jit(solution)/shard_map/dot_general | solution.py:112
  180.1 0.7 copy.56
  180.8 0.7 copy.57
  181.5 0.7 copy.58
  (5 shorter events, 0.1 us)
Async XLA Ops:
  7.2 6.2 %copy-start = (f32[128,2]{0,1:T(2,128)S(1)}, f32[128,2]{0,1:T(2,128)}, u32[]{:S(2)}) copy-start(f32[128,2]{0,1:T(2,128)} %param.9) | copy-start | bytes 3076
  7.2 6.3 %copy-start.3 = (bf16[128,1024]{1,0:T(8,128)(2,1)S(1)}, bf16[128,1024]{1,0:T(8,128)(2,1)}, u32[]{:S(2)}) copy-start(bf16[128,1024]{1,0:T(8,128)(2,1)} %param.7) | copy-start | bytes 786436
  7.2 81.8 %all-gather.3.cloned.1.call-start = ((), (), s32[]{:S(2)}) async-start(), calls=%async_computation.3 | async-start | bytes 2506752 | tf_op jit(solution)/shard_map/all_gather | solution.py:37
  8.8 163.2 %reduce-scatter.4.cloned.1.call-start = ((), (), s32[]{:S(2)}) async-start(), calls=%async_computation.4 | async-start | bytes 2506752
  89.0 2.9 %copy-start.1 = (bf16[1024,1152]{1,0:T(8,128)(2,1)S(1)}, bf16[1024,1152]{1,0:T(8,128)(2,1)}, u32[]{:S(2)}) copy-start(bf16[1024,1152]{1,0:T(8,128)(2,1)} %all-gather.3.cloned.1.call-done) | copy-start | bytes 7077892
  95.6 1.0 copy-start.4
  95.6 1.1 copy-start.5
  95.6 1.4 copy-start.7
  101.5 1.7 copy-start.2
  103.2 2.6 %copy-start.6 = (bf16[1024,384]{0,1:T(8,128)(2,1)S(1)}, bf16[1024,384]{0,1:T(8,128)(2,1)}, u32[]{:S(2)}) copy-start(bf16[1024,384]{0,1:T(8,128)(2,1)} %copy-done.5) | copy-start | bytes 2359300
  103.2 2.6 %copy-start.8 = (bf16[1024,384]{0,1:T(8,128)(2,1)S(1)}, bf16[1024,384]{0,1:T(8,128)(2,1)}, u32[]{:S(2)}) copy-start(bf16[1024,384]{0,1:T(8,128)(2,1)} %copy-done.7) | copy-start | bytes 2359300
  110.4 62.9 %all-to-all-start.1 = ((bf16[32,64,1024]{2,1,0:T(8,128)(2,1)}), bf16[32,64,1024]{2,1,0:T(8,128)(2,1)}, u32[]{:S(2)}, u32[]{:S(2)}) async-start(bf16[32,64,1024]{2,1,0:T(8,128)(2,1)} %pad_maximum_fusion), calls=%async_computation.1 | async-start | bytes 8388608 | tf_op jit(solution)/shard_map/all_to_all | solution.py:97
Sparse Core Ops, SparseCore 0:
  10.7 78.3 all-gather.2
  101.7 70.3 reduce-scatter.3

commit v10 on v9

--- a/solution.py
+++ b/solution.py
@@ -60,16 +60,22 @@
         tiled=True,
     )
     arrived, whole = lax.optimization_barrier((arrived, whole))
-    slot_rows = arrived[:, :capacity].reshape(total_rows, model_width)
-    grad_in = arrived[:, capacity:].reshape(total_rows, model_width)
+    slot_rows = arrived[:, :capacity]
+    grad_in = arrived[:, capacity:]
+    on_width = (((2,), (0,)), ((), ()))
+    on_rows = (((0, 1), (0, 1)), ((), ()))
 
-    both_pre = jnp.dot(slot_rows, gate_up, preferred_element_type=jnp.float32)
+    both_pre = lax.dot_general(
+        slot_rows, gate_up, on_width, preferred_element_type=jnp.float32
+    ).reshape(total_rows, 2 * hidden_width)
     gate_pre = both_pre[:, :hidden_width]
     up_pre = both_pre[:, hidden_width:]
     sigmoid_g = jax.nn.sigmoid(gate_pre)
     activated = gate_pre * sigmoid_g
     hidden = (activated * up_pre).astype(jnp.bfloat16)
-    back_hidden = jnp.dot(grad_in, down_t, preferred_element_type=jnp.float32)
+    back_hidden = lax.dot_general(
+        grad_in, down_t, on_width, preferred_element_type=jnp.float32
+    ).reshape(total_rows, hidden_width)
     back_gate = (back_hidden * up_pre * sigmoid_g * (1.0 + gate_pre * (1.0 - sigmoid_g))).astype(
         jnp.bfloat16
     )
@@ -78,8 +84,18 @@
 
     grad_terms = jnp.concatenate(
         [
-            contract_rows(slot_rows, back_both).astype(jnp.bfloat16),
-            contract_rows(grad_in, hidden).astype(jnp.bfloat16),
+            lax.dot_general(
+                slot_rows,
+                back_both.reshape(senders, capacity, 2 * hidden_width),
+                on_rows,
+                preferred_element_type=jnp.float32,
+            ).astype(jnp.bfloat16),
+            lax.dot_general(
+                grad_in,
+                hidden.reshape(senders, capacity, hidden_width),
+                on_rows,
+                preferred_element_type=jnp.float32,
+            ).astype(jnp.bfloat16),
         ],
         axis=1,
     )

time: 189 us -> 190 us (level)
  the two profiles are of different devices: /device:TPU:20 before, /device:TPU:12 now
where the time goes in v10:
time: 190 us; the launch traced here: 189 us
  waiting for transfers between devices  69.5 us (37%)
  blocking collectives  57.4 us (30%)
  matrix products  22.8 us (12%)
  between operations  14.3 us (8%)
  local copies, waits for them, and re-layouts  9.3 us (5%)
  other arithmetic  8.58 us (5%)
  starting transfers between devices  7.52 us (4%)
    all_to_all x1, blocking collectives, shards(): lax.all_to_all(outgoing.reshape(senders, 2 * capacity, model_width), 'exp...  57.4 us
    unnamed x3, waiting for transfers between devices  54.4 us
    all_gather x1, waiting for transfers between devices, shards(): whole = lax.all_gather(packed[None], 'dp', axis=1, tiled=True)[0]  15.1 us
    all_to_all x1, starting transfers between devices, shards(): lax.all_to_all(leaving, 'expert', split_axis=0, concat_axis=0, tiled=True)  7.44 us
    unnamed x25, local copies, waits for them, and re-layouts  7.4 us
    dot_general x2, matrix products, shards(): lax.dot_general(taker, back_home[:, half * capacity:(half + 1) * capacity...  6.82 us
    dot_general x2, matrix products, contract_cols(): lax.dot_general(left_op, right_op, (((1,), (1,)), ((), ())), preferred_el...  4.4 us
    dot_general x1, matrix products, shards(): lax.dot_general(slot_rows, gate_up, on_width, preferred_element_type=jnp....  3.98 us
  transfers between devices with their start and end apart: 3, of which 2 were waited for; matrix products, arithmetic and copies ran while one was open for 8% of the time, Pallas kernels for 0%

profile of v10, /device:TPU:12, one launch (start us, length us, event | category | flops | bytes accessed | tf_op | source)
XLA Modules:
  0.0 189.4 jit_solution(17026420559179845660)
XLA Ops:
  7.2 0.0 copy-start.7
  7.2 0.0 copy-start.9
  7.2 0.0 all-gather.3.cloned.1.call-start
  7.2 1.6 pad_maximum_fusion.3
  8.8 0.0 all-gather.3.cloned.1.call-update
  8.8 0.0 reduce-scatter.4.cloned.1.call-start
  8.9 0.8 copy.51
  9.7 0.1 eq.98
  9.8 0.1 eq.94
  9.9 0.6 reduce-window.6
  10.5 0.2 slice_reduce_fusion
  10.8 0.1 fusion.53
  10.9 0.1 reduce_sum.39
  11.0 0.1 copy.54
  11.1 0.7 add_bitcast_fusion.1
  11.8 0.3 iota_compare_fusion
  12.1 0.2 fusion.40
  12.4 1.0 convert_element_type.48
  13.4 0.0 copy-start.3
  13.4 0.8 copy-done.3
  14.2 0.0 copy-done.7
  14.2 0.1 fusion.39
  14.3 0.0 copy-done.9
  14.3 2.3 %convolution_convert_fusion = bf16[2048,1024]{1,0:T(8,128)(2,1)S(1)} fusion(pred[2048,256]{1,0:T(32,128)(4,1)S(1)} %iota_compare_fusion, pred[2048,128]{1,0:T(32,128)(4,1)S(1)} %fusion.40, bf16[256,1024]{1,0:T(8,128)(2,1)S(1)} %fusion.39, bf16[128,1024]{1,0:T(8,128)(2,1)S(1)} %copy-done.9), kind=kOutput, calls=%fused_computation.1 | convolution fusion | flops 1615069184 | bytes 5767168 | tf_op jit(solution)/shard_map/dot_general | solution.py:54
  16.7 57.4 %all_to_all.10 = bf16[32,64,1024]{2,1,0:T(8,128)(2,1)} all-to-all(bf16[32,64,1024]{2,1,0:T(8,128)(2,1)S(1)} %bitcast.100), channel_id=1, replica_groups=mesh['dp'=16,'expert'=32] {'expert'}, dimensions={0} | all-to-all | bytes 8388608 | tf_op jit(solution)/shard_map/all_to_all | solution.py:55
  74.1 15.1 %all-gather.3.cloned.1.call-done = bf16[1024,1152]{1,0:T(8,128)(2,1)} async-done(((bf16[64,1152]{1,0:T(8,128)(2,1)}), bf16[1024,1152]{1,0:T(8,128)(2,1)}) %all-gather.3.cloned.1.call-update) | async-done | bytes 2359312 | tf_op jit(solution)/shard_map/all_gather | solution.py:37
  89.1 0.0 copy-start
  89.1 4.0 %fusion.14 = f32[32,32,768]{2,1,0:T(8,128)S(1)} fusion(bf16[32,64,1024]{2,1,0:T(8,128)(2,1)} %all_to_all.10, bf16[1024,1152]{1,0:T(8,128)(2,1)} %all-gather.3.cloned.1.call-done), kind=kOutput, calls=%fused_computation.21 | convolution fusion | flops 1610612736 | bytes 6815744 | tf_op jit(solution)/shard_map/dot_general | solution.py:68
  93.1 0.0 copy-done
  93.1 2.4 %fusion.11 = f32[32,32,384]{2,1,0:T(8,128)S(1)} fusion(bf16[32,64,1024]{2,1,0:T(8,128)(2,1)S(1)} %copy-done, bf16[1024,1152]{1,0:T(8,128)(2,1)} %all-gather.3.cloned.1.call-done), kind=kOutput, calls=%fused_computation.18 | convolution fusion | flops 805306368 | bytes 4456448 | tf_op jit(solution)/shard_map/dot_general | solution.py:76
  95.5 0.9 fusion.18
  96.4 0.0 copy-start.1
  96.4 0.0 copy-start.5
  96.4 0.1 pad_maximum_fusion.2
  96.6 1.9 bitcast_convert_fusion
  98.4 0.0 copy-done.1
  98.4 0.0 copy-done.5
  98.4 1.0 bitcast_convert_fusion.1
  99.5 0.2 pad_maximum_fusion.1
  99.7 2.5 %copy.61 = bf16[1024,1152]{1,0:T(8,128)(2,1)} copy(bf16[1024,1152]{0,1:T(8,128)(2,1)S(1)} %pad_maximum_fusion.1) | data formatting | bytes 4718592
  102.2 0.0 copy-start.6
  102.2 0.0 reduce-scatter.4.cloned.1.call-update
  102.3 1.1 copy-done.6
  103.4 0.0 copy-start.2
  103.4 0.0 copy-start.8
  103.4 2.6 %convolution_convert_fusion.1 = bf16[1024,1024]{1,0:T(8,128)(2,1)S(1)} fusion(bf16[1024,384]{1,0:T(8,128)(2,1)S(1)} %copy-done.6, bf16[1024,1152]{1,0:T(8,128)(2,1)} %all-gather.3.cloned.1.call-done), kind=kOutput, calls=%fused_computation.14 | convolution fusion | flops 806354944 | bytes 3670016 | tf_op jit(solution)/shard_map/dot_general | solution.py:22
  106.0 0.0 copy-done.2
  106.0 0.0 copy-done.8
  106.0 1.8 convolution_convert_fusion.2
  107.8 2.7 %pad_maximum_fusion = bf16[32,64,1024]{2,1,0:T(8,128)(2,1)} fusion(bf16[32,32,1024]{2,1,0:T(8,128)(2,1)S(1)} %bitcast.103, bf16[32,32,1024]{2,1,0:T(8,128)(2,1)S(1)} %bitcast.102), kind=kLoop, calls=%fused_computation | loop fusion | flops 8388608 | bytes 8388608 | tf_op jit(solution)/shard_map/concatenate | solution.py:106
  110.5 7.4 %all-to-all-start.1 = ((bf16[32,64,1024]{2,1,0:T(8,128)(2,1)}), bf16[32,64,1024]{2,1,0:T(8,128)(2,1)}, u32[]{:S(2)}, u32[]{:S(2)}) async-start(bf16[32,64,1024]{2,1,0:T(8,128)(2,1)} %pad_maximum_fusion), calls=%async_computation.1 | async-start | bytes 8388608 | tf_op jit(solution)/shard_map/all_to_all | solution.py:113
  118.0 54.4 %reduce-scatter.4.cloned.1.call-done = bf16[64,1152]{1,0:T(8,128)(2,1)} async-done(((bf16[1024,1152]{1,0:T(8,128)(2,1)}), bf16[64,1152]{1,0:T(8,128)(2,1)}) %reduce-scatter.4.cloned.1.call-update) | async-done | bytes 147472
  172.4 0.9 fusion.57
  173.2 0.1 copy.63
  173.4 0.1 copy.64
  173.5 0.1 copy.65
  173.6 0.0 all-to-all-done.1
  173.6 0.0 copy-start.4
  173.6 3.4 %fusion.34 = bf16[128,1024]{1,0:T(8,128)(2,1)} fusion(bf16[32,64,1024]{2,1,0:T(8,128)(2,1)} %all-to-all-done.1, s32[2,128]{1,0:T(2,128)S(1)} %get-tuple-element.56, s32[32,32]{1,0:T(8,128)S(1)} %multiply_add_fusion), kind=kOutput, calls=%fused_computation.41 | convolution fusion | flops 537264128 | bytes 2364416 | tf_op jit(solution)/shard_map/dot_general | solution.py:128
  177.0 0.0 copy-done.4
  177.0 3.4 %multiply_reduce_fusion = (f32[2,128]{1,0:T(2,128)}, bf16[128,1024]{1,0:T(8,128)(2,1)}) fusion(f32[128,1024]{1,0:T(8,128)S(1)} %copy-done.4, f32[2,128]{1,0:T(2,128)S(1)} %bitcast.113, bf16[32,64,1024]{2,1,0:T(8,128)(2,1)} %all-to-all-done.1, s32[2,128]{1,0:T(2,128)S(1)} %get-tuple-element.56, s32[32,32]{1,0:T(8,128)S(1)} %multiply_add_fusion), kind=kOutput, calls=%fused_computation.44 | convolution fusion | flops 538050304 | bytes 2890752 | tf_op jit(solution)/shard_map/dot_general | solution.py:128
  180.4 0.7 copy.56
  181.2 0.7 copy.57
  181.9 0.7 copy.58
  (5 shorter events, 0.1 us)
Async XLA Ops:
  7.2 7.0 %copy-start.7 = (f32[128,2]{0,1:T(2,128)S(1)}, f32[128,2]{0,1:T(2,128)}, u32[]{:S(2)}) copy-start(f32[128,2]{0,1:T(2,128)} %param.9) | copy-start | bytes 3076
  7.2 7.1 %copy-start.9 = (bf16[128,1024]{1,0:T(8,128)(2,1)S(1)}, bf16[128,1024]{1,0:T(8,128)(2,1)}, u32[]{:S(2)}) copy-start(bf16[128,1024]{1,0:T(8,128)(2,1)} %param.7) | copy-start | bytes 786436
  7.2 81.9 %all-gather.3.cloned.1.call-start = ((), (), s32[]{:S(2)}) async-start(), calls=%async_computation.3 | async-start | bytes 2506752 | tf_op jit(solution)/shard_map/all_gather | solution.py:37
  8.8 163.6 %reduce-scatter.4.cloned.1.call-start = ((), (), s32[]{:S(2)}) async-start(), calls=%async_computation.4 | async-start | bytes 2506752
  13.4 0.8 copy-start.3
  89.1 4.0 %copy-start = (bf16[32,64,1024]{2,1,0:T(8,128)(2,1)S(1)}, bf16[32,64,1024]{2,1,0:T(8,128)(2,1)}, u32[]{:S(2)}) copy-start(bf16[32,64,1024]{2,1,0:T(8,128)(2,1)} %all_to_all.10) | copy-start | bytes 12582916
  96.4 2.0 %copy-start.1 = (bf16[1024,384]{1,0:T(8,128)(2,1)}, bf16[1024,384]{1,0:T(8,128)(2,1)S(1)}, u32[]{:S(2)}) copy-start(bf16[1024,384]{1,0:T(8,128)(2,1)S(1)} %get-tuple-element.51) | copy-start | bytes 2359300
  96.4 2.0 %copy-start.5 = (bf16[1024,384]{1,0:T(8,128)(2,1)}, bf16[1024,384]{1,0:T(8,128)(2,1)S(1)}, u32[]{:S(2)}) copy-start(bf16[1024,384]{1,0:T(8,128)(2,1)S(1)} %get-tuple-element.52) | copy-start | bytes 2359300
  102.2 1.1 copy-start.6
  103.4 2.6 %copy-start.2 = (bf16[1024,384]{1,0:T(8,128)(2,1)S(1)}, bf16[1024,384]{1,0:T(8,128)(2,1)}, u32[]{:S(2)}) copy-start(bf16[1024,384]{1,0:T(8,128)(2,1)} %copy-done.1) | copy-start | bytes 2359300
  103.4 2.6 %copy-start.8 = (bf16[1024,1152]{1,0:T(8,128)(2,1)S(1)}, bf16[1024,1152]{1,0:T(8,128)(2,1)}, u32[]{:S(2)}) copy-start(bf16[1024,1152]{1,0:T(8,128)(2,1)} %all-gather.3.cloned.1.call-done) | copy-start | bytes 7077892
  110.5 63.1 %all-to-all-start.1 = ((bf16[32,64,1024]{2,1,0:T(8,128)(2,1)}), bf16[32,64,1024]{2,1,0:T(8,128)(2,1)}, u32[]{:S(2)}, u32[]{:S(2)}) async-start(bf16[32,64,1024]{2,1,0:T(8,128)(2,1)} %pad_maximum_fusion), calls=%async_computation.1 | async-start | bytes 8388608 | tf_op jit(solution)/shard_map/all_to_all | solution.py:113
  173.6 3.4 %copy-start.4 = (f32[128,1024]{1,0:T(8,128)S(1)}, f32[128,1024]{1,0:T(8,128)}, u32[]{:S(2)}) copy-start(f32[128,1024]{1,0:T(8,128)} %copy-done.3) | copy-start | bytes 1572868
Sparse Core Ops, SparseCore 0:
  10.7 78.4 all-gather.2
  102.4 69.9 reduce-scatter.3

commit v11 on v8

--- a/solution.py
+++ b/solution.py
@@ -78,8 +78,8 @@
 
     grad_terms = jnp.concatenate(
         [
+            contract_rows(grad_in, hidden).astype(jnp.bfloat16),
             contract_rows(slot_rows, back_both).astype(jnp.bfloat16),
-            contract_rows(grad_in, hidden).astype(jnp.bfloat16),
         ],
         axis=1,
     )
@@ -115,9 +115,9 @@
     grad_probs = jnp.sum(grad_wide[None] * picked, axis=2).T
     grad_tokens = jnp.sum(back_picked.astype(jnp.float32), axis=0).astype(jnp.bfloat16)
 
-    grad_w_gate = summed[:, :hidden_width][None]
-    grad_w_up = summed[:, hidden_width : 2 * hidden_width][None]
-    grad_w_down = summed[:, 2 * hidden_width :].T[None]
+    grad_w_down = summed[:, :hidden_width].T[None]
+    grad_w_gate = summed[:, hidden_width : 2 * hidden_width][None]
+    grad_w_up = summed[:, 2 * hidden_width :][None]
     return (mixed_out, grad_tokens, grad_probs, grad_w_gate, grad_w_up, grad_w_down)
 
 

time: 189 us -> 189 us (level)
  the two profiles are of different devices: /device:TPU:20 before, /device:TPU:12 now
where the time goes in v11:
time: 189 us
  waiting for transfers between devices  70.1 us (37%)
  blocking collectives  57.4 us (30%)
  matrix products  19.9 us (11%)
  between operations  14.3 us (8%)
  local copies, waits for them, and re-layouts  12.2 us (6%)
  other arithmetic  7.57 us (4%)
  starting transfers between devices  7.53 us (4%)
    all_to_all x1, blocking collectives, shards(): lax.all_to_all(outgoing.reshape(senders, 2 * capacity, model_width), 'exp...  57.4 us
    unnamed x3, waiting for transfers between devices  54.3 us
    all_gather x1, waiting for transfers between devices, shards(): whole = lax.all_gather(packed[None], 'dp', axis=1, tiled=True)[0]  15.9 us
    unnamed x23, local copies, waits for them, and re-layouts  7.6 us
    all_to_all x1, starting transfers between devices, shards(): lax.all_to_all(leaving, 'expert', split_axis=0, concat_axis=0, tiled=True)  7.45 us
    dot_general x2, matrix products, shards(): lax.dot_general(taker, back_home[:, half * capacity:(half + 1) * capacity...  6.75 us
    dot_general x2, matrix products, contract_cols(): lax.dot_general(left_op, right_op, (((1,), (1,)), ((), ())), preferred_el...  4.42 us
  transfers between devices with their start and end apart: 3, of which 2 were waited for; matrix products, arithmetic and copies ran while one was open for 8% of the time, Pallas kernels for 0%

profile of v11, /device:TPU:12, one launch (start us, length us, event | category | flops | bytes accessed | tf_op | source)
XLA Modules:
  0.0 189.1 jit_solution(555220294489378156)
XLA Ops:
  7.2 0.0 copy-start
  7.2 0.0 copy-start.3
  7.2 0.0 all-gather.3.cloned.1.call-start
  7.2 1.6 pad_maximum_fusion.5
  8.8 0.0 all-gather.3.cloned.1.call-update
  8.8 0.0 reduce-scatter.4.cloned.1.call-start
  8.9 0.8 copy.51
  9.7 0.1 eq.98
  9.8 0.1 eq.94
  9.9 0.6 reduce-window.6
  10.5 0.2 slice_reduce_fusion
  10.8 0.1 fusion.40
  10.9 0.1 reduce_sum.39
  11.0 0.1 copy.54
  11.1 0.7 add_bitcast_fusion.1
  11.8 0.3 iota_compare_fusion
  12.1 0.2 fusion.27
  12.4 1.0 convert_element_type.48
  13.4 0.0 copy-done
  13.4 0.1 fusion.26
  13.5 0.0 copy-done.3
  13.5 2.3 %convolution_convert_fusion = bf16[2048,1024]{1,0:T(8,128)(2,1)S(1)} fusion(pred[2048,256]{1,0:T(32,128)(4,1)S(1)} %iota_compare_fusion, pred[2048,128]{1,0:T(32,128)(4,1)S(1)} %fusion.27, bf16[256,1024]{1,0:T(8,128)(2,1)S(1)} %fusion.26, bf16[128,1024]{1,0:T(8,128)(2,1)S(1)} %copy-done.3), kind=kOutput, calls=%fused_computation.1 | convolution fusion | flops 1615069184 | bytes 5767168 | tf_op jit(solution)/shard_map/dot_general | solution.py:54
  15.9 57.4 %all_to_all.10 = bf16[32,64,1024]{2,1,0:T(8,128)(2,1)} all-to-all(bf16[32,64,1024]{2,1,0:T(8,128)(2,1)S(1)} %bitcast.84), channel_id=1, replica_groups=mesh['dp'=16,'expert'=32] {'expert'}, dimensions={0} | all-to-all | bytes 8388608 | tf_op jit(solution)/shard_map/all_to_all | solution.py:55
  73.3 15.9 %all-gather.3.cloned.1.call-done = bf16[1024,1152]{1,0:T(8,128)(2,1)} async-done(((bf16[64,1152]{1,0:T(8,128)(2,1)}), bf16[1024,1152]{1,0:T(8,128)(2,1)}) %all-gather.3.cloned.1.call-update) | async-done | bytes 2359312 | tf_op jit(solution)/shard_map/all_gather | solution.py:37
  89.1 0.0 copy-start.1
  89.1 2.8 %fusion.46 = (bf16[32,32,1024]{2,1,0:T(8,128)(2,1)S(1)}, bf16[32,32,1024]{2,1,0:T(8,128)(2,1)S(1)}) fusion(bf16[32,64,1024]{2,1,0:T(8,128)(2,1)} %all_to_all.10), kind=kLoop, calls=%fused_computation.71 | loop fusion | bytes 8388608 | tf_op jit(solution)/shard_map/slice | solution.py:63
  92.0 0.1 copy-done.1
  92.1 1.9 %fusion.11 = f32[1024,768]{0,1:T(8,128)S(1)} fusion(bf16[1024,1024]{1,0:T(8,128)(2,1)S(1)} %bitcast.85, bf16[1024,1152]{1,0:T(8,128)(2,1)S(1)} %copy-done.1), kind=kOutput, calls=%fused_computation.24 | convolution fusion | flops 1610612736 | bytes 6815744 | tf_op jit(solution)/shard_map/dot_general | solution.py:66
  94.0 1.7 multiply_convert_fusion.1
  95.7 0.0 copy-start.4
  95.7 0.0 copy-start.5
  95.7 0.0 copy-start.7
  95.7 1.0 convolution_convert_fusion.4
  96.7 0.0 copy-done.4
  96.7 0.1 copy-done.5
  96.8 0.3 copy-done.7
  97.1 1.8 convolution_convert_fusion.3
  98.9 0.2 pad_maximum_fusion.1
  99.1 2.5 %copy.61 = bf16[1024,1152]{1,0:T(8,128)(2,1)} copy(bf16[1024,1152]{0,1:T(8,128)(2,1)S(1)} %pad_maximum_fusion.1) | data formatting | bytes 4718592
  101.6 0.0 copy-start.2
  101.6 0.0 reduce-scatter.4.cloned.1.call-update
  101.6 1.6 copy-done.2
  103.3 0.0 copy-start.6
  103.3 0.0 copy-start.8
  103.3 2.6 %convolution_convert_fusion.1 = bf16[1024,1024]{1,0:T(8,128)(2,1)S(1)} fusion(bf16[1024,384]{0,1:T(8,128)(2,1)} %copy-done.4, bf16[1024,1152]{1,0:T(8,128)(2,1)S(1)} %copy-done.2), kind=kOutput, calls=%fused_computation.13 | convolution fusion | flops 806354944 | bytes 3670016 | tf_op jit(solution)/shard_map/dot_general | solution.py:22
  105.9 0.0 copy-done.6
  105.9 0.0 copy-done.8
  105.9 1.9 convolution_convert_fusion.2
  107.7 2.7 %pad_maximum_fusion = bf16[32,64,1024]{2,1,0:T(8,128)(2,1)} fusion(bf16[32,32,1024]{2,1,0:T(8,128)(2,1)S(1)} %bitcast.90, bf16[32,32,1024]{2,1,0:T(8,128)(2,1)S(1)} %bitcast.89), kind=kLoop, calls=%fused_computation | loop fusion | flops 8388608 | bytes 8388608 | tf_op jit(solution)/shard_map/concatenate | solution.py:90
  110.4 7.4 %all-to-all-start.1 = ((bf16[32,64,1024]{2,1,0:T(8,128)(2,1)}), bf16[32,64,1024]{2,1,0:T(8,128)(2,1)}, u32[]{:S(2)}, u32[]{:S(2)}) async-start(bf16[32,64,1024]{2,1,0:T(8,128)(2,1)} %pad_maximum_fusion), calls=%async_computation.1 | async-start | bytes 8388608 | tf_op jit(solution)/shard_map/all_to_all | solution.py:97
  117.9 54.3 %reduce-scatter.4.cloned.1.call-done = bf16[64,1152]{1,0:T(8,128)(2,1)} async-done(((bf16[1024,1152]{1,0:T(8,128)(2,1)}), bf16[64,1152]{1,0:T(8,128)(2,1)}) %reduce-scatter.4.cloned.1.call-update) | async-done | bytes 147472
  172.2 1.1 copy.62
  173.3 0.0 all-to-all-done.1
  173.3 0.7 copy.56
  174.0 0.7 copy.57
  174.7 0.7 copy.58
  175.5 3.3 %fusion.21 = bf16[128,1024]{1,0:T(8,128)(2,1)} fusion(bf16[32,64,1024]{2,1,0:T(8,128)(2,1)} %all-to-all-done.1, s32[2,128]{1,0:T(2,128)S(1)} %get-tuple-element.54, s32[32,32]{1,0:T(8,128)S(1)} %multiply_add_fusion), kind=kOutput, calls=%fused_computation.30 | convolution fusion | flops 537264128 | bytes 2364416 | tf_op jit(solution)/shard_map/dot_general | solution.py:105
  178.8 3.4 %multiply_reduce_fusion = (f32[2,128]{1,0:T(2,128)}, bf16[128,1024]{1,0:T(8,128)(2,1)}) fusion(f32[128,1024]{1,0:T(8,128)S(1)} %convert_element_type.48, f32[2,128]{1,0:T(2,128)S(1)} %bitcast.95, bf16[32,64,1024]{2,1,0:T(8,128)(2,1)} %all-to-all-done.1, s32[2,128]{1,0:T(2,128)S(1)} %get-tuple-element.54, s32[32,32]{1,0:T(8,128)S(1)} %multiply_add_fusion), kind=kOutput, calls=%fused_computation.33 | convolution fusion | flops 538050304 | bytes 2890752 | tf_op jit(solution)/shard_map/dot_general | solution.py:105
  (6 shorter events, 0.1 us)
Async XLA Ops:
  7.2 6.2 %copy-start = (f32[128,2]{0,1:T(2,128)S(1)}, f32[128,2]{0,1:T(2,128)}, u32[]{:S(2)}) copy-start(f32[128,2]{0,1:T(2,128)} %param.9) | copy-start | bytes 3076
  7.2 6.3 %copy-start.3 = (bf16[128,1024]{1,0:T(8,128)(2,1)S(1)}, bf16[128,1024]{1,0:T(8,128)(2,1)}, u32[]{:S(2)}) copy-start(bf16[128,1024]{1,0:T(8,128)(2,1)} %param.7) | copy-start | bytes 786436
  7.2 81.9 %all-gather.3.cloned.1.call-start = ((), (), s32[]{:S(2)}) async-start(), calls=%async_computation.3 | async-start | bytes 2506752 | tf_op jit(solution)/shard_map/all_gather | solution.py:37
  8.8 163.3 %reduce-scatter.4.cloned.1.call-start = ((), (), s32[]{:S(2)}) async-start(), calls=%async_computation.4 | async-start | bytes 2506752
  89.1 2.9 %copy-start.1 = (bf16[1024,1152]{1,0:T(8,128)(2,1)S(1)}, bf16[1024,1152]{1,0:T(8,128)(2,1)}, u32[]{:S(2)}) copy-start(bf16[1024,1152]{1,0:T(8,128)(2,1)} %all-gather.3.cloned.1.call-done) | copy-start | bytes 7077892
  95.7 1.0 copy-start.4
  95.7 1.1 copy-start.5
  95.7 1.4 copy-start.7
  101.6 1.7 copy-start.2
  103.3 2.6 %copy-start.6 = (bf16[1024,384]{0,1:T(8,128)(2,1)S(1)}, bf16[1024,384]{0,1:T(8,128)(2,1)}, u32[]{:S(2)}) copy-start(bf16[1024,384]{0,1:T(8,128)(2,1)} %copy-done.5) | copy-start | bytes 2359300
  103.3 2.6 %copy-start.8 = (bf16[1024,384]{0,1:T(8,128)(2,1)S(1)}, bf16[1024,384]{0,1:T(8,128)(2,1)}, u32[]{:S(2)}) copy-start(bf16[1024,384]{0,1:T(8,128)(2,1)} %copy-done.7) | copy-start | bytes 2359300
  110.4 62.8 %all-to-all-start.1 = ((bf16[32,64,1024]{2,1,0:T(8,128)(2,1)}), bf16[32,64,1024]{2,1,0:T(8,128)(2,1)}, u32[]{:S(2)}, u32[]{:S(2)}) async-start(bf16[32,64,1024]{2,1,0:T(8,128)(2,1)} %pad_maximum_fusion), calls=%async_computation.1 | async-start | bytes 8388608 | tf_op jit(solution)/shard_map/all_to_all | solution.py:97
Sparse Core Ops, SparseCore 0:
  10.7 78.4 all-gather.2
  101.8 70.3 reduce-scatter.3
